TPU v7x, 32 devices: a whole 2x2x4 slice. The times are simulated.
32 devices in a mesh: groups: 2 (over y), ctx: 8 (over z, x), ch: 2 (over core).
Axes of the slice: x: 2, y: 2, z: 4, core: 2. Of those that a mesh axis runs over, the one named last changes fastest.
Arguments:
- gate_stream: bfloat16 [4096, 512], P(('groups', 'ctx'), 'ch'), parts along dimension 0, may hold values from -6 to 6
- outer_stream: bfloat16 [4096, 512], P(('groups', 'ctx'), 'ch'), parts along dimension 0, may hold values from -6 to 6
- value_stream: bfloat16 [4096, 512], P(('groups', 'ctx'), 'ch'), parts along dimension 0, may hold values from -6 to 6
- short_weight: bfloat16 [3, 3, 512], P(None, None, 'ch'), may hold values from -3.5 to 3.5
- long_filter: bfloat16 [2048, 512], P('ctx', 'ch'), may hold values from -0.125 to 0.125
- skip_gain: float32 [512], P('ch'), may hold values from -4 to 4
Outputs:
- output_rows: bfloat16 [4096, 512], P(('groups', 'ctx'), 'ch'), parts along dimension 0
There are 2 independent parts, one for each index of `groups`. A program takes and returns all parts, laid end to end along the dimension named above; an argument that names none is the same for every part. Nothing has to cross between parts.
All inputs are finite; a program needn't handle non-finite values.
Results may differ from a plain program's by a relative error of at most 0.001.
Values may be sent and summed in bfloat16 or wider, within the bound.
No kernel may reach another device: no remote copies, remote signals or barrier semaphores. Data moves between devices by JAX's collectives and lax.ppermute only.
A program may use at most 64 MiB of HBM per device.

v0:
```python
import math

import jax
import jax.numpy as jnp
from jax import lax
from jax.sharding import PartitionSpec as P

full_precision = lax.Precision.HIGHEST


def passed_along(block, axis, distance):
    devices = range(lax.axis_size(axis))
    route = [(i - distance, i) for i in devices if i - distance in devices]
    return lax.ppermute(block, axis, route)


def from_partner(value, axis, apart):
    mask = 2**apart
    pairs = [(source, source ^ mask) for source in range(lax.axis_size(axis))]
    return lax.ppermute(value, axis, pairs)


def phase_table(first_ids, second, period):
    product = jnp.outer(first_ids, second) % period
    return product.astype(jnp.float32) * (2.0 * math.pi / period)


def rotate(real_part, imag_part, cosine, sine_part):
    return (real_part * cosine - imag_part * sine_part, real_part * sine_part + imag_part * cosine)


def causal_short(stream, rim_rows, kernel):
    taps_count = kernel.shape[0]
    extended = jnp.concatenate([rim_rows, stream], axis=0).astype(jnp.float32)
    length = stream.shape[0]
    summed = jnp.zeros((length, stream.shape[1]), jnp.float32)
    for offset in range(taps_count):
        begin_at = taps_count - 1 - offset
        summed = (
            summed + kernel[offset].astype(jnp.float32) * extended[begin_at : begin_at + length]
        )
    return summed


def along_rows(real_part, imag_part, direction):
    row_count = real_part.shape[-2]
    row_ids = jnp.arange(row_count, dtype=jnp.int32)
    phases = phase_table(row_ids, row_ids, row_count)
    cosine = jnp.cos(phases)
    sine_part = jnp.sin(phases) * direction
    out_real = jnp.einsum(
        "kj,...jc->...kc", cosine, real_part, precision=full_precision
    ) - jnp.einsum("kj,...jc->...kc", sine_part, imag_part, precision=full_precision)
    out_imag = jnp.einsum(
        "kj,...jc->...kc", cosine, imag_part, precision=full_precision
    ) + jnp.einsum("kj,...jc->...kc", sine_part, real_part, precision=full_precision)
    return (out_real, out_imag)


def body(gate_stream, outer_stream, value_stream, short_weight, long_filter, skip_gain):
    rows_local = gate_stream.shape[0]
    rim_count = short_weight.shape[1] - 1
    tail_rows = jnp.stack(
        [
            gate_stream[rows_local - rim_count :],
            outer_stream[rows_local - rim_count :],
            value_stream[rows_local - rim_count :],
        ]
    )
    rim_block = passed_along(tail_rows, "ctx", 1)
    gate_conv = causal_short(gate_stream, rim_block[0], short_weight[0])
    outer_conv = causal_short(outer_stream, rim_block[1], short_weight[1])
    value_conv = causal_short(value_stream, rim_block[2], short_weight[2])
    gated_value = gate_conv * value_conv
    signals = jnp.stack([gated_value, long_filter.astype(jnp.float32)])
    parts_count = lax.axis_size("ctx")
    device = lax.axis_index("ctx")
    seq_total = rows_local * parts_count
    local_rows = jnp.arange(rows_local, dtype=jnp.int32)
    sections = parts_count.bit_length() - 1
    slot_ids = jnp.arange(2, dtype=jnp.int32)
    slot_phase = -math.pi * (device * slot_ids).astype(jnp.float32) / parts_count
    cos_slot = jnp.cos(slot_phase)[None, :, None, None]
    sin_slot = jnp.sin(slot_phase)[None, :, None, None]
    expanded = signals[:, None]
    current = jnp.stack([expanded * cos_slot, expanded * sin_slot])
    for bit_index in reversed(range(sections)):
        half_span = 1 << bit_index
        received = from_partner(current, "ctx", bit_index)
        is_lower = jnp.bitwise_and(device, half_span) == 0
        offset_phase = (
            -math.pi * jnp.bitwise_and(device, half_span - 1).astype(jnp.float32) / half_span
        )
        differ = received - current
        turned = jnp.stack(
            rotate(differ[0], differ[1], jnp.cos(offset_phase), jnp.sin(offset_phase))
        )
        current = jnp.where(is_lower, current + received, turned)
    reversed_index = jnp.zeros((), jnp.int32)
    for bit_index in range(sections):
        reversed_index = reversed_index + jnp.left_shift(
            jnp.bitwise_and(jnp.right_shift(device, bit_index), 1), sections - 1 - bit_index
        )
    freq_first = 2 * reversed_index + slot_ids
    twist_phase = phase_table(local_rows, freq_first, 2 * seq_total).T
    twist_cos = jnp.cos(twist_phase)[:, :, None]
    twist_sin = jnp.sin(twist_phase)[:, :, None]
    real_part, imag_part = rotate(current[0], current[1], twist_cos, -twist_sin)
    spec_real, spec_imag = along_rows(real_part, imag_part, -1.0)
    prod_real = spec_real[0] * spec_real[1] - spec_imag[0] * spec_imag[1]
    prod_imag = spec_real[0] * spec_imag[1] + spec_imag[0] * spec_real[1]
    back_real, back_imag = along_rows(prod_real, prod_imag, 1.0)
    current = jnp.stack(rotate(back_real, back_imag, twist_cos, twist_sin))
    for bit_index in range(sections):
        half_span = 1 << bit_index
        received = from_partner(current, "ctx", bit_index)
        is_lower = jnp.bitwise_and(device, half_span) == 0
        offset_phase = (
            math.pi * jnp.bitwise_and(device, half_span - 1).astype(jnp.float32) / half_span
        )
        from_peer = jnp.stack(
            rotate(received[0], received[1], jnp.cos(offset_phase), jnp.sin(offset_phase))
        )
        from_self = jnp.stack(
            rotate(current[0], current[1], jnp.cos(offset_phase), jnp.sin(offset_phase))
        )
        current = jnp.where(is_lower, current + from_peer, received - from_self)
    unslot_cos = jnp.cos(slot_phase)[:, None, None]
    unslot_sin = -jnp.sin(slot_phase)[:, None, None]
    long_sum = jnp.sum(current[0] * unslot_cos - current[1] * unslot_sin, axis=0)
    long_part = long_sum / (2.0 * seq_total)
    output_rows = outer_conv * (long_part + skip_gain[None, :] * gated_value)
    return output_rows.astype(jnp.bfloat16)


def solution(mesh):
    placed = (
        P(("groups", "ctx"), "ch"),
        P(("groups", "ctx"), "ch"),
        P(("groups", "ctx"), "ch"),
        P(None, None, "ch"),
        P("ctx", "ch"),
        P("ch"),
    )
    return jax.shard_map(
        body, mesh=mesh, in_specs=placed, out_specs=P(("groups", "ctx"), "ch"), check_vma=False
    )
```

profile of v0, /device:TPU:0, one launch (start us, length us, event | category | flops | bytes accessed | tf_op | source)
XLA Modules:
  0.0 334.1 jit_solution(14681126279518435443)
XLA Ops:
  0.0 0.7 slice_bitcast_fusion.9
  0.7 0.7 slice_bitcast_fusion.7
  1.4 0.2 copy.16
  1.6 4.9 %collective-permute-start = (bf16[3,2,256]{1,2,0:T(8,128)(2,1)S(1)}, bf16[3,2,256]{1,2,0:T(8,128)(2,1)S(1)}, u32[]{:S(2)}, u32[]{:S(2)}) collective-permute-start(bf16[3,2,256]{1,2,0:T(8,128)(2,1)S(1)} %copy.16), channel_id=1, source_target_pairs={{0,2},{2,4},{4,6},{6,8},{8,10},{10,12},{12,14},{1,3},{3,5},{5,7},{... | collective-permute-start | bytes 9224 | tf_op jit(solution)/shard_map/ppermute | solution.py:14
  6.5 0.9 slice_convert_fusion.8
  7.3 1.0 copy.20
  8.5 1.0 copy.18
  9.5 1.0 copy.19
  10.5 0.1 collective-permute-done
  10.6 0.1 maximum_convert_fusion.1
  10.8 0.1 maximum_convert_fusion.2
  10.9 0.5 fusion.22
  11.5 0.2 broadcast_multiply_fusion.1
  11.7 1.5 pad_maximum_fusion
  13.3 4.5 %collective-permute-start.1 = (f32[2,2,2,256,256]{3,4,2,1,0:T(8,128)}, f32[2,2,2,256,256]{3,4,2,1,0:T(8,128)}, u32[]{:S(2)}, u32[]{:S(2)}) collective-permute-start(f32[2,2,2,256,256]{3,4,2,1,0:T(8,128)} %pad_maximum_fusion), channel_id=1, source_target_pairs={{0,8},{2,10},{4,12},{6,14},{8,0},{10,2},{12,4},{14,6},{1,9},{3,11}... | collective-permute-start | bytes 6291464 | tf_op jit(solution)/shard_map/ppermute | solution.py:20
  17.9 89.8 %collective-permute-done.1 = f32[2,2,2,256,256]{3,4,2,1,0:T(8,128)} collective-permute-done((f32[2,2,2,256,256]{3,4,2,1,0:T(8,128)}, f32[2,2,2,256,256]{3,4,2,1,0:T(8,128)}, u32[]{:S(2)}, u32[]{:S(2)}) %collective-permute-start.1) | collective-permute-done | bytes 2097184 | tf_op jit(solution)/shard_map/ppermute | solution.py:20
  107.8 1.9 fusion.100
  109.6 0.2 multiply_subtract_fusion.3
  109.9 3.8 %maximum_select_fusion = f32[2,2,2,256,256]{3,4,2,1,0:T(8,128)} fusion(f32[1,2,2,256,256]{3,4,2,1,0:T(8,128)S(1)} %get-tuple-element.15, f32[1,2,2,256,256]{3,4,2,1,0:T(8,128)S(1)} %get-tuple-element.14, f32[2,2,2,256,256]{3,4,2,1,0:T(8,128)} %collective-permute-done.1, pred[]{:T(512)S(6)} %eq.17, f32[1,2,2,256,256]{3,4,2,1,0:T(8,128)S(1)} %get-tuple-element.27, ...), kind=kLoop, calls=%fused_computation.1 | loop fusion | flops 2097152 | bytes 8388609 | tf_op jit(solution)/shard_map/jit(_where)/select_n | solution.py:98
  113.6 0.7 collective-permute-start.2
  114.5 46.0 %collective-permute-done.2 = f32[2,2,2,256,256]{3,4,2,1,0:T(8,128)} collective-permute-done((f32[2,2,2,256,256]{3,4,2,1,0:T(8,128)}, f32[2,2,2,256,256]{3,4,2,1,0:T(8,128)}, u32[]{:S(2)}, u32[]{:S(2)}) %collective-permute-start.2) | collective-permute-done | bytes 2097184 | tf_op jit(solution)/shard_map/ppermute | solution.py:20
  160.5 3.1 fusion.105
  163.6 0.2 multiply_subtract_fusion.2
  163.8 1.0 copy-done.1
  164.8 4.6 %maximum_select_fusion.1 = f32[2,2,2,256,256]{3,4,2,1,0:T(8,128)} fusion(f32[1,2,2,256,256]{3,4,2,1,0:T(8,128)S(1)} %get-tuple-element.13, f32[1,2,2,256,256]{3,4,2,1,0:T(8,128)S(1)} %get-tuple-element.12, f32[2,2,2,256,256]{3,4,2,1,0:T(8,128)} %collective-permute-done.2, pred[]{:T(512)S(6)} %eq.18, f32[1,2,2,256,256]{3,4,2,1,0:T(8,128)S(1)} %copy-done.1, ...), kind=kLoop, calls=%fused_computation.2 | loop fusion | flops 3670016 | bytes 12582914 | tf_op jit(solution)/shard_map/jit(_where)/select_n | solution.py:98
  169.4 0.6 collective-permute-start.3
  170.0 0.1 fusion.60
  170.1 45.5 %collective-permute-done.3 = f32[2,2,2,256,256]{3,4,2,1,0:T(8,128)S(1)} collective-permute-done((f32[2,2,2,256,256]{3,4,2,1,0:T(8,128)}, f32[2,2,2,256,256]{3,4,2,1,0:T(8,128)S(1)}, u32[]{:S(2)}, u32[]{:S(2)}) %collective-permute-start.3) | collective-permute-done | bytes 2097184 | tf_op jit(solution)/shard_map/ppermute | solution.py:20
  215.6 1.9 sub.85
  217.4 0.2 multiply_subtract_fusion.1
  217.6 2.0 maximum_select_fusion.2
  219.6 2.0 fusion.38
  221.6 2.0 fusion.36
  223.6 2.0 fusion.1
  225.6 2.2 fusion
  227.8 0.1 multiply_subtract_fusion.10
  228.0 1.6 fusion.12
  229.5 1.6 fusion.16
  231.1 1.6 convolution_add_fusion.1
  232.7 1.7 fusion.11
  234.3 0.1 pad_maximum_fusion.1
  234.4 0.7 collective-permute-start.4
  235.1 0.1 fusion.9
  235.2 21.9 %collective-permute-done.4 = f32[2,2,256,256]{2,3,1,0:T(8,128)S(1)} collective-permute-done((f32[2,2,256,256]{2,3,1,0:T(8,128)S(1)}, f32[2,2,256,256]{2,3,1,0:T(8,128)S(1)}, u32[]{:S(2)}, u32[]{:S(2)}) %collective-permute-start.4) | collective-permute-done | bytes 1048608 | tf_op jit(solution)/shard_map/ppermute | solution.py:20
  257.1 0.1 multiply_subtract_fusion.8
  257.2 1.3 fusion.2
  258.5 3.3 collective-permute-start.5
  262.0 1.5 multiply_subtract_fusion.6
  263.4 19.2 %collective-permute-done.5 = f32[2,2,256,256]{2,3,1,0:T(8,128)S(1)} collective-permute-done((f32[2,2,256,256]{2,3,1,0:T(8,128)}, f32[2,2,256,256]{2,3,1,0:T(8,128)S(1)}, u32[]{:S(2)}, u32[]{:S(2)}) %collective-permute-start.5) | collective-permute-done | bytes 1048608 | tf_op jit(solution)/shard_map/ppermute | solution.py:20
  282.6 0.1 multiply_subtract_fusion.7
  282.8 0.9 copy-done.10
  283.6 1.7 fusion.3
  285.3 4.4 %collective-permute-start.6 = (f32[2,2,256,256]{2,3,1,0:T(8,128)S(1)}, f32[2,2,256,256]{2,3,1,0:T(8,128)S(1)}, u32[]{:S(2)}, u32[]{:S(2)}) collective-permute-start(f32[2,2,256,256]{2,3,1,0:T(8,128)S(1)} %fusion.3), channel_id=1, source_target_pairs={{0,8},{2,10},{4,12},{6,14},{8,0},{10,2},{12,4},{14,6},{1,9},{3,11}... | collective-permute-start | bytes 3145736 | tf_op jit(solution)/shard_map/ppermute | solution.py:20
  289.9 1.0 copy.17
  291.0 0.1 maximum_convert_fusion
  291.1 0.1 multiply_subtract_fusion.4
  291.2 41.0 %collective-permute-done.6 = f32[2,2,256,256]{2,3,1,0:T(8,128)S(1)} collective-permute-done((f32[2,2,256,256]{2,3,1,0:T(8,128)S(1)}, f32[2,2,256,256]{2,3,1,0:T(8,128)S(1)}, u32[]{:S(2)}, u32[]{:S(2)}) %collective-permute-start.6) | collective-permute-done | bytes 1048608 | tf_op jit(solution)/shard_map/ppermute | solution.py:20
  332.2 0.1 multiply_subtract_fusion.5
  332.3 0.0 copy-start.11
  332.3 0.3 fusion.4
  332.7 0.1 fusion.7
  332.8 0.2 copy-done.11
  333.0 0.3 fusion.28
  333.3 0.8 copy.21
  (28 shorter events, 0.3 us)
Async XLA Ops:
  1.6 9.0 %collective-permute-start = (bf16[3,2,256]{1,2,0:T(8,128)(2,1)S(1)}, bf16[3,2,256]{1,2,0:T(8,128)(2,1)S(1)}, u32[]{:S(2)}, u32[]{:S(2)}) collective-permute-start(bf16[3,2,256]{1,2,0:T(8,128)(2,1)S(1)} %copy.16), channel_id=1, source_target_pairs={{0,2},{2,4},{4,6},{6,8},{8,10},{10,12},{12,14},{1,3},{3,5},{5,7},{... | collective-permute-start | bytes 9224 | tf_op jit(solution)/shard_map/ppermute | solution.py:14
  13.3 94.5 %collective-permute-start.1 = (f32[2,2,2,256,256]{3,4,2,1,0:T(8,128)}, f32[2,2,2,256,256]{3,4,2,1,0:T(8,128)}, u32[]{:S(2)}, u32[]{:S(2)}) collective-permute-start(f32[2,2,2,256,256]{3,4,2,1,0:T(8,128)} %pad_maximum_fusion), channel_id=1, source_target_pairs={{0,8},{2,10},{4,12},{6,14},{8,0},{10,2},{12,4},{14,6},{1,9},{3,11}... | collective-permute-start | bytes 6291464 | tf_op jit(solution)/shard_map/ppermute | solution.py:20
  109.9 3.8 %copy-start = (f32[1,2,2,256,256]{3,4,2,1,0:T(8,128)}, f32[1,2,2,256,256]{3,4,2,1,0:T(8,128)S(1)}, u32[]{:S(2)}) copy-start(f32[1,2,2,256,256]{3,4,2,1,0:T(8,128)S(1)} %get-tuple-element.15) | copy-start | bytes 3145732
  113.6 46.9 %collective-permute-start.2 = (f32[2,2,2,256,256]{3,4,2,1,0:T(8,128)}, f32[2,2,2,256,256]{3,4,2,1,0:T(8,128)}, u32[]{:S(2)}, u32[]{:S(2)}) collective-permute-start(f32[2,2,2,256,256]{3,4,2,1,0:T(8,128)} %maximum_select_fusion), channel_id=1, source_target_pairs={{0,4},{2,6},{4,0},{6,2},{8,12},{10,14},{12,8},{14,10},{1,5},{3,7},... | collective-permute-start | bytes 6291464 | tf_op jit(solution)/shard_map/ppermute | solution.py:20
  163.6 1.2 copy-start.1
  169.4 46.2 %collective-permute-start.3 = (f32[2,2,2,256,256]{3,4,2,1,0:T(8,128)}, f32[2,2,2,256,256]{3,4,2,1,0:T(8,128)S(1)}, u32[]{:S(2)}, u32[]{:S(2)}) collective-permute-start(f32[2,2,2,256,256]{3,4,2,1,0:T(8,128)} %maximum_select_fusion.1), channel_id=1, source_target_pairs={{0,2},{2,0},{4,6},{6,4},{8,10},{10,8},{12,14},{14,12},{1,3},{3,1},... | collective-permute-start | bytes 6291464 | tf_op jit(solution)/shard_map/ppermute | solution.py:20
  234.3 22.8 %copy-start.4 = (f32[1,2,256,256]{2,3,1,0:T(8,128)}, f32[1,2,256,256]{2,3,1,0:T(8,128)S(1)}, u32[]{:S(2)}) copy-start(f32[1,2,256,256]{2,3,1,0:T(8,128)S(1)} %get-tuple-element.5) | copy-start | bytes 1572868
  234.4 22.6 %collective-permute-start.4 = (f32[2,2,256,256]{2,3,1,0:T(8,128)S(1)}, f32[2,2,256,256]{2,3,1,0:T(8,128)S(1)}, u32[]{:S(2)}, u32[]{:S(2)}) collective-permute-start(f32[2,2,256,256]{2,3,1,0:T(8,128)S(1)} %pad_maximum_fusion.1), channel_id=1, source_target_pairs={{0,2},{2,0},{4,6},{6,4},{8,10},{10,8},{12,14},{14,12},{1,3},{3,1},... | collective-permute-start | bytes 3145736 | tf_op jit(solution)/shard_map/ppermute | solution.py:20
  235.1 23.4 %copy-start.2 = (f32[1,2,256,256]{2,3,1,0:T(8,128)}, f32[1,2,256,256]{2,3,1,0:T(8,128)S(1)}, u32[]{:S(2)}) copy-start(f32[1,2,256,256]{2,3,1,0:T(8,128)S(1)} %fusion.9) | copy-start | bytes 1572868
  257.1 1.4 copy-start.6
  257.1 1.4 copy-start.8
  258.5 24.1 %collective-permute-start.5 = (f32[2,2,256,256]{2,3,1,0:T(8,128)}, f32[2,2,256,256]{2,3,1,0:T(8,128)S(1)}, u32[]{:S(2)}, u32[]{:S(2)}) collective-permute-start(f32[2,2,256,256]{2,3,1,0:T(8,128)} %fusion.2), channel_id=1, source_target_pairs={{0,4},{2,6},{4,0},{6,2},{8,12},{10,14},{12,8},{14,10},{1,5},{3,7},... | collective-permute-start | bytes 3145736 | tf_op jit(solution)/shard_map/ppermute | solution.py:20
  261.9 21.7 %copy-start.3 = (f32[1,2,256,256]{2,3,1,0:T(8,128)S(1)}, f32[1,2,256,256]{2,3,1,0:T(8,128)}, u32[]{:S(2)}) copy-start(f32[1,2,256,256]{2,3,1,0:T(8,128)} %copy-done.2) | copy-start | bytes 1572868
  262.0 21.7 %copy-start.5 = (f32[1,2,256,256]{2,3,1,0:T(8,128)S(1)}, f32[1,2,256,256]{2,3,1,0:T(8,128)}, u32[]{:S(2)}) copy-start(f32[1,2,256,256]{2,3,1,0:T(8,128)} %copy-done.4) | copy-start | bytes 1572868
  262.0 21.7 %copy-start.7 = (f32[1,2,256,256]{2,3,1,0:T(8,128)S(1)}, f32[1,2,256,256]{2,3,1,0:T(8,128)}, u32[]{:S(2)}) copy-start(f32[1,2,256,256]{2,3,1,0:T(8,128)} %copy-done.6) | copy-start | bytes 1572868
  262.0 21.7 %copy-start.9 = (f32[1,2,256,256]{2,3,1,0:T(8,128)S(1)}, f32[1,2,256,256]{2,3,1,0:T(8,128)}, u32[]{:S(2)}) copy-start(f32[1,2,256,256]{2,3,1,0:T(8,128)} %copy-done.8) | copy-start | bytes 1572868
  282.6 1.0 copy-start.10
  285.3 46.8 %collective-permute-start.6 = (f32[2,2,256,256]{2,3,1,0:T(8,128)S(1)}, f32[2,2,256,256]{2,3,1,0:T(8,128)S(1)}, u32[]{:S(2)}, u32[]{:S(2)}) collective-permute-start(f32[2,2,256,256]{2,3,1,0:T(8,128)S(1)} %fusion.3), channel_id=1, source_target_pairs={{0,8},{2,10},{4,12},{6,14},{8,0},{10,2},{12,4},{14,6},{1,9},{3,11}... | collective-permute-start | bytes 3145736 | tf_op jit(solution)/shard_map/ppermute | solution.py:20
  332.3 0.7 copy-start.11
where the time goes:
time: 335 us; the launch traced here: 334 us
  waiting for transfers between devices  263 us (79%)
  other arithmetic  27.7 us (8%)
  starting transfers between devices  19 us (6%)
  matrix products  14.5 us (4%)
  local copies, waits for them, and re-layouts  8.45 us (3%)
    ppermute x6, waiting for transfers between devices, from_partner(): return lax.ppermute(value, axis, pairs)  263 us
    ppermute x6, starting transfers between devices, from_partner(): return lax.ppermute(value, axis, pairs)  14.1 us
    select_n x3, other arithmetic, body(): current = jnp.where(is_lower, current + received, turned)  10.3 us
    sub x3, other arithmetic, body(): differ = received - current  6.82 us
  transfers between devices with their start and end apart: 7, of which 7 were waited for; matrix products, arithmetic and copies ran while one was open for 2% of the time, Pallas kernels for 0%

commit v1 on v0

v1 whole, which is shorter than its diff:
```python
import math

import numpy as np

import jax
import jax.numpy as jnp
from jax import lax
from jax.sharding import PartitionSpec as P

full_precision = lax.Precision.HIGHEST


def transform_tables(blocks, rows):
    total = 2 * blocks * rows
    k2 = np.arange(blocks + 1)
    d = np.arange(blocks)
    r = np.arange(rows)
    block_angle = 2.0 * np.pi * np.outer(k2, d) / (2 * blocks)
    first = np.concatenate([np.cos(block_angle), -np.sin(block_angle)], axis=0)
    twist_angle = -2.0 * np.pi * np.outer(k2, r) / total
    twist = np.stack([np.cos(twist_angle), np.sin(twist_angle)])
    row_angle = 2.0 * np.pi * np.outer(r, r) / rows
    cosine, sine = np.cos(row_angle), np.sin(row_angle)
    forward = np.block([[cosine, -sine], [sine, cosine]])
    backward = np.block([[cosine, sine], [-sine, cosine]])
    weight = np.full(blocks + 1, 2.0)
    weight[0] = 1.0
    weight[-1] = 1.0
    last_angle = 2.0 * np.pi * np.outer(d, k2) / (2 * blocks)
    last = np.concatenate(
        [weight * np.cos(last_angle), -weight * np.sin(last_angle)], axis=1
    ) / total
    as_f32 = lambda a: jnp.asarray(a.astype(np.float32))
    return tuple(as_f32(a) for a in (first, twist, forward, backward, last))


def shifted(x, lag):
    if lag == 0:
        return x
    earlier = jnp.concatenate([jnp.zeros_like(x[:1]), x[:-1]], axis=0)
    return jnp.concatenate([earlier[:, :, -lag:], x[:, :, :-lag]], axis=2)


def short_conv(x, kernel):
    summed = kernel[0][None, :, None] * x
    for lag in range(1, kernel.shape[0]):
        summed = summed + kernel[lag][None, :, None] * shifted(x, lag)
    return summed


def complex_rows(re, im, table):
    both = jnp.concatenate([re, im], axis=-1)
    out = jnp.einsum("...j,jk->...k", both, table, precision=full_precision)
    half = out.shape[-1] // 2
    return out[..., :half], out[..., half:]


def body(gate_stream, outer_stream, value_stream, short_weight, long_filter, skip_gain):
    rows, chans = gate_stream.shape
    blocks = lax.axis_size("ctx")
    piece = chans // blocks
    me = lax.axis_index("ctx")
    first, twist, forward, backward, last = transform_tables(blocks, rows)

    stacked = jnp.stack([gate_stream, value_stream, outer_stream, long_filter])
    stacked = jnp.swapaxes(stacked, 1, 2).reshape(4, blocks, piece, rows)
    gathered = lax.all_to_all(stacked, "ctx", 1, 1)
    signals = gathered.astype(jnp.float32)

    kernels = lax.dynamic_slice_in_dim(short_weight, me * piece, piece, axis=2).astype(jnp.float32)
    gain = lax.dynamic_slice_in_dim(skip_gain, me * piece, piece)

    gate_conv = short_conv(signals[0], kernels[0])
    value_conv = short_conv(signals[1], kernels[2])
    outer_conv = short_conv(signals[2], kernels[1])
    gated_value = gate_conv * value_conv

    pair = jnp.stack([gated_value, signals[3]])
    spread = jnp.einsum("kd,sdcr->skcr", first, pair, precision=full_precision)
    half = blocks + 1
    a_re, a_im = spread[:, :half], spread[:, half:]
    t_re = twist[0][None, :, None, :]
    t_im = twist[1][None, :, None, :]
    b_re = a_re * t_re - a_im * t_im
    b_im = a_re * t_im + a_im * t_re
    x_re, x_im = complex_rows(b_re, b_im, forward)
    q_re = x_re[0] * x_re[1] - x_im[0] * x_im[1]
    q_im = x_re[0] * x_im[1] + x_im[0] * x_re[1]
    y_re, y_im = complex_rows(q_re, q_im, backward)
    u_re = y_re * twist[0][:, None, :] + y_im * twist[1][:, None, :]
    u_im = y_im * twist[0][:, None, :] - y_re * twist[1][:, None, :]
    long_part = jnp.einsum(
        "dk,kcr->dcr", last, jnp.concatenate([u_re, u_im], axis=0), precision=full_precision
    )

    out = outer_conv * (long_part + gain[None, :, None] * gated_value)
    out = out.astype(jnp.bfloat16)
    returned = lax.all_to_all(out, "ctx", 0, 0)
    return jnp.swapaxes(returned.reshape(chans, rows), 0, 1)


def solution(mesh):
    placed = (
        P(("groups", "ctx"), "ch"),
        P(("groups", "ctx"), "ch"),
        P(("groups", "ctx"), "ch"),
        P(None, None, "ch"),
        P("ctx", "ch"),
        P("ch"),
    )
    return jax.shard_map(
        body, mesh=mesh, in_specs=placed, out_specs=P(("groups", "ctx"), "ch"), check_vma=False
    )
```

time: 335 us -> 57.6 us (0.17)
  waiting for transfers between devices: 263 us -> 13.1 us
  other arithmetic: 27.7 us -> 2.92 us
  starting transfers between devices: 19 us -> 7.25 us
  blocking collectives: 0 us -> 10.8 us
  matrix products: 14.5 us -> 7.26 us
  local copies, waits for them, and re-layouts: 8.45 us -> 15.4 us
    ppermute x7 -> x0, waiting for transfers between devices: 263 us -> none  [the longest x6 263 us: from_partner(): return lax.ppermute(value, axis, pairs)]
    ppermute x7 -> x0, starting transfers between devices: 19 us -> none  [the longest x6 14.1 us: from_partner(): return lax.ppermute(value, axis, pairs)]
    select_n x6 -> x0, other arithmetic: 13.7 us -> none  [the longest x3 10.3 us: body(): current = jnp.where(is_lower, current + received, turned)]
    all_to_all x0 -> x1, waiting for transfers between devices: none -> 13.1 us  [body(): gathered = lax.all_to_all(stacked, 'ctx', 1, 1)]
    all_to_all x0 -> x1, blocking collectives: none -> 10.8 us  [body(): returned = lax.all_to_all(out, 'ctx', 0, 0)]
    sub x12 -> x2, other arithmetic: 9.5 us -> 0.39 us  [the longest x1 0.31 us: body(): b_re = a_re * t_re - a_im * t_im]
    all_to_all x0 -> x1, starting transfers between devices: none -> 7.25 us  [body(): gathered = lax.all_to_all(stacked, 'ctx', 1, 1)]
    dot_general x8 -> x4, matrix products: 14.5 us -> 7.26 us  [the longest x2 3.77 us: complex_rows(): out = jnp.einsum('...j,jk->...k', both, table, precision=full_precision)]
  transfers between devices with their start and end apart: 7 -> 1, of which waited for: 7 -> 1; matrix products, arithmetic and copies ran while one was open for 2% -> 2% of each run, Pallas kernels for 0% -> 0%
where the time goes in v1:
time: 57.6 us; the launch traced here: 57.1 us
  local copies, waits for them, and re-layouts  15.4 us (27%)
  waiting for transfers between devices  13.1 us (23%)
  blocking collectives  10.8 us (19%)
  matrix products  7.26 us (13%)
  starting transfers between devices  7.25 us (13%)
  other arithmetic  2.92 us (5%)
    all_to_all x1, waiting for transfers between devices, body(): gathered = lax.all_to_all(stacked, 'ctx', 1, 1)  13.1 us
    all_to_all x1, blocking collectives, body(): returned = lax.all_to_all(out, 'ctx', 0, 0)  10.8 us
    all_to_all x1, starting transfers between devices, body(): gathered = lax.all_to_all(stacked, 'ctx', 1, 1)  7.25 us
    unnamed x46, local copies, waits for them, and re-layouts  7 us
    dot_general x2, matrix products, complex_rows(): out = jnp.einsum('...j,jk->...k', both, table, precision=full_precision)  3.77 us
    slice x8, local copies, waits for them, and re-layouts, shifted(): return jnp.concatenate([earlier[:, :, -lag:], x[:, :, :-lag]], axis=2)  3.75 us
    dot_general x1, matrix products, body(): spread = jnp.einsum('kd,sdcr->skcr', first, pair, precision=full_precision)  2.12 us
    mul x1, other arithmetic, body(): gated_value = gate_conv * value_conv  1.64 us
  transfers between devices with their start and end apart: 1, of which 1 were waited for; matrix products, arithmetic and copies ran while one was open for 2% of the time, Pallas kernels for 0%

profile of v1, /device:TPU:0, one launch (start us, length us, event | category | flops | bytes accessed | tf_op | source)
XLA Modules:
  0.0 57.1 jit_solution(11432889425278784420)
XLA Ops:
  0.0 1.0 %copy.29 = bf16[256,256]{0,1:T(8,128)(2,1)S(1)} copy(bf16[256,256]{1,0:T(8,128)(2,1)} %param.11) | data formatting | bytes 262144 | tf_op args[0]
  1.0 1.0 %copy.31 = bf16[256,256]{0,1:T(8,128)(2,1)S(1)} copy(bf16[256,256]{1,0:T(8,128)(2,1)} %param.12) | data formatting | bytes 262144 | tf_op args[1]
  2.0 1.0 %copy.30 = bf16[256,256]{0,1:T(8,128)(2,1)S(1)} copy(bf16[256,256]{1,0:T(8,128)(2,1)} %param.13) | data formatting | bytes 262144 | tf_op args[2]
  3.0 1.0 %copy.32 = bf16[256,256]{0,1:T(8,128)(2,1)S(1)} copy(bf16[256,256]{1,0:T(8,128)(2,1)} %param.15) | data formatting | bytes 262144 | tf_op args[4]
  4.0 0.0 copy-start.20
  4.1 0.0 copy-start.18
  4.1 0.1 pad_maximum_fusion.2
  4.1 0.8 %copy.33 = bf16[4,8,32,256]{3,2,0,1:T(8,128)(2,1)} copy(bf16[4,8,32,256]{3,2,1,0:T(8,128)(2,1)S(1)} %bitcast.82) | data formatting | bytes 1048576 | tf_op jit(solution)/shard_map/reshape | solution.py:66
  5.0 7.3 %all-to-all-start = ((bf16[4,8,32,256]{3,2,0,1:T(8,128)(2,1)}), bf16[4,8,32,256]{3,2,0,1:T(8,128)(2,1)S(1)}, u32[]{:S(2)}, u32[]{:S(2)}) async-start(bf16[4,8,32,256]{3,2,0,1:T(8,128)(2,1)} %copy.33), calls=%async_computation | async-start | bytes 1048576 | tf_op jit(solution)/shard_map/all_to_all | solution.py:67
  12.2 0.0 copy-done.20
  12.2 0.7 %dynamic_slice.7 = f32[32]{0:T(128)} dynamic-slice(f32[256]{0:T(256)S(1)} %copy-done.20, s32[]{:T(128)S(6)} %select_n.4), dynamic_slice_sizes={32} | dynamic-slice | bytes 260 | tf_op jit(solution)/shard_map/dynamic_slice | solution.py:71
  12.9 0.0 copy-done.18
  12.9 0.1 dynamic-slice_convert_fusion
  13.0 0.6 %slice_bitcast_fusion.14 = (f32[32]{0:T(128)}, f32[32]{0:T(128)S(1)}, f32[32]{0:T(128)S(1)}, f32[32]{0:T(128)}, f32[32]{0:T(128)}, /*index=5*/f32[32]{0:T(128)}, f32[32]{0:T(128)}, f32[32]{0:T(128)}, f32[32]{0:T(128)}) fusion(f32[3,3,32]{2,1,0:T(4,128)S(1)} %dynamic-slice_convert_fusion), kind=kLoop, calls=%fused_computation.68 | loop fusion | bytes 2304 | tf_op jit(solution)/shard_map/mul | solution.py:45
  13.6 13.1 %all-to-all-done = bf16[4,8,32,256]{3,2,0,1:T(8,128)(2,1)S(1)} async-done(((bf16[4,8,32,256]{3,2,0,1:T(8,128)(2,1)}), bf16[4,8,32,256]{3,2,0,1:T(8,128)(2,1)S(1)}, u32[]{:S(2)}, u32[]{:S(2)}) %all-to-all-start) | async-done | bytes 524320 | tf_op jit(solution)/shard_map/all_to_all | solution.py:67
  26.7 0.3 copy_convert_fusion
  27.0 0.1 slice_bitcast_fusion.2
  27.1 0.8 %pad_slice_fusion.4 = f32[8,32,2]{2,0,1:T(8,128)} fusion(f32[7,32,256]{2,0,1:T(8,128)S(1)} %get-tuple-element.9), kind=kLoop, calls=%fused_computation.57 | loop fusion | bytes 231424 | tf_op jit(solution)/shard_map/slice | solution.py:41
  27.9 0.8 %pad_slice_fusion.5 = f32[8,32,1]{2,0,1:T(8,128)} fusion(f32[7,32,256]{2,0,1:T(8,128)S(1)} %get-tuple-element.9), kind=kLoop, calls=%fused_computation.58 | loop fusion | bytes 230400 | tf_op jit(solution)/shard_map/slice | solution.py:41
  28.6 0.1 pad_slice_fusion.1
  28.8 1.0 %pad_slice_fusion = (f32[8,32,2]{2,0,1:T(8,128)}, f32[1,8,32,2]{3,1,2,0:T(8,128)}, f32[1,8,32,2]{3,1,2,0:T(8,128)}, f32[8,32,2]{2,0,1:T(8,128)}) fusion(f32[7,32,256]{2,0,1:T(8,128)S(1)} %get-tuple-element.10, f32[7,32,256]{2,0,1:T(8,128)S(1)} %get-tuple-element.11), kind=kLoop, calls=%fused_computation.53 | loop fusion | bytes 466944 | tf_op jit(solution)/shard_map/slice | solution.py:41
  29.7 0.8 %slice_bitcast_fusion.3 = (f32[8,32,256]{2,0,1:T(8,128)S(1)}, f32[8,32,256]{2,0,1:T(8,128)S(1)}, f32[1,8,32,256]{3,1,2,0:T(8,128)}, f32[8,32,256]{2,0,1:T(8,128)S(1)}) fusion(f32[4,8,32,256]{3,1,2,0:T(8,128)S(1)} %copy_convert_fusion), kind=kLoop, calls=%fused_computation.27 | loop fusion | bytes 2097152 | tf_op jit(solution)/shard_map/squeeze | solution.py:75
  30.5 0.1 fusion.29
  30.6 0.8 %fusion.30 = (f32[8,32,255]{2,0,1:T(8,128)S(1)}, f32[1,8,32,255]{3,1,2,0:T(8,128)S(1)}, f32[1,8,32,255]{3,1,2,0:T(8,128)S(1)}, f32[8,32,255]{2,0,1:T(8,128)}) fusion(f32[8,32,256]{2,0,1:T(8,128)S(1)} %get-tuple-element.13, f32[8,32,256]{2,0,1:T(8,128)S(1)} %get-tuple-element.15), kind=kLoop, calls=%fused_computation.78 | loop fusion | bytes 1566720 | tf_op jit(solution)/shard_map/slice | solution.py:41
  31.4 0.1 copy.37
  31.5 0.1 copy.35
  31.6 0.2 copy.36
  31.8 0.8 %copy.38 = f32[1,8,32,1]{3,1,2,0:T(8,128)} copy(f32[1,8,32,1]{2,1,3,0:T(8,128)S(1)} %bitcast.88) | data formatting | bytes 2048 | tf_op jit(solution)/shard_map/concatenate | solution.py:41
  32.6 1.6 %fusion.16 = f32[1,8,32,256]{3,1,2,0:T(8,128)S(1)} fusion(f32[1,8,32,255]{3,1,2,0:T(8,128)S(1)} %get-tuple-element.41, f32[1,8,32,1]{3,1,2,0:T(8,128)S(1)} %copy.36, f32[1,8,32,254]{3,1,2,0:T(8,128)S(1)} %get-tuple-element.39, f32[1,8,32,2]{3,1,2,0:T(8,128)} %get-tuple-element.43, f32[1,8,32,255]{3,1,2,0:T(8,128)S(1)} %get-tuple-element.23, ...), kind=kLoop, calls=%fused_computation.35 | loop fusion | flops 983040 | bytes 1835776 | tf_op jit(solution)/shard_map/mul | solution.py:76
  34.2 0.0 copy-start.8
  34.2 0.0 copy-start.9
  34.3 0.0 copy-done.3
  34.3 2.1 %convolution_bitcast_fusion = f32[2,18,32,256]{3,1,2,0:T(8,128)S(1)} fusion(f32[18,8,1,1]{0,1,3,2:T(8,128)} %constant.40, f32[1,8,32,256]{3,1,2,0:T(8,128)S(1)} %copy-done.3, f32[1,8,32,256]{3,1,2,0:T(8,128)S(1)} %fusion.16), kind=kOutput, calls=%fused_computation.1 | convolution fusion | flops 28442624 | bytes 1704512 | tf_op jit(solution)/shard_map/kd,sdcr->skcr/dot_general | solution.py:79
  36.4 0.0 copy-done.8
  36.4 0.0 copy-done.9
  36.4 0.3 multiply_subtract_fusion
  36.7 0.0 copy-start.1
  36.7 0.3 pad_maximum_fusion
  37.1 0.9 %copy-done.1 = f32[512,512,1,1]{1,0,3,2:T(8,128)S(1)} copy-done((f32[512,512,1,1]{1,0,3,2:T(8,128)S(1)}, f32[512,512,1,1]{1,0,3,2:T(8,128)}, u32[]{:S(2)}) %copy-start.1) | copy-done | bytes 1048600
  38.0 2.6 %fusion = f32[2,9,32,512]{3,2,1,0:T(8,128)S(1)} fusion(f32[512,512,1,1]{1,0,3,2:T(8,128)S(1)} %copy-done.1, f32[2,9,32,512]{3,1,2,0:T(8,128)S(1)} %pad_maximum_fusion), kind=kOutput, calls=%fused_computation.2 | convolution fusion | flops 1811939328 | bytes 3407872 | tf_op jit(solution)/shard_map/...j,jk->...k/dot_general | solution.py:53
  40.6 0.0 copy-start
  40.6 0.1 subtract_bitcast_fusion
  40.7 1.1 %copy-done = f32[512,512,1]{1,0,2:T(8,128)S(1)} copy-done((f32[512,512,1]{1,0,2:T(8,128)S(1)}, f32[512,512,1]{1,0,2:T(8,128)}, u32[]{:S(2)}) %copy-start) | copy-done | bytes 1048600
  41.8 1.2 %fusion.5 = f32[9,32,512]{2,1,0:T(8,128)S(1)} fusion(f32[512,512,1]{1,0,2:T(8,128)S(1)} %copy-done, f32[9,32,256]{2,1,0:T(8,128)S(1)} %get-tuple-element.8, f32[9,32,256]{2,1,0:T(8,128)S(1)} %get-tuple-element.7), kind=kOutput, calls=%fused_computation.10 | convolution fusion | flops 906117120 | bytes 2228224 | tf_op jit(solution)/shard_map/...j,jk->...k/dot_general | solution.py:53
  43.0 0.0 copy-start.2
  43.0 0.0 copy-start.4
  43.0 0.0 copy-start.5
  43.0 0.0 copy-start.6
  43.0 0.0 copy-start.7
  43.0 0.0 copy-start.10
  43.0 0.0 copy-start.11
  43.0 0.0 copy-start.12
  43.1 0.0 copy-start.14
  43.1 0.1 multiply_add_fusion.1
  43.3 0.7 %copy-done.2 = f32[8,32,255]{2,0,1:T(8,128)S(1)} copy-done((f32[8,32,255]{2,0,1:T(8,128)S(1)}, f32[8,32,255]{2,0,1:T(8,128)}, u32[]{:S(2)}) %copy-start.2) | copy-done | bytes 261144
  43.9 0.0 copy-done.4
  44.0 0.1 copy-done.5
  44.0 0.1 copy-done.6
  44.1 0.0 copy-done.7
  44.1 0.0 copy-done.10
  44.1 0.0 copy-done.12
  44.2 1.4 %fusion.3 = bf16[8,32,256]{2,0,1:T(8,128)(2,1)S(1)} fusion(f32[8,18,1]{1,0,2:T(8,128)S(1)} %copy-done.14, f32[18,32,256]{2,1,0:T(8,128)S(1)} %pad_maximum_fusion.1, f32[8,32,255]{2,0,1:T(8,128)S(1)} %bitcast.80, f32[8,32,1]{2,0,1:T(8,128)S(1)} %copy-done.5, f32[8,32,254]{2,0,1:T(8,128)S(1)} %bitcast.81, f32[8,32,2]{2,0,1:T(8,128)S(1)} %copy-done.4, ...), kind=kOutput, calls=%fused_computation.6 | convolution fusion | flops 15859712 | bytes 3082048 | tf_op jit(solution)/shard_map/dk,kcr->dcr/dot_general | solution.py:92
  45.6 10.8 %all_to_all.10 = bf16[8,32,256]{2,1,0:T(8,128)(2,1)S(1)} all-to-all(bf16[8,32,256]{2,1,0:T(8,128)(2,1)S(1)} %copy.41), channel_id=1, replica_groups=mesh['groups'=2,'ctx'=8,'ch'=2] {'ctx'}, dimensions={0} | all-to-all | bytes 262144 | tf_op jit(solution)/shard_map/all_to_all | solution.py:98
  56.4 0.8 %copy.42 = bf16[256,256]{1,0:T(8,128)(2,1)} copy(bf16[256,256]{0,1:T(8,128)(2,1)S(1)} %bitcast.83) | data formatting | bytes 262144 | tf_op jit(solution)/shard_map/transpose | solution.py:99
  (15 shorter events, 0.1 us)
Async XLA Ops:
  4.0 8.2 %copy-start.20 = (f32[256]{0:T(256)S(1)}, f32[256]{0:T(256)}, u32[]{:S(2)}) copy-start(f32[256]{0:T(256)} %param.16) | copy-start | bytes 3076
  4.1 8.9 %copy-start.18 = (bf16[3,3,256]{2,1,0:T(4,128)(2,1)S(1)}, bf16[3,3,256]{2,1,0:T(4,128)(2,1)}, u32[]{:S(2)}) copy-start(bf16[3,3,256]{2,1,0:T(4,128)(2,1)} %param.14) | copy-start | bytes 13828
  5.0 21.7 %all-to-all-start = ((bf16[4,8,32,256]{3,2,0,1:T(8,128)(2,1)}), bf16[4,8,32,256]{3,2,0,1:T(8,128)(2,1)S(1)}, u32[]{:S(2)}, u32[]{:S(2)}) async-start(bf16[4,8,32,256]{3,2,0,1:T(8,128)(2,1)} %copy.33), calls=%async_computation | async-start | bytes 1048576 | tf_op jit(solution)/shard_map/all_to_all | solution.py:67
  32.6 1.7 %copy-start.3 = (f32[1,8,32,256]{3,1,2,0:T(8,128)S(1)}, f32[1,8,32,256]{3,1,2,0:T(8,128)}, u32[]{:S(2)}) copy-start(f32[1,8,32,256]{3,1,2,0:T(8,128)} %get-tuple-element.14) | copy-start | bytes 786436
  34.2 2.2 %copy-start.8 = (f32[9,256]{1,0:T(8,128)S(1)}, f32[9,256]{1,0:T(8,128)}, u32[]{:S(2)}) copy-start(f32[9,256]{1,0:T(8,128)} %constant.38) | copy-start | bytes 27652
  34.2 2.2 %copy-start.9 = (f32[9,256]{1,0:T(8,128)S(1)}, f32[9,256]{1,0:T(8,128)}, u32[]{:S(2)}) copy-start(f32[9,256]{1,0:T(8,128)} %constant.36) | copy-start | bytes 27652
  36.7 1.2 %copy-start.1 = (f32[512,512,1,1]{1,0,3,2:T(8,128)S(1)}, f32[512,512,1,1]{1,0,3,2:T(8,128)}, u32[]{:S(2)}) copy-start(f32[512,512,1,1]{1,0,3,2:T(8,128)} %constant.41) | copy-start | bytes 3145732
  40.6 1.2 %copy-start = (f32[512,512,1]{1,0,2:T(8,128)S(1)}, f32[512,512,1]{1,0,2:T(8,128)}, u32[]{:S(2)}) copy-start(f32[512,512,1]{1,0,2:T(8,128)} %constant.42) | copy-start | bytes 3145732
  43.0 1.0 %copy-start.2 = (f32[8,32,255]{2,0,1:T(8,128)S(1)}, f32[8,32,255]{2,0,1:T(8,128)}, u32[]{:S(2)}) copy-start(f32[8,32,255]{2,0,1:T(8,128)} %get-tuple-element.42) | copy-start | bytes 783364
  43.0 1.0 %copy-start.4 = (f32[8,32,2]{2,0,1:T(8,128)S(1)}, f32[8,32,2]{2,0,1:T(8,128)}, u32[]{:S(2)}) copy-start(f32[8,32,2]{2,0,1:T(8,128)} %pad_slice_fusion.4) | copy-start | bytes 6148
  43.0 1.0 %copy-start.5 = (f32[8,32,1]{2,0,1:T(8,128)S(1)}, f32[8,32,1]{2,0,1:T(8,128)}, u32[]{:S(2)}) copy-start(f32[8,32,1]{2,0,1:T(8,128)} %pad_slice_fusion.5) | copy-start | bytes 3076
  43.0 1.1 %copy-start.6 = (f32[8,32,2]{2,0,1:T(8,128)S(1)}, f32[8,32,2]{2,0,1:T(8,128)}, u32[]{:S(2)}) copy-start(f32[8,32,2]{2,0,1:T(8,128)} %get-tuple-element.18) | copy-start | bytes 6148
  43.0 1.1 %copy-start.7 = (f32[8,32,2]{2,0,1:T(8,128)S(1)}, f32[8,32,2]{2,0,1:T(8,128)}, u32[]{:S(2)}) copy-start(f32[8,32,2]{2,0,1:T(8,128)} %get-tuple-element.44) | copy-start | bytes 6148
  43.0 1.1 %copy-start.10 = (f32[32]{0:T(128)S(1)}, f32[32]{0:T(128)}, u32[]{:S(2)}) copy-start(f32[32]{0:T(128)} %get-tuple-element.33) | copy-start | bytes 388
  43.0 1.1 %copy-start.11 = (f32[32]{0:T(128)S(1)}, f32[32]{0:T(128)}, u32[]{:S(2)}) copy-start(f32[32]{0:T(128)} %get-tuple-element.34) | copy-start | bytes 388
  43.0 1.1 %copy-start.12 = (f32[32]{0:T(128)S(1)}, f32[32]{0:T(128)}, u32[]{:S(2)}) copy-start(f32[32]{0:T(128)} %get-tuple-element.35) | copy-start | bytes 388
  43.1 1.1 %copy-start.13 = (f32[32]{0:T(128)S(1)}, f32[32]{0:T(128)}, u32[]{:S(2)}) copy-start(f32[32]{0:T(128)} %get-tuple-element.36) | copy-start | bytes 388
  43.1 1.1 %copy-start.14 = (f32[8,18,1]{1,0,2:T(8,128)S(1)}, f32[8,18,1]{1,0,2:T(8,128)}, u32[]{:S(2)}) copy-start(f32[8,18,1]{1,0,2:T(8,128)} %constant.39) | copy-start | bytes 1732
  43.1 1.1 %copy-start.15 = (f32[32]{0:T(128)S(1)}, f32[32]{0:T(128)}, u32[]{:S(2)}) copy-start(f32[32]{0:T(128)} %get-tuple-element.30) | copy-start | bytes 388
  43.1 1.1 %copy-start.16 = (f32[32]{0:T(128)S(1)}, f32[32]{0:T(128)}, u32[]{:S(2)}) copy-start(f32[32]{0:T(128)} %get-tuple-element.37) | copy-start | bytes 388
  43.1 1.1 %copy-start.17 = (f32[32]{0:T(128)S(1)}, f32[32]{0:T(128)}, u32[]{:S(2)}) copy-start(f32[32]{0:T(128)} %get-tuple-element.38) | copy-start | bytes 388
  43.1 1.1 %copy-start.19 = (f32[32]{0:T(128)S(1)}, f32[32]{0:T(128)}, u32[]{:S(2)}) copy-start(f32[32]{0:T(128)} %dynamic_slice.7) | copy-start | bytes 388

commit v2 on v1

--- a/solution.py
+++ b/solution.py
@@ -55,6 +55,17 @@
     return out[..., :half], out[..., half:]
 
 
+def exchange(x, count, me, axis):
+    received = [lax.index_in_dim(lax.dynamic_slice_in_dim(x, me, 1, axis), 0, axis, keepdims=False)]
+    for distance in range(1, count):
+        pairs = [(i, (i + distance) % count) for i in range(count)]
+        part = lax.dynamic_slice_in_dim(x, (me + distance) % count, 1, axis)
+        received.append(lax.index_in_dim(lax.ppermute(part, "ctx", pairs), 0, axis, keepdims=False))
+    by_distance = jnp.stack(received, axis=axis)
+    order = (me - jnp.arange(count, dtype=jnp.int32)) % count
+    return jnp.take(by_distance, order, axis=axis)
+
+
 def body(gate_stream, outer_stream, value_stream, short_weight, long_filter, skip_gain):
     rows, chans = gate_stream.shape
     blocks = lax.axis_size("ctx")
@@ -64,7 +75,7 @@
 
     stacked = jnp.stack([gate_stream, value_stream, outer_stream, long_filter])
     stacked = jnp.swapaxes(stacked, 1, 2).reshape(4, blocks, piece, rows)
-    gathered = lax.all_to_all(stacked, "ctx", 1, 1)
+    gathered = exchange(stacked, blocks, me, 1)
     signals = gathered.astype(jnp.float32)
 
     kernels = lax.dynamic_slice_in_dim(short_weight, me * piece, piece, axis=2).astype(jnp.float32)
@@ -95,7 +106,7 @@
 
     out = outer_conv * (long_part + gain[None, :, None] * gated_value)
     out = out.astype(jnp.bfloat16)
-    returned = lax.all_to_all(out, "ctx", 0, 0)
+    returned = exchange(out, blocks, me, 0)
     return jnp.swapaxes(returned.reshape(chans, rows), 0, 1)
 
 

time: 57.6 us -> 67.8 us (1.18)
  starting transfers between devices: 7.25 us -> 18.9 us
  blocking collectives: 10.8 us -> 0 us
  waiting for transfers between devices: 13.1 us -> 21.7 us
  local copies, waits for them, and re-layouts: 15.4 us -> 16.6 us
    ppermute x0 -> x14, waiting for transfers between devices: none -> 21.7 us  [exchange(): lax.ppermute(part, 'ctx', pairs)]
    ppermute x0 -> x14, starting transfers between devices: none -> 18.9 us  [exchange(): lax.ppermute(part, 'ctx', pairs)]
    all_to_all x1 -> x0, waiting for transfers between devices: 13.1 us -> none  [body(): gathered = lax.all_to_all(stacked, 'ctx', 1, 1)]
    all_to_all x1 -> x0, blocking collectives: 10.8 us -> none  [body(): returned = lax.all_to_all(out, 'ctx', 0, 0)]
    all_to_all x1 -> x0, starting transfers between devices: 7.25 us -> none  [body(): gathered = lax.all_to_all(stacked, 'ctx', 1, 1)]
    gather x0 -> x2, local copies, waits for them, and re-layouts: none -> 1.14 us  [exchange(): return jnp.take(by_distance, order, axis=axis)]
    reshape x1 -> x0, local copies, waits for them, and re-layouts: 0.84 us -> none  [body(): stacked = jnp.swapaxes(stacked, 1, 2).reshape(4, blocks, piece, rows)]
    dot_general x1, matrix products: 2.12 us -> 1.43 us  [body(): spread = jnp.einsum('kd,sdcr->skcr', first, pair, precision=full_precision)]
  transfers between devices with their start and end apart: 1 -> 14, of which waited for: 1 -> 6; matrix products, arithmetic and copies ran while one was open for 2% -> 2% of each run, Pallas kernels for 0% -> 0%
where the time goes in v2:
time: 67.8 us; the launch traced here: 67.5 us
  waiting for transfers between devices  21.7 us (32%)
  starting transfers between devices  18.9 us (28%)
  local copies, waits for them, and re-layouts  16.6 us (24%)
  matrix products  6.6 us (10%)
  other arithmetic  3.11 us (5%)
    ppermute x14, waiting for transfers between devices, exchange(): lax.ppermute(part, 'ctx', pairs)  21.7 us
    ppermute x14, starting transfers between devices, exchange(): lax.ppermute(part, 'ctx', pairs)  18.9 us
    unnamed x60, local copies, waits for them, and re-layouts  7.07 us
    dot_general x2, matrix products, complex_rows(): out = jnp.einsum('...j,jk->...k', both, table, precision=full_precision)  3.8 us
    slice x8, local copies, waits for them, and re-layouts, shifted(): return jnp.concatenate([earlier[:, :, -lag:], x[:, :, :-lag]], axis=2)  3.74 us
    mul x1, other arithmetic, body(): gated_value = gate_conv * value_conv  1.66 us
    dot_general x1, matrix products, body(): spread = jnp.einsum('kd,sdcr->skcr', first, pair, precision=full_precision)  1.43 us
    dot_general x1, matrix products, body(): jnp.einsum('dk,kcr->dcr', last, jnp.concatenate([u_re, u_im], axis=0), pr...  1.37 us
  transfers between devices with their start and end apart: 14, of which 6 were waited for; matrix products, arithmetic and copies ran while one was open for 2% of the time, Pallas kernels for 0%

profile of v2, /device:TPU:0, one launch (start us, length us, event | category | flops | bytes accessed | tf_op | source)
XLA Modules:
  0.0 67.5 jit_solution(15961298947692293267)
XLA Ops:
  0.0 1.0 %copy.16 = bf16[256,256]{0,1:T(8,128)(2,1)S(1)} copy(bf16[256,256]{1,0:T(8,128)(2,1)} %param.11) | data formatting | bytes 262144 | tf_op args[0]
  1.0 1.0 %copy.18 = bf16[256,256]{0,1:T(8,128)(2,1)S(1)} copy(bf16[256,256]{1,0:T(8,128)(2,1)} %param.12) | data formatting | bytes 262144 | tf_op args[1]
  2.1 1.0 %copy.17 = bf16[256,256]{0,1:T(8,128)(2,1)S(1)} copy(bf16[256,256]{1,0:T(8,128)(2,1)} %param.13) | data formatting | bytes 262144 | tf_op args[2]
  3.1 1.0 %copy.19 = bf16[256,256]{0,1:T(8,128)(2,1)S(1)} copy(bf16[256,256]{1,0:T(8,128)(2,1)} %param.15) | data formatting | bytes 262144 | tf_op args[4]
  4.1 0.1 pad_maximum_fusion.2
  4.2 0.1 constant_dynamic-slice_fusion.8
  4.3 6.0 %collective-permute-start.6 = (bf16[4,1,32,256]{3,2,1,0:T(8,128)(2,1)S(1)}, bf16[4,1,32,256]{3,2,1,0:T(8,128)(2,1)S(1)}, u32[]{:S(2)}, u32[]{:S(2)}) collective-permute-start(bf16[4,1,32,256]{3,2,1,0:T(8,128)(2,1)S(1)} %get-tuple-element.18), channel_id=1, source_target_pairs={{0,14},{2,0},{4,2},{6,4},{8,6},{10,8},{12,10},{14,12},{1,15},{3,1}... | collective-permute-start | bytes 196616 | tf_op jit(solution)/shard_map/ppermute | solution.py:63
  10.3 0.4 collective-permute-start.5
  10.7 3.0 %collective-permute-start.3 = (bf16[4,1,32,256]{3,2,1,0:T(8,128)(2,1)S(1)}, bf16[4,1,32,256]{3,2,1,0:T(8,128)(2,1)S(1)}, u32[]{:S(2)}, u32[]{:S(2)}) collective-permute-start(bf16[4,1,32,256]{3,2,1,0:T(8,128)(2,1)S(1)} %get-tuple-element.21), channel_id=1, source_target_pairs={{0,8},{2,10},{4,12},{6,14},{8,0},{10,2},{12,4},{14,6},{1,9},{3,11}... | collective-permute-start | bytes 196616 | tf_op jit(solution)/shard_map/ppermute | solution.py:63
  13.7 1.5 %collective-permute-start = (bf16[4,1,32,256]{3,2,1,0:T(8,128)(2,1)S(1)}, bf16[4,1,32,256]{3,2,1,0:T(8,128)(2,1)S(1)}, u32[]{:S(2)}, u32[]{:S(2)}) collective-permute-start(bf16[4,1,32,256]{3,2,1,0:T(8,128)(2,1)S(1)} %get-tuple-element.24), channel_id=1, source_target_pairs={{0,2},{2,4},{4,6},{6,8},{8,10},{10,12},{12,14},{14,0},{1,3},{3,5},... | collective-permute-start | bytes 196616 | tf_op jit(solution)/shard_map/ppermute | solution.py:63
  15.3 0.6 dynamic_slice.63
  15.8 0.1 fusion.25
  15.9 0.6 slice_bitcast_fusion.14
  16.6 4.2 %collective-permute-done = bf16[4,1,32,256]{3,2,1,0:T(8,128)(2,1)S(1)} collective-permute-done((bf16[4,1,32,256]{3,2,1,0:T(8,128)(2,1)S(1)}, bf16[4,1,32,256]{3,2,1,0:T(8,128)(2,1)S(1)}, u32[]{:S(2)}, u32[]{:S(2)}) %collective-permute-start) | collective-permute-done | bytes 65568 | tf_op jit(solution)/shard_map/ppermute | solution.py:63
  20.7 6.5 %collective-permute-done.1 = bf16[4,1,32,256]{3,2,1,0:T(8,128)(2,1)S(1)} collective-permute-done((bf16[4,1,32,256]{3,2,1,0:T(8,128)(2,1)S(1)}, bf16[4,1,32,256]{3,2,1,0:T(8,128)(2,1)S(1)}, u32[]{:S(2)}, u32[]{:S(2)}) %collective-permute-start.1) | collective-permute-done | bytes 65568 | tf_op jit(solution)/shard_map/ppermute | solution.py:63
  27.2 6.1 %collective-permute-done.2 = bf16[4,1,32,256]{3,2,1,0:T(8,128)(2,1)S(1)} collective-permute-done((bf16[4,1,32,256]{3,2,1,0:T(8,128)(2,1)S(1)}, bf16[4,1,32,256]{3,2,1,0:T(8,128)(2,1)S(1)}, u32[]{:S(2)}, u32[]{:S(2)}) %collective-permute-start.2) | collective-permute-done | bytes 65568 | tf_op jit(solution)/shard_map/ppermute | solution.py:63
  33.4 0.6 gather_fusion
  34.0 0.3 convert_bitcast_fusion
  34.3 0.1 slice_bitcast_fusion.2
  34.4 0.7 %pad_slice_fusion.4 = f32[8,32,2]{2,0,1:T(8,128)} fusion(f32[7,32,256]{2,0,1:T(8,128)S(1)} %get-tuple-element.9), kind=kLoop, calls=%fused_computation.60 | loop fusion | bytes 231424 | tf_op jit(solution)/shard_map/slice | solution.py:41
  35.1 0.8 %pad_slice_fusion.5 = f32[8,32,1]{2,0,1:T(8,128)} fusion(f32[7,32,256]{2,0,1:T(8,128)S(1)} %get-tuple-element.9), kind=kLoop, calls=%fused_computation.61 | loop fusion | bytes 230400 | tf_op jit(solution)/shard_map/slice | solution.py:41
  35.9 0.1 pad_slice_fusion.1
  36.0 1.0 %pad_slice_fusion = (f32[8,32,2]{2,0,1:T(8,128)}, f32[1,8,32,2]{3,1,2,0:T(8,128)}, f32[1,8,32,2]{3,1,2,0:T(8,128)}, f32[8,32,2]{2,0,1:T(8,128)}) fusion(f32[7,32,256]{2,0,1:T(8,128)S(1)} %get-tuple-element.10, f32[7,32,256]{2,0,1:T(8,128)S(1)} %get-tuple-element.11), kind=kLoop, calls=%fused_computation.56 | loop fusion | bytes 466944 | tf_op jit(solution)/shard_map/slice | solution.py:41
  37.0 0.8 %slice_bitcast_fusion.3 = (f32[8,32,256]{2,0,1:T(8,128)S(1)}, f32[8,32,256]{2,0,1:T(8,128)S(1)}, f32[1,8,32,256]{3,1,2,0:T(8,128)}, f32[8,32,256]{2,0,1:T(8,128)S(1)}) fusion(f32[4,8,32,256]{3,1,2,0:T(8,128)S(1)} %convert_bitcast_fusion), kind=kLoop, calls=%fused_computation.30 | loop fusion | bytes 2097152 | tf_op jit(solution)/shard_map/squeeze | solution.py:86
  37.8 0.1 fusion.33
  37.9 0.8 %fusion.34 = (f32[8,32,255]{2,0,1:T(8,128)S(1)}, f32[1,8,32,255]{3,1,2,0:T(8,128)S(1)}, f32[1,8,32,255]{3,1,2,0:T(8,128)S(1)}, f32[8,32,255]{2,0,1:T(8,128)}) fusion(f32[8,32,256]{2,0,1:T(8,128)S(1)} %get-tuple-element.13, f32[8,32,256]{2,0,1:T(8,128)S(1)} %get-tuple-element.15), kind=kLoop, calls=%fused_computation.119 | loop fusion | bytes 1566720 | tf_op jit(solution)/shard_map/slice | solution.py:41
  38.7 0.1 copy.23
  38.8 0.1 copy.21
  39.0 0.2 copy.22
  39.1 0.0 copy-start.15
  39.1 0.8 %copy.24 = f32[1,8,32,1]{3,1,2,0:T(8,128)} copy(f32[1,8,32,1]{2,1,3,0:T(8,128)S(1)} %bitcast.92) | data formatting | bytes 2048 | tf_op jit(solution)/shard_map/concatenate | solution.py:41
  39.9 1.7 %fusion.16 = f32[1,8,32,256]{3,1,2,0:T(8,128)S(1)} fusion(f32[1,8,32,255]{3,1,2,0:T(8,128)S(1)} %get-tuple-element.57, f32[1,8,32,1]{3,1,2,0:T(8,128)S(1)} %copy.22, f32[1,8,32,254]{3,1,2,0:T(8,128)S(1)} %get-tuple-element.55, f32[1,8,32,2]{3,1,2,0:T(8,128)} %get-tuple-element.59, f32[1,8,32,255]{3,1,2,0:T(8,128)S(1)} %get-tuple-element.31, ...), kind=kLoop, calls=%fused_computation.38 | loop fusion | flops 983040 | bytes 1835776 | tf_op jit(solution)/shard_map/mul | solution.py:87
  41.6 0.0 copy-start.8
  41.6 1.4 %convolution_bitcast_fusion = f32[2,18,32,256]{3,1,2,0:T(8,128)S(1)} fusion(f32[18,8,1,1]{0,1,3,2:T(8,128)S(1)} %copy-done.15, f32[1,8,32,256]{3,1,2,0:T(8,128)S(1)} %copy-done.3, f32[1,8,32,256]{3,1,2,0:T(8,128)S(1)} %fusion.16), kind=kOutput, calls=%fused_computation.3 | convolution fusion | flops 28442624 | bytes 1704512 | tf_op jit(solution)/shard_map/kd,sdcr->skcr/dot_general | solution.py:90
  43.1 0.3 multiply_subtract_fusion
  43.4 0.3 pad_maximum_fusion
  43.7 0.9 %copy-done.1 = f32[512,512,1,1]{1,0,3,2:T(8,128)S(1)} copy-done((f32[512,512,1,1]{1,0,3,2:T(8,128)S(1)}, f32[512,512,1,1]{1,0,3,2:T(8,128)}, u32[]{:S(2)}) %copy-start.1) | copy-done | bytes 1048600
  44.6 2.7 %fusion = f32[2,9,32,512]{3,2,1,0:T(8,128)S(1)} fusion(f32[512,512,1,1]{1,0,3,2:T(8,128)S(1)} %copy-done.1, f32[2,9,32,512]{3,1,2,0:T(8,128)S(1)} %pad_maximum_fusion), kind=kOutput, calls=%fused_computation.4 | convolution fusion | flops 1811939328 | bytes 3407872 | tf_op jit(solution)/shard_map/...j,jk->...k/dot_general | solution.py:53
  47.3 0.1 subtract_bitcast_fusion
  47.4 1.1 %copy-done = f32[512,512,1]{1,0,2:T(8,128)S(1)} copy-done((f32[512,512,1]{1,0,2:T(8,128)S(1)}, f32[512,512,1]{1,0,2:T(8,128)}, u32[]{:S(2)}) %copy-start) | copy-done | bytes 1048600
  48.5 1.1 %fusion.5 = f32[9,32,512]{2,1,0:T(8,128)S(1)} fusion(f32[512,512,1]{1,0,2:T(8,128)S(1)} %copy-done, f32[9,32,256]{2,1,0:T(8,128)S(1)} %get-tuple-element.8, f32[9,32,256]{2,1,0:T(8,128)S(1)} %get-tuple-element.7), kind=kOutput, calls=%fused_computation.13 | convolution fusion | flops 906117120 | bytes 2228224 | tf_op jit(solution)/shard_map/...j,jk->...k/dot_general | solution.py:53
  49.8 0.1 multiply_add_fusion.1
  50.0 0.7 copy-done.2
  50.6 0.0 copy-done.4
  50.6 0.1 copy-done.5
  50.7 0.1 copy-done.6
  50.8 0.0 copy-done.7
  50.9 1.4 %fusion.3 = bf16[8,32,256]{2,0,1:T(8,128)(2,1)S(1)} fusion(f32[8,18,1]{1,0,2:T(8,128)S(1)} %copy-done.16, f32[18,32,256]{2,1,0:T(8,128)S(1)} %pad_maximum_fusion.1, f32[8,32,255]{2,0,1:T(8,128)S(1)} %bitcast.84, f32[8,32,1]{2,0,1:T(8,128)S(1)} %copy-done.5, f32[8,32,254]{2,0,1:T(8,128)S(1)} %bitcast.85, f32[8,32,2]{2,0,1:T(8,128)S(1)} %copy-done.4, ...), kind=kOutput, calls=%fused_computation.8 | convolution fusion | flops 15859712 | bytes 3082048 | tf_op jit(solution)/shard_map/dk,kcr->dcr/dot_general | solution.py:103
  52.3 0.3 constant_dynamic-slice_fusion
  52.6 0.1 collective-permute-start.13
  52.7 1.1 %collective-permute-start.12 = (bf16[1,32,256]{2,0,1:T(2,128)(2,1)S(1)}, bf16[1,32,256]{2,0,1:T(2,128)(2,1)S(1)}, u32[]{:S(2)}, u32[]{:S(2)}) collective-permute-start(bf16[1,32,256]{2,0,1:T(2,128)(2,1)S(1)} %get-tuple-element.39), channel_id=1, source_target_pairs={{0,12},{2,14},{4,0},{6,2},{8,4},{10,6},{12,8},{14,10},{1,13},{3,15... | collective-permute-start | bytes 49160 | tf_op jit(solution)/shard_map/ppermute | solution.py:63
  53.8 3.5 %collective-permute-start.10 = (bf16[1,32,256]{2,0,1:T(2,128)(2,1)S(1)}, bf16[1,32,256]{2,0,1:T(2,128)(2,1)S(1)}, u32[]{:S(2)}, u32[]{:S(2)}) collective-permute-start(bf16[1,32,256]{2,0,1:T(2,128)(2,1)S(1)} %get-tuple-element.41), channel_id=1, source_target_pairs={{0,8},{2,10},{4,12},{6,14},{8,0},{10,2},{12,4},{14,6},{1,9},{3,11}... | collective-permute-start | bytes 49160 | tf_op jit(solution)/shard_map/ppermute | solution.py:63
  57.3 1.0 %collective-permute-start.9 = (bf16[1,32,256]{2,0,1:T(2,128)(2,1)S(1)}, bf16[1,32,256]{2,0,1:T(2,128)(2,1)S(1)}, u32[]{:S(2)}, u32[]{:S(2)}) collective-permute-start(bf16[1,32,256]{2,0,1:T(2,128)(2,1)S(1)} %get-tuple-element.42), channel_id=1, source_target_pairs={{0,6},{2,8},{4,10},{6,12},{8,14},{10,0},{12,2},{14,4},{1,7},{3,9},... | collective-permute-start | bytes 49160 | tf_op jit(solution)/shard_map/ppermute | solution.py:63
  58.3 0.8 %collective-permute-start.8 = (bf16[1,32,256]{2,0,1:T(2,128)(2,1)S(1)}, bf16[1,32,256]{2,0,1:T(2,128)(2,1)S(1)}, u32[]{:S(2)}, u32[]{:S(2)}) collective-permute-start(bf16[1,32,256]{2,0,1:T(2,128)(2,1)S(1)} %get-tuple-element.43), channel_id=1, source_target_pairs={{0,4},{2,6},{4,8},{6,10},{8,12},{10,14},{12,0},{14,2},{1,5},{3,7},... | collective-permute-start | bytes 49160 | tf_op jit(solution)/shard_map/ppermute | solution.py:63
  59.1 1.5 %collective-permute-start.7 = (bf16[1,32,256]{2,0,1:T(2,128)(2,1)S(1)}, bf16[1,32,256]{2,0,1:T(2,128)(2,1)S(1)}, u32[]{:S(2)}, u32[]{:S(2)}) collective-permute-start(bf16[1,32,256]{2,0,1:T(2,128)(2,1)S(1)} %get-tuple-element.44), channel_id=1, source_target_pairs={{0,2},{2,4},{4,6},{6,8},{8,10},{10,12},{12,14},{14,0},{1,3},{3,5},... | collective-permute-start | bytes 49160 | tf_op jit(solution)/shard_map/ppermute | solution.py:63
  60.5 0.1 broadcast_in_dim.25
  60.6 0.1 broadcast_in_dim.26
  60.7 2.3 %collective-permute-done.9 = bf16[1,32,256]{2,0,1:T(2,128)(2,1)S(1)} collective-permute-done((bf16[1,32,256]{2,0,1:T(2,128)(2,1)S(1)}, bf16[1,32,256]{2,0,1:T(2,128)(2,1)S(1)}, u32[]{:S(2)}, u32[]{:S(2)}) %collective-permute-start.9) | collective-permute-done | bytes 16416 | tf_op jit(solution)/shard_map/ppermute | solution.py:63
  63.0 1.0 %collective-permute-done.8 = bf16[1,32,256]{2,0,1:T(2,128)(2,1)S(1)} collective-permute-done((bf16[1,32,256]{2,0,1:T(2,128)(2,1)S(1)}, bf16[1,32,256]{2,0,1:T(2,128)(2,1)S(1)}, u32[]{:S(2)}, u32[]{:S(2)}) %collective-permute-start.8) | collective-permute-done | bytes 16416 | tf_op jit(solution)/shard_map/ppermute | solution.py:63
  64.0 1.7 %collective-permute-done.7 = bf16[1,32,256]{2,0,1:T(2,128)(2,1)S(1)} collective-permute-done((bf16[1,32,256]{2,0,1:T(2,128)(2,1)S(1)}, bf16[1,32,256]{2,0,1:T(2,128)(2,1)S(1)}, u32[]{:S(2)}, u32[]{:S(2)}) %collective-permute-start.7) | collective-permute-done | bytes 16416 | tf_op jit(solution)/shard_map/ppermute | solution.py:63
  65.7 0.4 stack.32
  66.1 0.6 gather_fusion.1
  66.7 0.1 bitcast_select_fusion
  66.8 0.8 %copy.28 = bf16[256,256]{1,0:T(8,128)(2,1)} copy(bf16[256,256]{0,1:T(8,128)(2,1)S(1)} %bitcast.87) | data formatting | bytes 262144 | tf_op jit(solution)/shard_map/transpose | solution.py:110
  (65 shorter events, 0.3 us)
Async XLA Ops:
  0.0 15.3 %copy-start.24 = (f32[256]{0:T(256)S(1)}, f32[256]{0:T(256)}, u32[]{:S(2)}) copy-start(f32[256]{0:T(256)} %param.16) | copy-start | bytes 3076
  0.0 15.8 %copy-start.20 = (bf16[3,3,256]{2,1,0:T(4,128)(2,1)S(1)}, bf16[3,3,256]{2,1,0:T(4,128)(2,1)}, u32[]{:S(2)}) copy-start(bf16[3,3,256]{2,1,0:T(4,128)(2,1)} %param.14) | copy-start | bytes 13828
  4.3 29.1 %collective-permute-start.6 = (bf16[4,1,32,256]{3,2,1,0:T(8,128)(2,1)S(1)}, bf16[4,1,32,256]{3,2,1,0:T(8,128)(2,1)S(1)}, u32[]{:S(2)}, u32[]{:S(2)}) collective-permute-start(bf16[4,1,32,256]{3,2,1,0:T(8,128)(2,1)S(1)} %get-tuple-element.18), channel_id=1, source_target_pairs={{0,14},{2,0},{4,2},{6,4},{8,6},{10,8},{12,10},{14,12},{1,15},{3,1}... | collective-permute-start | bytes 196616 | tf_op jit(solution)/shard_map/ppermute | solution.py:63
  10.3 23.1 %collective-permute-start.5 = (bf16[4,1,32,256]{3,2,1,0:T(8,128)(2,1)S(1)}, bf16[4,1,32,256]{3,2,1,0:T(8,128)(2,1)S(1)}, u32[]{:S(2)}, u32[]{:S(2)}) collective-permute-start(bf16[4,1,32,256]{3,2,1,0:T(8,128)(2,1)S(1)} %get-tuple-element.19), channel_id=1, source_target_pairs={{0,12},{2,14},{4,0},{6,2},{8,4},{10,6},{12,8},{14,10},{1,13},{3,15... | collective-permute-start | bytes 196616 | tf_op jit(solution)/shard_map/ppermute | solution.py:63
  10.7 22.6 %collective-permute-start.4 = (bf16[4,1,32,256]{3,2,1,0:T(8,128)(2,1)S(1)}, bf16[4,1,32,256]{3,2,1,0:T(8,128)(2,1)S(1)}, u32[]{:S(2)}, u32[]{:S(2)}) collective-permute-start(bf16[4,1,32,256]{3,2,1,0:T(8,128)(2,1)S(1)} %get-tuple-element.20), channel_id=1, source_target_pairs={{0,10},{2,12},{4,14},{6,0},{8,2},{10,4},{12,6},{14,8},{1,11},{3,13... | collective-permute-start | bytes 196616 | tf_op jit(solution)/shard_map/ppermute | solution.py:63
  10.7 22.6 %collective-permute-start.3 = (bf16[4,1,32,256]{3,2,1,0:T(8,128)(2,1)S(1)}, bf16[4,1,32,256]{3,2,1,0:T(8,128)(2,1)S(1)}, u32[]{:S(2)}, u32[]{:S(2)}) collective-permute-start(bf16[4,1,32,256]{3,2,1,0:T(8,128)(2,1)S(1)} %get-tuple-element.21), channel_id=1, source_target_pairs={{0,8},{2,10},{4,12},{6,14},{8,0},{10,2},{12,4},{14,6},{1,9},{3,11}... | collective-permute-start | bytes 196616 | tf_op jit(solution)/shard_map/ppermute | solution.py:63
  13.7 7.0 %collective-permute-start = (bf16[4,1,32,256]{3,2,1,0:T(8,128)(2,1)S(1)}, bf16[4,1,32,256]{3,2,1,0:T(8,128)(2,1)S(1)}, u32[]{:S(2)}, u32[]{:S(2)}) collective-permute-start(bf16[4,1,32,256]{3,2,1,0:T(8,128)(2,1)S(1)} %get-tuple-element.24), channel_id=1, source_target_pairs={{0,2},{2,4},{4,6},{6,8},{8,10},{10,12},{12,14},{14,0},{1,3},{3,5},... | collective-permute-start | bytes 196616 | tf_op jit(solution)/shard_map/ppermute | solution.py:63
  16.5 17.8 %copy-start.21 = (pred[8]{0:T(512)(128)(4,1)}, pred[8]{0:T(512)(128)(4,1)S(1)}, u32[]{:S(2)}) copy-start(pred[8]{0:T(512)(128)(4,1)S(1)} %compare_and_fusion) | copy-start | bytes 28
  20.7 6.5 %collective-permute-start.1 = (bf16[4,1,32,256]{3,2,1,0:T(8,128)(2,1)S(1)}, bf16[4,1,32,256]{3,2,1,0:T(8,128)(2,1)S(1)}, u32[]{:S(2)}, u32[]{:S(2)}) collective-permute-start(bf16[4,1,32,256]{3,2,1,0:T(8,128)(2,1)S(1)} %get-tuple-element.23), channel_id=1, source_target_pairs={{0,4},{2,6},{4,8},{6,10},{8,12},{10,14},{12,0},{14,2},{1,5},{3,7},... | collective-permute-start | bytes 196616 | tf_op jit(solution)/shard_map/ppermute | solution.py:63
  27.2 6.1 %collective-permute-start.2 = (bf16[4,1,32,256]{3,2,1,0:T(8,128)(2,1)S(1)}, bf16[4,1,32,256]{3,2,1,0:T(8,128)(2,1)S(1)}, u32[]{:S(2)}, u32[]{:S(2)}) collective-permute-start(bf16[4,1,32,256]{3,2,1,0:T(8,128)(2,1)S(1)} %get-tuple-element.22), channel_id=1, source_target_pairs={{0,6},{2,8},{4,10},{6,12},{8,14},{10,0},{12,2},{14,4},{1,7},{3,9},... | collective-permute-start | bytes 196616 | tf_op jit(solution)/shard_map/ppermute | solution.py:63
  39.1 2.5 %copy-start.15 = (f32[18,8,1,1]{0,1,3,2:T(8,128)S(1)}, f32[18,8,1,1]{0,1,3,2:T(8,128)}, u32[]{:S(2)}) copy-start(f32[18,8,1,1]{0,1,3,2:T(8,128)} %constant.141) | copy-start | bytes 1732
  39.9 1.7 %copy-start.3 = (f32[1,8,32,256]{3,1,2,0:T(8,128)S(1)}, f32[1,8,32,256]{3,1,2,0:T(8,128)}, u32[]{:S(2)}) copy-start(f32[1,8,32,256]{3,1,2,0:T(8,128)} %get-tuple-element.14) | copy-start | bytes 786436
  41.6 1.5 %copy-start.8 = (f32[9,256]{1,0:T(8,128)S(1)}, f32[9,256]{1,0:T(8,128)}, u32[]{:S(2)}) copy-start(f32[9,256]{1,0:T(8,128)} %constant.139) | copy-start | bytes 27652
  41.6 1.5 %copy-start.9 = (f32[9,256]{1,0:T(8,128)S(1)}, f32[9,256]{1,0:T(8,128)}, u32[]{:S(2)}) copy-start(f32[9,256]{1,0:T(8,128)} %constant.137) | copy-start | bytes 27652
  43.4 1.2 %copy-start.1 = (f32[512,512,1,1]{1,0,3,2:T(8,128)S(1)}, f32[512,512,1,1]{1,0,3,2:T(8,128)}, u32[]{:S(2)}) copy-start(f32[512,512,1,1]{1,0,3,2:T(8,128)} %constant.142) | copy-start | bytes 3145732
  47.3 1.2 %copy-start = (f32[512,512,1]{1,0,2:T(8,128)S(1)}, f32[512,512,1]{1,0,2:T(8,128)}, u32[]{:S(2)}) copy-start(f32[512,512,1]{1,0,2:T(8,128)} %constant.143) | copy-start | bytes 3145732
  49.7 1.0 %copy-start.2 = (f32[8,32,255]{2,0,1:T(8,128)S(1)}, f32[8,32,255]{2,0,1:T(8,128)}, u32[]{:S(2)}) copy-start(f32[8,32,255]{2,0,1:T(8,128)} %get-tuple-element.58) | copy-start | bytes 783364
  49.7 1.0 %copy-start.4 = (f32[8,32,2]{2,0,1:T(8,128)S(1)}, f32[8,32,2]{2,0,1:T(8,128)}, u32[]{:S(2)}) copy-start(f32[8,32,2]{2,0,1:T(8,128)} %pad_slice_fusion.4) | copy-start | bytes 6148
  49.7 1.0 %copy-start.5 = (f32[8,32,1]{2,0,1:T(8,128)S(1)}, f32[8,32,1]{2,0,1:T(8,128)}, u32[]{:S(2)}) copy-start(f32[8,32,1]{2,0,1:T(8,128)} %pad_slice_fusion.5) | copy-start | bytes 3076
  49.7 1.1 %copy-start.6 = (f32[8,32,2]{2,0,1:T(8,128)S(1)}, f32[8,32,2]{2,0,1:T(8,128)}, u32[]{:S(2)}) copy-start(f32[8,32,2]{2,0,1:T(8,128)} %get-tuple-element.26) | copy-start | bytes 6148
  49.7 1.1 %copy-start.7 = (f32[8,32,2]{2,0,1:T(8,128)S(1)}, f32[8,32,2]{2,0,1:T(8,128)}, u32[]{:S(2)}) copy-start(f32[8,32,2]{2,0,1:T(8,128)} %get-tuple-element.60) | copy-start | bytes 6148
  49.7 1.1 %copy-start.10 = (f32[32]{0:T(128)S(1)}, f32[32]{0:T(128)}, u32[]{:S(2)}) copy-start(f32[32]{0:T(128)} %get-tuple-element.48) | copy-start | bytes 388
  49.7 1.1 %copy-start.11 = (f32[32]{0:T(128)S(1)}, f32[32]{0:T(128)}, u32[]{:S(2)}) copy-start(f32[32]{0:T(128)} %get-tuple-element.49) | copy-start | bytes 388
  49.7 1.1 %copy-start.12 = (f32[32]{0:T(128)S(1)}, f32[32]{0:T(128)}, u32[]{:S(2)}) copy-start(f32[32]{0:T(128)} %get-tuple-element.50) | copy-start | bytes 388
  49.7 1.1 %copy-start.13 = (f32[32]{0:T(128)S(1)}, f32[32]{0:T(128)}, u32[]{:S(2)}) copy-start(f32[32]{0:T(128)} %get-tuple-element.51) | copy-start | bytes 388
  49.8 1.1 %copy-start.14 = (f32[32]{0:T(128)S(1)}, f32[32]{0:T(128)}, u32[]{:S(2)}) copy-start(f32[32]{0:T(128)} %get-tuple-element.52) | copy-start | bytes 388
  49.8 1.1 %copy-start.16 = (f32[8,18,1]{1,0,2:T(8,128)S(1)}, f32[8,18,1]{1,0,2:T(8,128)}, u32[]{:S(2)}) copy-start(f32[8,18,1]{1,0,2:T(8,128)} %constant.140) | copy-start | bytes 1732
  49.8 1.1 %copy-start.17 = (f32[32]{0:T(128)S(1)}, f32[32]{0:T(128)}, u32[]{:S(2)}) copy-start(f32[32]{0:T(128)} %get-tuple-element.46) | copy-start | bytes 388
  49.8 1.1 %copy-start.18 = (f32[32]{0:T(128)S(1)}, f32[32]{0:T(128)}, u32[]{:S(2)}) copy-start(f32[32]{0:T(128)} %get-tuple-element.53) | copy-start | bytes 388
  49.8 1.1 %copy-start.19 = (f32[32]{0:T(128)S(1)}, f32[32]{0:T(128)}, u32[]{:S(2)}) copy-start(f32[32]{0:T(128)} %get-tuple-element.54) | copy-start | bytes 388
  49.8 1.1 %copy-start.23 = (f32[32]{0:T(128)S(1)}, f32[32]{0:T(128)}, u32[]{:S(2)}) copy-start(f32[32]{0:T(128)} %dynamic_slice.63) | copy-start | bytes 388
  50.9 9.7 %copy-start.22 = (pred[8]{0:T(512)(128)(4,1)S(1)}, pred[8]{0:T(512)(128)(4,1)}, u32[]{:S(2)}) copy-start(pred[8]{0:T(512)(128)(4,1)} %copy-done.21) | copy-start | bytes 28
  52.6 5.7 %collective-permute-start.13 = (bf16[1,32,256]{2,0,1:T(2,128)(2,1)S(1)}, bf16[1,32,256]{2,0,1:T(2,128)(2,1)S(1)}, u32[]{:S(2)}, u32[]{:S(2)}) collective-permute-start(bf16[1,32,256]{2,0,1:T(2,128)(2,1)S(1)} %get-tuple-element.38), channel_id=1, source_target_pairs={{0,14},{2,0},{4,2},{6,4},{8,6},{10,8},{12,10},{14,12},{1,15},{3,1}... | collective-permute-start | bytes 49160 | tf_op jit(solution)/shard_map/ppermute | solution.py:63
  52.7 6.4 %collective-permute-start.12 = (bf16[1,32,256]{2,0,1:T(2,128)(2,1)S(1)}, bf16[1,32,256]{2,0,1:T(2,128)(2,1)S(1)}, u32[]{:S(2)}, u32[]{:S(2)}) collective-permute-start(bf16[1,32,256]{2,0,1:T(2,128)(2,1)S(1)} %get-tuple-element.39), channel_id=1, source_target_pairs={{0,12},{2,14},{4,0},{6,2},{8,4},{10,6},{12,8},{14,10},{1,13},{3,15... | collective-permute-start | bytes 49160 | tf_op jit(solution)/shard_map/ppermute | solution.py:63
  53.8 6.9 %collective-permute-start.11 = (bf16[1,32,256]{2,0,1:T(2,128)(2,1)S(1)}, bf16[1,32,256]{2,0,1:T(2,128)(2,1)S(1)}, u32[]{:S(2)}, u32[]{:S(2)}) collective-permute-start(bf16[1,32,256]{2,0,1:T(2,128)(2,1)S(1)} %get-tuple-element.40), channel_id=1, source_target_pairs={{0,10},{2,12},{4,14},{6,0},{8,2},{10,4},{12,6},{14,8},{1,11},{3,13... | collective-permute-start | bytes 49160 | tf_op jit(solution)/shard_map/ppermute | solution.py:63
  53.8 6.9 %collective-permute-start.10 = (bf16[1,32,256]{2,0,1:T(2,128)(2,1)S(1)}, bf16[1,32,256]{2,0,1:T(2,128)(2,1)S(1)}, u32[]{:S(2)}, u32[]{:S(2)}) collective-permute-start(bf16[1,32,256]{2,0,1:T(2,128)(2,1)S(1)} %get-tuple-element.41), channel_id=1, source_target_pairs={{0,8},{2,10},{4,12},{6,14},{8,0},{10,2},{12,4},{14,6},{1,9},{3,11}... | collective-permute-start | bytes 49160 | tf_op jit(solution)/shard_map/ppermute | solution.py:63
  57.3 5.7 %collective-permute-start.9 = (bf16[1,32,256]{2,0,1:T(2,128)(2,1)S(1)}, bf16[1,32,256]{2,0,1:T(2,128)(2,1)S(1)}, u32[]{:S(2)}, u32[]{:S(2)}) collective-permute-start(bf16[1,32,256]{2,0,1:T(2,128)(2,1)S(1)} %get-tuple-element.42), channel_id=1, source_target_pairs={{0,6},{2,8},{4,10},{6,12},{8,14},{10,0},{12,2},{14,4},{1,7},{3,9},... | collective-permute-start | bytes 49160 | tf_op jit(solution)/shard_map/ppermute | solution.py:63
  58.3 5.7 %collective-permute-start.8 = (bf16[1,32,256]{2,0,1:T(2,128)(2,1)S(1)}, bf16[1,32,256]{2,0,1:T(2,128)(2,1)S(1)}, u32[]{:S(2)}, u32[]{:S(2)}) collective-permute-start(bf16[1,32,256]{2,0,1:T(2,128)(2,1)S(1)} %get-tuple-element.43), channel_id=1, source_target_pairs={{0,4},{2,6},{4,8},{6,10},{8,12},{10,14},{12,0},{14,2},{1,5},{3,7},... | collective-permute-start | bytes 49160 | tf_op jit(solution)/shard_map/ppermute | solution.py:63
  59.1 6.6 %collective-permute-start.7 = (bf16[1,32,256]{2,0,1:T(2,128)(2,1)S(1)}, bf16[1,32,256]{2,0,1:T(2,128)(2,1)S(1)}, u32[]{:S(2)}, u32[]{:S(2)}) collective-permute-start(bf16[1,32,256]{2,0,1:T(2,128)(2,1)S(1)} %get-tuple-element.44), channel_id=1, source_target_pairs={{0,2},{2,4},{4,6},{6,8},{8,10},{10,12},{12,14},{14,0},{1,3},{3,5},... | collective-permute-start | bytes 49160 | tf_op jit(solution)/shard_map/ppermute | solution.py:63

commit v3 on v1

v3 whole, which is shorter than its diff:
```python
import math

import ml_dtypes
import numpy as np

import jax
import jax.numpy as jnp
from jax import lax
from jax.experimental import pallas as pl
from jax.experimental.pallas import tpu as pltpu
from jax.sharding import PartitionSpec as P

full_precision = lax.Precision.HIGHEST


def split_table(table):
    high = table.astype(ml_dtypes.bfloat16)
    low = (table - high.astype(np.float64)).astype(ml_dtypes.bfloat16)
    return jnp.asarray(high), jnp.asarray(low)


def kernel_tables(blocks, rows, piece):
    total = 2 * blocks * rows
    half = blocks + 1
    k2 = np.arange(half)
    d = np.arange(blocks)
    r = np.arange(rows)
    clean = lambda a: np.where(np.abs(a) < 1e-12, 0.0, a)
    block_angle = 2.0 * np.pi * np.outer(k2, d) / (2 * blocks)
    first = clean(np.concatenate([np.cos(block_angle), -np.sin(block_angle)], axis=0))
    twist_angle = -2.0 * np.pi * np.outer(k2, r) / total
    twist = np.stack([np.cos(twist_angle), np.sin(twist_angle)])
    twist = np.repeat(twist, piece, axis=1)
    row_angle = 2.0 * np.pi * np.outer(r, r) / rows
    cosine, sine = np.cos(row_angle), np.sin(row_angle)
    forward = np.block([[cosine, -sine], [sine, cosine]])
    backward = np.block([[cosine, sine], [-sine, cosine]])
    weight = np.full(half, 2.0)
    weight[0] = 1.0
    weight[-1] = 1.0
    last_angle = 2.0 * np.pi * np.outer(d, k2) / (2 * blocks)
    last = clean(np.concatenate([weight * np.cos(last_angle), -weight * np.sin(last_angle)], axis=1))
    last = last / total
    as_f32 = lambda a: jnp.asarray(a.astype(np.float32))
    return (as_f32(first), as_f32(last), as_f32(twist)) + split_table(forward) + split_table(backward)


def dot3(a, high_ref, low_ref):
    a_high = a.astype(jnp.bfloat16)
    a_low = (a - a_high.astype(jnp.float32)).astype(jnp.bfloat16)
    high = high_ref[...]
    out = jnp.dot(a_high, high, preferred_element_type=jnp.float32)
    out = out + jnp.dot(a_low, high, preferred_element_type=jnp.float32)
    return out + jnp.dot(a_high, low_ref[...], preferred_element_type=jnp.float32)


def local_kernel(first, last, sig, kern, gain, twist, fwd_hi, fwd_lo, bwd_hi, bwd_lo, out,
                 ext, g_s, o_s, a_g, a_h):
    blocks, piece, rows = out.shape
    half = blocks + 1
    taps = kern.shape[1]
    tile = min(piece, 8)
    unrolled = blocks <= 16
    f32 = jnp.float32
    lane = lax.broadcasted_iota(jnp.int32, (blocks, piece, rows), 2)
    ext[0] = jnp.zeros((piece, rows), f32)

    def conv(stream, weights):
        x = sig[stream].astype(f32)
        total = kern[weights, 0] * x
        for lag in range(1, taps):
            rolled = pltpu.roll(x, lag, 2)
            ext[pl.ds(1, blocks)] = rolled
            earlier = jnp.where(lane < lag, ext[pl.ds(0, blocks)], rolled)
            total = total + kern[weights, lag] * earlier
        return total

    g_s[...] = conv(0, 0) * conv(1, 2)
    o_s[...] = conv(2, 1)

    def load_block(which, d, at):
        if which == 0:
            return g_s[d, at, :]
        return sig[3, d, at, :].astype(f32)

    for tile_index in range(piece // tile):
        at = pl.ds(tile_index * tile, tile)
        for which, dst in ((0, a_g), (1, a_h)):
            if unrolled:
                xs = [load_block(which, d, at) for d in range(blocks)]
                for k in range(half):
                    for part in range(2):
                        acc = first[part * half + k, 0] * xs[0]
                        for d in range(1, blocks):
                            acc = acc + first[part * half + k, d] * xs[d]
                        dst[pl.ds(k * piece + tile_index * tile, tile), pl.ds(part * rows, rows)] = acc
            else:
                for k in range(half):
                    for part in range(2):
                        dst[pl.ds(k * piece + tile_index * tile, tile), pl.ds(part * rows, rows)] = (
                            jnp.zeros((tile, rows), f32))

                def step(d, carry):
                    xd = load_block(which, d, at)
                    for k in range(half):
                        for part in range(2):
                            where = (pl.ds(k * piece + tile_index * tile, tile), pl.ds(part * rows, rows))
                            dst[where] = dst[where] + first[part * half + k, d] * xd
                    return carry

                lax.fori_loop(0, blocks, step, 0)

    t_re = twist[0]
    t_im = twist[1]
    spectra = []
    for src in (a_g, a_h):
        re = src[:, pl.ds(0, rows)]
        im = src[:, pl.ds(rows, rows)]
        turned = jnp.concatenate([re * t_re - im * t_im, re * t_im + im * t_re], axis=1)
        spectra.append(dot3(turned, fwd_hi, fwd_lo))
    xg, xh = spectra
    gr, gi = xg[:, :rows], xg[:, rows:]
    hr, hi = xh[:, :rows], xh[:, rows:]
    product = jnp.concatenate([gr * hr - gi * hi, gr * hi + gi * hr], axis=1)
    back = dot3(product, bwd_hi, bwd_lo)
    y_re, y_im = back[:, :rows], back[:, rows:]
    a_h[:, pl.ds(0, rows)] = y_re * t_re + y_im * t_im
    a_h[:, pl.ds(rows, rows)] = y_im * t_re - y_re * t_im

    for tile_index in range(piece // tile):
        at = pl.ds(tile_index * tile, tile)
        scale = gain[at]

        def finish(d, us):
            acc = None
            for k in range(half):
                for part in range(2):
                    term = last[d, part * half + k] * us(k, part)
                    acc = term if acc is None else acc + term
            gated = g_s[d, at, :]
            out[d, at, :] = (o_s[d, at, :] * (acc + scale * gated)).astype(out.dtype)

        if unrolled:
            held = {}
            for k in range(half):
                for part in range(2):
                    held[k, part] = a_h[pl.ds(k * piece + tile_index * tile, tile), pl.ds(part * rows, rows)]
            for d in range(blocks):
                finish(d, lambda k, part: held[k, part])
        else:
            def step(d, carry):
                finish(d, lambda k, part: a_h[
                    pl.ds(k * piece + tile_index * tile, tile), pl.ds(part * rows, rows)])
                return carry

            lax.fori_loop(0, blocks, step, 0)


def body(gate_stream, outer_stream, value_stream, short_weight, long_filter, skip_gain):
    rows, chans = gate_stream.shape
    blocks = lax.axis_size("ctx")
    piece = chans // blocks
    half = blocks + 1
    me = lax.axis_index("ctx")
    first, last, twist, fwd_hi, fwd_lo, bwd_hi, bwd_lo = kernel_tables(blocks, rows, piece)

    stacked = jnp.stack([gate_stream, value_stream, outer_stream, long_filter])
    stacked = jnp.swapaxes(stacked, 1, 2).reshape(4, blocks, piece, rows)
    gathered = lax.all_to_all(stacked, "ctx", 1, 1)

    kern = lax.dynamic_slice_in_dim(short_weight, me * piece, piece, axis=2).astype(jnp.float32)
    kern = kern[..., None]
    gain = lax.dynamic_slice_in_dim(skip_gain, me * piece, piece)[:, None]

    smem = pl.BlockSpec(memory_space=pltpu.SMEM)
    vmem = pl.BlockSpec(memory_space=pltpu.VMEM)
    f32 = jnp.float32
    out = pl.pallas_call(
        local_kernel,
        out_shape=jax.ShapeDtypeStruct((blocks, piece, rows), jnp.bfloat16),
        in_specs=[smem, smem] + [vmem] * 8,
        out_specs=vmem,
        scratch_shapes=[
            pltpu.VMEM((blocks + 1, piece, rows), f32),
            pltpu.VMEM((blocks, piece, rows), f32),
            pltpu.VMEM((blocks, piece, rows), f32),
            pltpu.VMEM((half * piece, 2 * rows), f32),
            pltpu.VMEM((half * piece, 2 * rows), f32),
        ],
    )(first, last, gathered, kern, gain, twist, fwd_hi, fwd_lo, bwd_hi, bwd_lo)

    returned = lax.all_to_all(out, "ctx", 0, 0)
    return jnp.swapaxes(returned.reshape(chans, rows), 0, 1)


def solution(mesh):
    placed = (
        P(("groups", "ctx"), "ch"),
        P(("groups", "ctx"), "ch"),
        P(("groups", "ctx"), "ch"),
        P(None, None, "ch"),
        P("ctx", "ch"),
        P("ch"),
    )
    return jax.shard_map(
        body, mesh=mesh, in_specs=placed, out_specs=P(("groups", "ctx"), "ch"), check_vma=False
    )
```

time: 57.6 us -> 44.1 us (0.77)
  local copies, waits for them, and re-layouts: 15.4 us -> 7.59 us
  matrix products: 7.26 us -> 0 us
  Pallas kernels: 0 us -> 5.47 us
  other arithmetic: 2.92 us -> 0.14 us
  waiting for transfers between devices: 13.1 us -> 12.2 us
    dot_general x4 -> x0, matrix products: 7.26 us -> none  [the longest x2 3.77 us: complex_rows(): out = jnp.einsum('...j,jk->...k', both, table, precision=full_precision)]
    pallas_call x0 -> x1, Pallas kernels: none -> 5.47 us  [body(): pl.pallas_call(local_kernel, out_shape=jax.ShapeDtypeStruct((blocks, piec...]
    slice x9 -> x0, local copies, waits for them, and re-layouts: 3.8 us -> none  [the longest x8 3.75 us: shifted(): return jnp.concatenate([earlier[:, :, -lag:], x[:, :, :-lag]], axis=2)]
    unnamed x46 -> x14, local copies, waits for them, and re-layouts: 7 us -> 3.62 us
    mul x1 -> x0, other arithmetic: 1.64 us -> none  [body(): gated_value = gate_conv * value_conv]
    broadcast_in_dim x0 -> x3, local copies, waits for them, and re-layouts: none -> 1.54 us  [the longest x1 0.78 us: body(): kern = kern[..., None]]
    all_to_all x1, waiting for transfers between devices: 13.1 us -> 12.2 us  [body(): gathered = lax.all_to_all(stacked, 'ctx', 1, 1)]
    concatenate x2 -> x0, local copies, waits for them, and re-layouts: 0.94 us -> none  [shifted(): return jnp.concatenate([earlier[:, :, -lag:], x[:, :, :-lag]], axis=2)]
  transfers between devices with their start and end apart: 1 -> 1, of which waited for: 1 -> 1; matrix products, arithmetic and copies ran while one was open for 2% -> 4% of each run, Pallas kernels for 0% -> 0%
where the time goes in v3:
time: 44.1 us; the launch traced here: 43.7 us
  waiting for transfers between devices  12.2 us (28%)
  blocking collectives  11 us (25%)
  local copies, waits for them, and re-layouts  7.59 us (17%)
  starting transfers between devices  7.25 us (16%)
  Pallas kernels  5.47 us (12%)
    all_to_all x1, waiting for transfers between devices, body(): gathered = lax.all_to_all(stacked, 'ctx', 1, 1)  12.2 us
    all_to_all x1, blocking collectives, body(): returned = lax.all_to_all(out, 'ctx', 0, 0)  11 us
    all_to_all x1, starting transfers between devices, body(): gathered = lax.all_to_all(stacked, 'ctx', 1, 1)  7.25 us
    pallas_call x1, Pallas kernels, body(): pl.pallas_call(local_kernel, out_shape=jax.ShapeDtypeStruct((blocks, piec...  5.47 us
    unnamed x14, local copies, waits for them, and re-layouts  3.62 us
  transfers between devices with their start and end apart: 1, of which 1 were waited for; matrix products, arithmetic and copies ran while one was open for 4% of the time, Pallas kernels for 0%

profile of v3, /device:TPU:0, one launch (start us, length us, event | category | flops | bytes accessed | tf_op | source)
XLA Modules:
  0.0 43.7 jit_solution(4684956191123662174)
XLA Ops:
  0.0 0.0 copy-start
  0.0 0.0 copy-start.1
  0.0 1.0 %copy.28 = bf16[256,256]{0,1:T(8,128)(2,1)S(1)} copy(bf16[256,256]{1,0:T(8,128)(2,1)} %param.17) | data formatting | bytes 262144 | tf_op args[4]
  1.0 0.0 copy-done.1
  1.1 0.0 copy-start.2
  1.1 0.1 copy.27
  1.2 0.8 %copy-done.2 = bf16[256,256]{1,0:T(8,128)(2,1)S(1)} copy-done((bf16[256,256]{1,0:T(8,128)(2,1)S(1)}, bf16[256,256]{1,0:T(8,128)(2,1)}, u32[]{:S(2)}) %copy-start.2) | copy-done | bytes 131096
  2.0 0.0 copy-start.3
  2.0 0.1 copy.26
  2.1 0.8 %copy-done.3 = bf16[256,256]{1,0:T(8,128)(2,1)S(1)} copy-done((bf16[256,256]{1,0:T(8,128)(2,1)S(1)}, bf16[256,256]{1,0:T(8,128)(2,1)}, u32[]{:S(2)}) %copy-start.3) | copy-done | bytes 131096
  2.9 0.1 copy.25
  3.0 0.1 pad_maximum_fusion
  3.1 0.8 %copy.29 = bf16[4,8,32,256]{3,2,0,1:T(8,128)(2,1)} copy(bf16[4,8,32,256]{3,2,1,0:T(8,128)(2,1)S(1)} %bitcast.14) | data formatting | bytes 1048576 | tf_op jit(solution)/shard_map/reshape | solution.py:168
  3.9 7.3 %all-to-all-start = ((bf16[4,8,32,256]{3,2,0,1:T(8,128)(2,1)}), bf16[4,8,32,256]{3,2,0,1:T(8,128)(2,1)S(1)}, u32[]{:S(2)}, u32[]{:S(2)}) async-start(bf16[4,8,32,256]{3,2,0,1:T(8,128)(2,1)} %copy.29), calls=%async_computation | async-start | bytes 1048576 | tf_op jit(solution)/shard_map/all_to_all | solution.py:169
  11.1 0.0 copy-start.4
  11.2 0.7 %copy-done.4 = bf16[3,3,256]{2,1,0:T(4,128)(2,1)S(1)} copy-done((bf16[3,3,256]{2,1,0:T(4,128)(2,1)S(1)}, bf16[3,3,256]{2,1,0:T(4,128)(2,1)}, u32[]{:S(2)}) %copy-start.4) | copy-done | bytes 4632
  11.8 0.1 bitcast_convert_fusion
  11.9 0.8 %copy.31.kern = f32[3,3,32,1]{3,2,1,0:T(8,128)} copy(f32[3,3,32,1]{2,1,0,3:T(4,128)S(1)} %bitcast_convert_fusion) | data formatting | bytes 2304 | tf_op jit(solution)/shard_map/broadcast_in_dim | solution.py:172
  12.7 0.0 copy-done
  12.7 0.1 dynamic-slice_bitcast_fusion
  12.8 0.7 %copy.32.gain = f32[32,1]{1,0:T(8,128)} copy(f32[32,1]{0,1:T(1,128)S(1)} %dynamic-slice_bitcast_fusion) | data formatting | bytes 256 | tf_op jit(solution)/shard_map/broadcast_in_dim | solution.py:173
  13.5 12.2 %all-to-all-done = bf16[4,8,32,256]{3,2,0,1:T(8,128)(2,1)S(1)} async-done(((bf16[4,8,32,256]{3,2,0,1:T(8,128)(2,1)}), bf16[4,8,32,256]{3,2,0,1:T(8,128)(2,1)S(1)}, u32[]{:S(2)}, u32[]{:S(2)}) %all-to-all-start) | async-done | bytes 524320 | tf_op jit(solution)/shard_map/all_to_all | solution.py:169
  25.6 0.8 %copy.30.sig = bf16[4,8,32,256]{3,2,1,0:T(8,128)(2,1)} copy(bf16[4,8,32,256]{3,2,0,1:T(8,128)(2,1)S(1)} %all-to-all-done) | data formatting | bytes 1048576 | tf_op jit(solution)/shard_map/all_to_all | solution.py:169
  26.5 5.5 %shard_map.127 = bf16[8,32,256]{2,1,0:T(8,128)(2,1)} custom-call(f32[18,8]{1,0:T(8,128)} %constant.26.clone.first, f32[8,18]{1,0:T(8,128)} %constant.27.clone.last, bf16[4,8,32,256]{3,2,1,0:T(8,128)(2,1)} %copy.30.sig, f32[3,3,32,1]{3,2,1,0:T(8,128)} %copy.31.kern, f32[32,1]{1,0:T(8,128)} %copy.32.gain, f32[2,288,256]{2,1,0:T(8,128)} %constant.28.clone.twist, ...), custom_call_target="tpu_custom_call" | custom-call | tf_op jit(solution)/shard_map/pallas_call | solution.py:178
  31.9 11.0 %all_to_all.10 = bf16[8,32,256]{2,1,0:T(8,128)(2,1)S(1)} all-to-all(bf16[8,32,256]{2,1,0:T(8,128)(2,1)} %shard_map.127), channel_id=1, replica_groups=mesh['groups'=2,'ctx'=8,'ch'=2] {'ctx'}, dimensions={0} | all-to-all | bytes 262144 | tf_op jit(solution)/shard_map/all_to_all | solution.py:192
  42.9 0.8 %copy.33 = bf16[256,256]{0,1:T(8,128)(2,1)} copy(bf16[256,256]{1,0:T(8,128)(2,1)S(1)} %bitcast.15) | data formatting | bytes 262144 | tf_op jit(solution)/shard_map/reshape | solution.py:193
Async XLA Ops:
  0.0 12.7 %copy-start = (f32[256]{0:T(256)S(1)}, f32[256]{0:T(256)}, u32[]{:S(2)}) copy-start(f32[256]{0:T(256)} %param.18) | copy-start | bytes 3076
  0.0 1.0 %copy-start.1 = (bf16[256,256]{1,0:T(8,128)(2,1)S(1)}, bf16[256,256]{1,0:T(8,128)(2,1)}, u32[]{:S(2)}) copy-start(bf16[256,256]{1,0:T(8,128)(2,1)} %param.14) | copy-start | bytes 393220
  1.1 0.9 %copy-start.2 = (bf16[256,256]{1,0:T(8,128)(2,1)S(1)}, bf16[256,256]{1,0:T(8,128)(2,1)}, u32[]{:S(2)}) copy-start(bf16[256,256]{1,0:T(8,128)(2,1)} %param.15) | copy-start | bytes 393220
  2.0 0.9 %copy-start.3 = (bf16[256,256]{1,0:T(8,128)(2,1)S(1)}, bf16[256,256]{1,0:T(8,128)(2,1)}, u32[]{:S(2)}) copy-start(bf16[256,256]{1,0:T(8,128)(2,1)} %param.13) | copy-start | bytes 393220
  3.9 21.7 %all-to-all-start = ((bf16[4,8,32,256]{3,2,0,1:T(8,128)(2,1)}), bf16[4,8,32,256]{3,2,0,1:T(8,128)(2,1)S(1)}, u32[]{:S(2)}, u32[]{:S(2)}) async-start(bf16[4,8,32,256]{3,2,0,1:T(8,128)(2,1)} %copy.29), calls=%async_computation | async-start | bytes 1048576 | tf_op jit(solution)/shard_map/all_to_all | solution.py:169
  11.1 0.7 %copy-start.4 = (bf16[3,3,256]{2,1,0:T(4,128)(2,1)S(1)}, bf16[3,3,256]{2,1,0:T(4,128)(2,1)}, u32[]{:S(2)}) copy-start(bf16[3,3,256]{2,1,0:T(4,128)(2,1)} %param.16) | copy-start | bytes 13828

commit v4 on v3

--- a/solution.py
+++ b/solution.py
@@ -66,7 +66,7 @@
     ext[0] = jnp.zeros((piece, rows), f32)
 
     def conv(stream, weights):
-        x = sig[stream].astype(f32)
+        x = sig[:, stream].astype(f32)
         total = kern[weights, 0] * x
         for lag in range(1, taps):
             rolled = pltpu.roll(x, lag, 2)
@@ -81,7 +81,7 @@
     def load_block(which, d, at):
         if which == 0:
             return g_s[d, at, :]
-        return sig[3, d, at, :].astype(f32)
+        return sig[d, 3, at, :].astype(f32)
 
     for tile_index in range(piece // tile):
         at = pl.ds(tile_index * tile, tile)
@@ -156,6 +156,22 @@
             lax.fori_loop(0, blocks, step, 0)
 
 
+def to_blocks_kernel(*refs):
+    *streams, out, held = refs
+    blocks, _, piece, rows = out.shape
+    for index, stream in enumerate(streams):
+        held[...] = jnp.transpose(stream[...].astype(jnp.float32))
+        for j in range(blocks):
+            out[j, index] = held[pl.ds(j * piece, piece), :].astype(out.dtype)
+
+
+def from_blocks_kernel(pieces, out, held):
+    blocks, piece, rows = pieces.shape
+    for j in range(blocks):
+        held[pl.ds(j * piece, piece), :] = pieces[j].astype(jnp.float32)
+    out[...] = jnp.transpose(held[...]).astype(out.dtype)
+
+
 def body(gate_stream, outer_stream, value_stream, short_weight, long_filter, skip_gain):
     rows, chans = gate_stream.shape
     blocks = lax.axis_size("ctx")
@@ -164,16 +180,21 @@
     me = lax.axis_index("ctx")
     first, last, twist, fwd_hi, fwd_lo, bwd_hi, bwd_lo = kernel_tables(blocks, rows, piece)
 
-    stacked = jnp.stack([gate_stream, value_stream, outer_stream, long_filter])
-    stacked = jnp.swapaxes(stacked, 1, 2).reshape(4, blocks, piece, rows)
-    gathered = lax.all_to_all(stacked, "ctx", 1, 1)
+    vmem = pl.BlockSpec(memory_space=pltpu.VMEM)
+    stacked = pl.pallas_call(
+        to_blocks_kernel,
+        out_shape=jax.ShapeDtypeStruct((blocks, 4, piece, rows), jnp.bfloat16),
+        in_specs=[vmem] * 4,
+        out_specs=vmem,
+        scratch_shapes=[pltpu.VMEM((chans, rows), jnp.float32)],
+    )(gate_stream, value_stream, outer_stream, long_filter)
+    gathered = lax.all_to_all(stacked, "ctx", 0, 0)
 
     kern = lax.dynamic_slice_in_dim(short_weight, me * piece, piece, axis=2).astype(jnp.float32)
     kern = kern[..., None]
     gain = lax.dynamic_slice_in_dim(skip_gain, me * piece, piece)[:, None]
 
     smem = pl.BlockSpec(memory_space=pltpu.SMEM)
-    vmem = pl.BlockSpec(memory_space=pltpu.VMEM)
     f32 = jnp.float32
     out = pl.pallas_call(
         local_kernel,
@@ -190,7 +211,13 @@
     )(first, last, gathered, kern, gain, twist, fwd_hi, fwd_lo, bwd_hi, bwd_lo)
 
     returned = lax.all_to_all(out, "ctx", 0, 0)
-    return jnp.swapaxes(returned.reshape(chans, rows), 0, 1)
+    return pl.pallas_call(
+        from_blocks_kernel,
+        out_shape=jax.ShapeDtypeStruct((rows, chans), jnp.bfloat16),
+        in_specs=[vmem],
+        out_specs=vmem,
+        scratch_shapes=[pltpu.VMEM((chans, rows), jnp.float32)],
+    )(returned)
 
 
 def solution(mesh):

time: 44.1 us -> 43.5 us (0.986)
  local copies, waits for them, and re-layouts: 7.59 us -> 3.04 us
  Pallas kernels: 5.47 us -> 9.24 us
    pallas_call x0 -> x2, Pallas kernels: none -> 3.77 us  [the longest x1 2.11 us: body(): pl.pallas_call(to_blocks_kernel, out_shape=jax.ShapeDtypeStruct((blocks,...]
    unnamed x14 -> x6, local copies, waits for them, and re-layouts: 3.62 us -> 1.49 us
    reshape x2 -> x0, local copies, waits for them, and re-layouts: 1.59 us -> none  [the longest x1 0.84 us: body(): stacked = jnp.swapaxes(stacked, 1, 2).reshape(4, blocks, piece, rows)]
    all_to_all x1 -> x0, local copies, waits for them, and re-layouts: 0.83 us -> none  [body(): gathered = lax.all_to_all(stacked, 'ctx', 1, 1)]
where the time goes in v4:
time: 43.5 us; the launch traced here: 43.1 us
  waiting for transfers between devices  12.2 us (28%)
  blocking collectives  11.3 us (26%)
  Pallas kernels  9.24 us (21%)
  starting transfers between devices  7.25 us (17%)
  local copies, waits for them, and re-layouts  3.04 us (7%)
    all_to_all x1, waiting for transfers between devices, body(): gathered = lax.all_to_all(stacked, 'ctx', 0, 0)  12.2 us
    all_to_all x1, blocking collectives, body(): returned = lax.all_to_all(out, 'ctx', 0, 0)  11.3 us
    all_to_all x1, starting transfers between devices, body(): gathered = lax.all_to_all(stacked, 'ctx', 0, 0)  7.25 us
    pallas_call x1, Pallas kernels, body(): pl.pallas_call(local_kernel, out_shape=jax.ShapeDtypeStruct((blocks, piec...  5.47 us
    pallas_call x1, Pallas kernels, body(): pl.pallas_call(to_blocks_kernel, out_shape=jax.ShapeDtypeStruct((blocks,...  2.11 us
    pallas_call x1, Pallas kernels, body(): pl.pallas_call(from_blocks_kernel, out_shape=jax.ShapeDtypeStruct((rows,...  1.66 us
    unnamed x6, local copies, waits for them, and re-layouts  1.49 us
  transfers between devices with their start and end apart: 1, of which 1 were waited for; matrix products, arithmetic and copies ran while one was open for 4% of the time, Pallas kernels for 0%

profile of v4, /device:TPU:0, one launch (start us, length us, event | category | flops | bytes accessed | tf_op | source)
XLA Modules:
  0.0 43.1 jit_solution(5988192965336853549)
XLA Ops:
  0.0 0.0 copy-start
  0.0 2.1 %shard_map.127 = bf16[8,4,32,256]{3,2,1,0:T(8,128)(2,1)} custom-call(bf16[256,256]{1,0:T(8,128)(2,1)} %refs_0_.1, bf16[256,256]{1,0:T(8,128)(2,1)} %refs_1_.1, bf16[256,256]{1,0:T(8,128)(2,1)} %refs_2_.1, bf16[256,256]{1,0:T(8,128)(2,1)} %refs_3_.1), custom_call_target="tpu_custom_call" | custom-call | tf_op jit(solution)/shard_map/pallas_call | solution.py:184
  2.1 7.3 %all-to-all-start = ((bf16[8,4,32,256]{3,2,1,0:T(8,128)(2,1)}), bf16[8,4,32,256]{3,2,1,0:T(8,128)(2,1)S(1)}, u32[]{:S(2)}, u32[]{:S(2)}) async-start(bf16[8,4,32,256]{3,2,1,0:T(8,128)(2,1)} %shard_map.127), calls=%async_computation | async-start | bytes 1048576 | tf_op jit(solution)/shard_map/all_to_all | solution.py:191
  9.4 0.0 copy-start.2
  9.4 0.7 %copy-done.2 = bf16[3,3,256]{2,1,0:T(4,128)(2,1)S(1)} copy-done((bf16[3,3,256]{2,1,0:T(4,128)(2,1)S(1)}, bf16[3,3,256]{2,1,0:T(4,128)(2,1)}, u32[]{:S(2)}) %copy-start.2) | copy-done | bytes 4632
  10.1 0.1 bitcast_convert_fusion
  10.1 0.8 %copy.15.kern = f32[3,3,32,1]{3,2,1,0:T(8,128)} copy(f32[3,3,32,1]{2,1,0,3:T(4,128)S(1)} %bitcast_convert_fusion) | data formatting | bytes 2304 | tf_op jit(solution)/shard_map/broadcast_in_dim | solution.py:194
  10.9 0.0 copy-done
  10.9 0.1 dynamic-slice_bitcast_fusion
  11.0 0.7 %copy.16.gain = f32[32,1]{1,0:T(8,128)} copy(f32[32,1]{0,1:T(1,128)S(1)} %dynamic-slice_bitcast_fusion) | data formatting | bytes 256 | tf_op jit(solution)/shard_map/broadcast_in_dim | solution.py:195
  11.7 12.2 %all-to-all-done.sig = bf16[8,4,32,256]{3,2,1,0:T(8,128)(2,1)S(1)} async-done(((bf16[8,4,32,256]{3,2,1,0:T(8,128)(2,1)}), bf16[8,4,32,256]{3,2,1,0:T(8,128)(2,1)S(1)}, u32[]{:S(2)}, u32[]{:S(2)}) %all-to-all-start) | async-done | bytes 524320 | tf_op jit(solution)/shard_map/all_to_all | solution.py:191
  23.9 0.0 copy-start.1
  23.9 0.8 %copy-done.1 = bf16[8,4,32,256]{3,2,1,0:T(8,128)(2,1)} copy-done((bf16[8,4,32,256]{3,2,1,0:T(8,128)(2,1)}, bf16[8,4,32,256]{3,2,1,0:T(8,128)(2,1)S(1)}, u32[]{:S(2)}) %copy-start.1) | copy-done | bytes 524312
  24.7 5.5 %shard_map.128 = bf16[8,32,256]{2,1,0:T(8,128)(2,1)} custom-call(f32[18,8]{1,0:T(8,128)} %constant.26.clone.first, f32[8,18]{1,0:T(8,128)} %constant.27.clone.last, bf16[8,4,32,256]{3,2,1,0:T(8,128)(2,1)} %copy-done.1, f32[3,3,32,1]{3,2,1,0:T(8,128)} %copy.15.kern, f32[32,1]{1,0:T(8,128)} %copy.16.gain, f32[2,288,256]{2,1,0:T(8,128)} %constant.28.clone.twist, ...), custom_call_target="tpu_custom_call" | custom-call | tf_op jit(solution)/shard_map/pallas_call | solution.py:199
  30.1 11.3 %all_to_all.10.pieces = bf16[8,32,256]{2,1,0:T(8,128)(2,1)} all-to-all(bf16[8,32,256]{2,1,0:T(8,128)(2,1)} %shard_map.128), channel_id=1, replica_groups=mesh['groups'=2,'ctx'=8,'ch'=2] {'ctx'}, dimensions={0} | all-to-all | bytes 262144 | tf_op jit(solution)/shard_map/all_to_all | solution.py:213
  41.4 1.7 %shard_map.129 = bf16[256,256]{1,0:T(8,128)(2,1)} custom-call(bf16[8,32,256]{2,1,0:T(8,128)(2,1)} %all_to_all.10.pieces), custom_call_target="tpu_custom_call" | custom-call | tf_op jit(solution)/shard_map/pallas_call | solution.py:214
Async XLA Ops:
  0.0 10.9 %copy-start = (f32[256]{0:T(256)S(1)}, f32[256]{0:T(256)}, u32[]{:S(2)}) copy-start(f32[256]{0:T(256)} %param.18) | copy-start | bytes 3076
  2.1 21.7 %all-to-all-start = ((bf16[8,4,32,256]{3,2,1,0:T(8,128)(2,1)}), bf16[8,4,32,256]{3,2,1,0:T(8,128)(2,1)S(1)}, u32[]{:S(2)}, u32[]{:S(2)}) async-start(bf16[8,4,32,256]{3,2,1,0:T(8,128)(2,1)} %shard_map.127), calls=%async_computation | async-start | bytes 1048576 | tf_op jit(solution)/shard_map/all_to_all | solution.py:191
  9.4 0.7 %copy-start.2 = (bf16[3,3,256]{2,1,0:T(4,128)(2,1)S(1)}, bf16[3,3,256]{2,1,0:T(4,128)(2,1)}, u32[]{:S(2)}) copy-start(bf16[3,3,256]{2,1,0:T(4,128)(2,1)} %param.16) | copy-start | bytes 13828
  23.9 0.8 %copy-start.1 = (bf16[8,4,32,256]{3,2,1,0:T(8,128)(2,1)}, bf16[8,4,32,256]{3,2,1,0:T(8,128)(2,1)S(1)}, u32[]{:S(2)}) copy-start(bf16[8,4,32,256]{3,2,1,0:T(8,128)(2,1)S(1)} %all-to-all-done.sig) | copy-start | bytes 1572868

commit v5 on v4

--- a/solution.py
+++ b/solution.py
@@ -19,7 +19,7 @@
     return jnp.asarray(high), jnp.asarray(low)
 
 
-def kernel_tables(blocks, rows, piece):
+def kernel_tables(blocks, rows):
     total = 2 * blocks * rows
     half = blocks + 1
     k2 = np.arange(half)
@@ -29,33 +29,73 @@
     block_angle = 2.0 * np.pi * np.outer(k2, d) / (2 * blocks)
     first = clean(np.concatenate([np.cos(block_angle), -np.sin(block_angle)], axis=0))
     twist_angle = -2.0 * np.pi * np.outer(k2, r) / total
-    twist = np.stack([np.cos(twist_angle), np.sin(twist_angle)])
-    twist = np.repeat(twist, piece, axis=1)
+    twist = np.stack([np.cos(twist_angle), np.sin(twist_angle)])[:, :, None, :]
+    untwist = np.stack([np.cos(twist_angle), -np.sin(twist_angle)])[:, :, None, :] / total
     row_angle = 2.0 * np.pi * np.outer(r, r) / rows
-    cosine, sine = np.cos(row_angle), np.sin(row_angle)
-    forward = np.block([[cosine, -sine], [sine, cosine]])
-    backward = np.block([[cosine, sine], [-sine, cosine]])
     weight = np.full(half, 2.0)
     weight[0] = 1.0
     weight[-1] = 1.0
     last_angle = 2.0 * np.pi * np.outer(d, k2) / (2 * blocks)
     last = clean(np.concatenate([weight * np.cos(last_angle), -weight * np.sin(last_angle)], axis=1))
-    last = last / total
     as_f32 = lambda a: jnp.asarray(a.astype(np.float32))
-    return (as_f32(first), as_f32(last), as_f32(twist)) + split_table(forward) + split_table(backward)
-
-
-def dot3(a, high_ref, low_ref):
-    a_high = a.astype(jnp.bfloat16)
-    a_low = (a - a_high.astype(jnp.float32)).astype(jnp.bfloat16)
-    high = high_ref[...]
-    out = jnp.dot(a_high, high, preferred_element_type=jnp.float32)
-    out = out + jnp.dot(a_low, high, preferred_element_type=jnp.float32)
-    return out + jnp.dot(a_high, low_ref[...], preferred_element_type=jnp.float32)
-
-
-def local_kernel(first, last, sig, kern, gain, twist, fwd_hi, fwd_lo, bwd_hi, bwd_lo, out,
-                 ext, g_s, o_s, a_g, a_h):
+    return ((as_f32(first), as_f32(last), as_f32(twist), as_f32(untwist))
+            + split_table(np.cos(row_angle)) + split_table(np.sin(row_angle)))
+
+
+def scaled(terms):
+    total = None
+    for array, constant in terms:
+        if array is None or constant == 0.0:
+            continue
+        if constant == 1.0:
+            term = array
+        elif constant == -1.0:
+            term = -array
+        else:
+            term = constant * array
+        total = term if total is None else total + term
+    return total
+
+
+def unit(angle):
+    c, s = math.cos(angle), math.sin(angle)
+    snap = lambda v: 0.0 if abs(v) < 1e-12 else (1.0 if abs(v - 1) < 1e-12 else (-1.0 if abs(v + 1) < 1e-12 else v))
+    return snap(c), snap(s)
+
+
+def fft(values, sign):
+    count = len(values)
+    if count == 1:
+        return values
+    even = fft(values[0::2], sign)
+    odd = fft(values[1::2], sign)
+    out = [None] * count
+    for k in range(count // 2):
+        c, s = unit(sign * 2.0 * math.pi * k / count)
+        o_re, o_im = odd[k]
+        t_re = scaled([(o_re, c), (o_im, -s)])
+        t_im = scaled([(o_re, s), (o_im, c)])
+        e_re, e_im = even[k]
+        out[k] = (scaled([(e_re, 1.0), (t_re, 1.0)]), scaled([(e_im, 1.0), (t_im, 1.0)]))
+        out[k + count // 2] = (scaled([(e_re, 1.0), (t_re, -1.0)]), scaled([(e_im, 1.0), (t_im, -1.0)]))
+    return out
+
+
+def halves(a):
+    high = a.astype(jnp.bfloat16)
+    return high, (a - high.astype(jnp.float32)).astype(jnp.bfloat16)
+
+
+def times(parts, high_ref, low_ref):
+    high, low = parts
+    table = high_ref[...]
+    out = jnp.dot(high, table, preferred_element_type=jnp.float32)
+    out = out + jnp.dot(low, table, preferred_element_type=jnp.float32)
+    return out + jnp.dot(high, low_ref[...], preferred_element_type=jnp.float32)
+
+
+def local_kernel(first, last, sig, kern, gain, twist, untwist, c_hi, c_lo, s_hi, s_lo, out,
+                 ext, g_s, o_s, a_all, a_h):
     blocks, piece, rows = out.shape
     half = blocks + 1
     taps = kern.shape[1]
@@ -85,47 +125,61 @@
 
     for tile_index in range(piece // tile):
         at = pl.ds(tile_index * tile, tile)
-        for which, dst in ((0, a_g), (1, a_h)):
+        for which in range(2):
+            base = which * half * piece
             if unrolled:
-                xs = [load_block(which, d, at) for d in range(blocks)]
+                xs = [(load_block(which, d, at), None) for d in range(blocks)]
+                spectrum = fft(xs + [(None, None)] * blocks, -1.0)
                 for k in range(half):
                     for part in range(2):
-                        acc = first[part * half + k, 0] * xs[0]
-                        for d in range(1, blocks):
-                            acc = acc + first[part * half + k, d] * xs[d]
-                        dst[pl.ds(k * piece + tile_index * tile, tile), pl.ds(part * rows, rows)] = acc
+                        value = spectrum[k][part]
+                        if value is None:
+                            value = jnp.zeros((tile, rows), f32)
+                        a_all[pl.ds(base + k * piece + tile_index * tile, tile), pl.ds(part * rows, rows)] = value
             else:
                 for k in range(half):
                     for part in range(2):
-                        dst[pl.ds(k * piece + tile_index * tile, tile), pl.ds(part * rows, rows)] = (
+                        a_all[pl.ds(base + k * piece + tile_index * tile, tile), pl.ds(part * rows, rows)] = (
                             jnp.zeros((tile, rows), f32))
 
                 def step(d, carry):
                     xd = load_block(which, d, at)
                     for k in range(half):
                         for part in range(2):
-                            where = (pl.ds(k * piece + tile_index * tile, tile), pl.ds(part * rows, rows))
-                            dst[where] = dst[where] + first[part * half + k, d] * xd
+                            where = (pl.ds(base + k * piece + tile_index * tile, tile), pl.ds(part * rows, rows))
+                            a_all[where] = a_all[where] + first[part * half + k, d] * xd
                     return carry
 
                 lax.fori_loop(0, blocks, step, 0)
 
-    t_re = twist[0]
-    t_im = twist[1]
-    spectra = []
-    for src in (a_g, a_h):
-        re = src[:, pl.ds(0, rows)]
-        im = src[:, pl.ds(rows, rows)]
-        turned = jnp.concatenate([re * t_re - im * t_im, re * t_im + im * t_re], axis=1)
-        spectra.append(dot3(turned, fwd_hi, fwd_lo))
-    xg, xh = spectra
-    gr, gi = xg[:, :rows], xg[:, rows:]
-    hr, hi = xh[:, :rows], xh[:, rows:]
-    product = jnp.concatenate([gr * hr - gi * hi, gr * hi + gi * hr], axis=1)
-    back = dot3(product, bwd_hi, bwd_lo)
-    y_re, y_im = back[:, :rows], back[:, rows:]
-    a_h[:, pl.ds(0, rows)] = y_re * t_re + y_im * t_im
-    a_h[:, pl.ds(rows, rows)] = y_im * t_re - y_re * t_im
+    for which in range(2):
+        for k in range(half):
+            at_rows = pl.ds(which * half * piece + k * piece, piece)
+            re = a_all[at_rows, pl.ds(0, rows)]
+            im = a_all[at_rows, pl.ds(rows, rows)]
+            t_re = twist[0, k]
+            t_im = twist[1, k]
+            a_all[at_rows, pl.ds(0, rows)] = re * t_re - im * t_im
+            a_all[at_rows, pl.ds(rows, rows)] = re * t_im + im * t_re
+    re = halves(a_all[:, pl.ds(0, rows)])
+    im = halves(a_all[:, pl.ds(rows, rows)])
+    x_re = times(re, c_hi, c_lo) + times(im, s_hi, s_lo)
+    x_im = times(im, c_hi, c_lo) - times(re, s_hi, s_lo)
+    count = half * piece
+    gr, gi = x_re[:count], x_im[:count]
+    hr, hi = x_re[count:], x_im[count:]
+    q_re = halves(gr * hr - gi * hi)
+    q_im = halves(gr * hi + gi * hr)
+    y_re = times(q_re, c_hi, c_lo) - times(q_im, s_hi, s_lo)
+    y_im = times(q_re, s_hi, s_lo) + times(q_im, c_hi, c_lo)
+    for k in range(half):
+        at_rows = pl.ds(k * piece, piece)
+        u_re = untwist[0, k]
+        u_im = untwist[1, k]
+        yr = y_re[k * piece:(k + 1) * piece]
+        yi = y_im[k * piece:(k + 1) * piece]
+        a_h[at_rows, pl.ds(0, rows)] = yr * u_re - yi * u_im
+        a_h[at_rows, pl.ds(rows, rows)] = yr * u_im + yi * u_re
 
     for tile_index in range(piece // tile):
         at = pl.ds(tile_index * tile, tile)
@@ -141,12 +195,16 @@
             out[d, at, :] = (o_s[d, at, :] * (acc + scale * gated)).astype(out.dtype)
 
         if unrolled:
-            held = {}
-            for k in range(half):
-                for part in range(2):
-                    held[k, part] = a_h[pl.ds(k * piece + tile_index * tile, tile), pl.ds(part * rows, rows)]
+            held = [
+                tuple(a_h[pl.ds(k * piece + tile_index * tile, tile), pl.ds(part * rows, rows)]
+                      for part in range(2))
+                for k in range(half)
+            ]
+            full = held + [(re, -im) for re, im in reversed(held[1:blocks])]
+            signal = fft(full, 1.0)
             for d in range(blocks):
-                finish(d, lambda k, part: held[k, part])
+                gated = g_s[d, at, :]
+                out[d, at, :] = (o_s[d, at, :] * (signal[d][0] + scale * gated)).astype(out.dtype)
         else:
             def step(d, carry):
                 finish(d, lambda k, part: a_h[
@@ -178,7 +236,7 @@
     piece = chans // blocks
     half = blocks + 1
     me = lax.axis_index("ctx")
-    first, last, twist, fwd_hi, fwd_lo, bwd_hi, bwd_lo = kernel_tables(blocks, rows, piece)
+    first, last, twist, untwist, c_hi, c_lo, s_hi, s_lo = kernel_tables(blocks, rows)
 
     vmem = pl.BlockSpec(memory_space=pltpu.VMEM)
     stacked = pl.pallas_call(
@@ -199,16 +257,16 @@
     out = pl.pallas_call(
         local_kernel,
         out_shape=jax.ShapeDtypeStruct((blocks, piece, rows), jnp.bfloat16),
-        in_specs=[smem, smem] + [vmem] * 8,
+        in_specs=[smem, smem] + [vmem] * 9,
         out_specs=vmem,
         scratch_shapes=[
             pltpu.VMEM((blocks + 1, piece, rows), f32),
             pltpu.VMEM((blocks, piece, rows), f32),
             pltpu.VMEM((blocks, piece, rows), f32),
-            pltpu.VMEM((half * piece, 2 * rows), f32),
+            pltpu.VMEM((2 * half * piece, 2 * rows), f32),
             pltpu.VMEM((half * piece, 2 * rows), f32),
         ],
-    )(first, last, gathered, kern, gain, twist, fwd_hi, fwd_lo, bwd_hi, bwd_lo)
+    )(first, last, gathered, kern, gain, twist, untwist, c_hi, c_lo, s_hi, s_lo)
 
     returned = lax.all_to_all(out, "ctx", 0, 0)
     return pl.pallas_call(

time: 43.5 us -> 42.9 us (0.986)
  Pallas kernels: 9.24 us -> 8.7 us
    pallas_call x1, Pallas kernels: 5.47 us -> 4.92 us  [body(): pl.pallas_call(local_kernel, out_shape=jax.ShapeDtypeStruct((blocks, piec...]
where the time goes in v5:
time: 42.9 us; the launch traced here: 42.6 us
  waiting for transfers between devices  12.2 us (28%)
  blocking collectives  11.3 us (26%)
  Pallas kernels  8.7 us (20%)
  starting transfers between devices  7.25 us (17%)
  local copies, waits for them, and re-layouts  3.04 us (7%)
    all_to_all x1, waiting for transfers between devices, body(): gathered = lax.all_to_all(stacked, 'ctx', 0, 0)  12.2 us
    all_to_all x1, blocking collectives, body(): returned = lax.all_to_all(out, 'ctx', 0, 0)  11.3 us
    all_to_all x1, starting transfers between devices, body(): gathered = lax.all_to_all(stacked, 'ctx', 0, 0)  7.25 us
    pallas_call x1, Pallas kernels, body(): pl.pallas_call(local_kernel, out_shape=jax.ShapeDtypeStruct((blocks, piec...  4.92 us
    pallas_call x1, Pallas kernels, body(): pl.pallas_call(to_blocks_kernel, out_shape=jax.ShapeDtypeStruct((blocks,...  2.11 us
    pallas_call x1, Pallas kernels, body(): pl.pallas_call(from_blocks_kernel, out_shape=jax.ShapeDtypeStruct((rows,...  1.66 us
    unnamed x6, local copies, waits for them, and re-layouts  1.49 us
  transfers between devices with their start and end apart: 1, of which 1 were waited for; matrix products, arithmetic and copies ran while one was open for 4% of the time, Pallas kernels for 0%

profile of v5, /device:TPU:0, one launch (start us, length us, event | category | flops | bytes accessed | tf_op | source)
XLA Modules:
  0.0 42.6 jit_solution(11519985934026551939)
XLA Ops:
  0.0 0.0 copy-start
  0.0 2.1 %shard_map.136 = bf16[8,4,32,256]{3,2,1,0:T(8,128)(2,1)} custom-call(bf16[256,256]{1,0:T(8,128)(2,1)} %refs_0_.1, bf16[256,256]{1,0:T(8,128)(2,1)} %refs_1_.1, bf16[256,256]{1,0:T(8,128)(2,1)} %refs_2_.1, bf16[256,256]{1,0:T(8,128)(2,1)} %refs_3_.1), custom_call_target="tpu_custom_call" | custom-call | tf_op jit(solution)/shard_map/pallas_call | solution.py:242
  2.1 7.3 %all-to-all-start = ((bf16[8,4,32,256]{3,2,1,0:T(8,128)(2,1)}), bf16[8,4,32,256]{3,2,1,0:T(8,128)(2,1)S(1)}, u32[]{:S(2)}, u32[]{:S(2)}) async-start(bf16[8,4,32,256]{3,2,1,0:T(8,128)(2,1)} %shard_map.136), calls=%async_computation | async-start | bytes 1048576 | tf_op jit(solution)/shard_map/all_to_all | solution.py:249
  9.4 0.0 copy-start.2
  9.4 0.7 %copy-done.2 = bf16[3,3,256]{2,1,0:T(4,128)(2,1)S(1)} copy-done((bf16[3,3,256]{2,1,0:T(4,128)(2,1)S(1)}, bf16[3,3,256]{2,1,0:T(4,128)(2,1)}, u32[]{:S(2)}) %copy-start.2) | copy-done | bytes 4632
  10.1 0.1 bitcast_convert_fusion
  10.1 0.8 %copy.16.kern = f32[3,3,32,1]{3,2,1,0:T(8,128)} copy(f32[3,3,32,1]{2,1,0,3:T(4,128)S(1)} %bitcast_convert_fusion) | data formatting | bytes 2304 | tf_op jit(solution)/shard_map/broadcast_in_dim | solution.py:252
  10.9 0.0 copy-done
  10.9 0.1 dynamic-slice_bitcast_fusion
  11.0 0.7 %copy.17.gain = f32[32,1]{1,0:T(8,128)} copy(f32[32,1]{0,1:T(1,128)S(1)} %dynamic-slice_bitcast_fusion) | data formatting | bytes 256 | tf_op jit(solution)/shard_map/broadcast_in_dim | solution.py:253
  11.7 12.2 %all-to-all-done.sig = bf16[8,4,32,256]{3,2,1,0:T(8,128)(2,1)S(1)} async-done(((bf16[8,4,32,256]{3,2,1,0:T(8,128)(2,1)}), bf16[8,4,32,256]{3,2,1,0:T(8,128)(2,1)S(1)}, u32[]{:S(2)}, u32[]{:S(2)}) %all-to-all-start) | async-done | bytes 524320 | tf_op jit(solution)/shard_map/all_to_all | solution.py:249
  23.9 0.0 copy-start.1
  23.9 0.8 %copy-done.1 = bf16[8,4,32,256]{3,2,1,0:T(8,128)(2,1)} copy-done((bf16[8,4,32,256]{3,2,1,0:T(8,128)(2,1)}, bf16[8,4,32,256]{3,2,1,0:T(8,128)(2,1)S(1)}, u32[]{:S(2)}) %copy-start.1) | copy-done | bytes 524312
  24.7 4.9 %shard_map.137 = bf16[8,32,256]{2,1,0:T(8,128)(2,1)} custom-call(f32[18,8]{1,0:T(8,128)} %constant.28.clone.first, f32[8,18]{1,0:T(8,128)} %constant.29.clone.last, bf16[8,4,32,256]{3,2,1,0:T(8,128)(2,1)} %copy-done.1, f32[3,3,32,1]{3,2,1,0:T(8,128)} %copy.16.kern, f32[32,1]{1,0:T(8,128)} %copy.17.gain, f32[2,9,1,256]{3,2,1,0:T(1,128)} %constant.30.clone.twist, ...), custom_call_target="tpu_custom_call" | custom-call | tf_op jit(solution)/shard_map/pallas_call | solution.py:257
  29.6 11.3 %all_to_all.10.pieces = bf16[8,32,256]{2,1,0:T(8,128)(2,1)} all-to-all(bf16[8,32,256]{2,1,0:T(8,128)(2,1)} %shard_map.137), channel_id=1, replica_groups=mesh['groups'=2,'ctx'=8,'ch'=2] {'ctx'}, dimensions={0} | all-to-all | bytes 262144 | tf_op jit(solution)/shard_map/all_to_all | solution.py:271
  40.9 1.7 %shard_map.138 = bf16[256,256]{1,0:T(8,128)(2,1)} custom-call(bf16[8,32,256]{2,1,0:T(8,128)(2,1)} %all_to_all.10.pieces), custom_call_target="tpu_custom_call" | custom-call | tf_op jit(solution)/shard_map/pallas_call | solution.py:272
Async XLA Ops:
  0.0 10.9 %copy-start = (f32[256]{0:T(256)S(1)}, f32[256]{0:T(256)}, u32[]{:S(2)}) copy-start(f32[256]{0:T(256)} %param.19) | copy-start | bytes 3076
  2.1 21.7 %all-to-all-start = ((bf16[8,4,32,256]{3,2,1,0:T(8,128)(2,1)}), bf16[8,4,32,256]{3,2,1,0:T(8,128)(2,1)S(1)}, u32[]{:S(2)}, u32[]{:S(2)}) async-start(bf16[8,4,32,256]{3,2,1,0:T(8,128)(2,1)} %shard_map.136), calls=%async_computation | async-start | bytes 1048576 | tf_op jit(solution)/shard_map/all_to_all | solution.py:249
  9.4 0.7 %copy-start.2 = (bf16[3,3,256]{2,1,0:T(4,128)(2,1)S(1)}, bf16[3,3,256]{2,1,0:T(4,128)(2,1)}, u32[]{:S(2)}) copy-start(bf16[3,3,256]{2,1,0:T(4,128)(2,1)} %param.17) | copy-start | bytes 13828
  23.9 0.8 %copy-start.1 = (bf16[8,4,32,256]{3,2,1,0:T(8,128)(2,1)}, bf16[8,4,32,256]{3,2,1,0:T(8,128)(2,1)S(1)}, u32[]{:S(2)}) copy-start(bf16[8,4,32,256]{3,2,1,0:T(8,128)(2,1)S(1)} %all-to-all-done.sig) | copy-start | bytes 1572868

commit v6 on v5

--- a/solution.py
+++ b/solution.py
@@ -94,8 +94,17 @@
     return out + jnp.dot(high, low_ref[...], preferred_element_type=jnp.float32)
 
 
-def local_kernel(first, last, sig, kern, gain, twist, untwist, c_hi, c_lo, s_hi, s_lo, out,
-                 ext, g_s, o_s, a_all, a_h):
+def local_kernel(first, last, sig_any, kern, gain, *refs):
+    sources = refs[:6]
+    out = refs[6]
+    sig, held_tables, sems, ext, g_s, o_s, a_all, a_h = refs[7], refs[8:14], refs[14], *refs[15:]
+    arrival = pltpu.make_async_copy(sig_any, sig, sems.at[6])
+    arrival.start()
+    loads = [pltpu.make_async_copy(src, dst, sems.at[i]) for i, (src, dst) in enumerate(zip(sources, held_tables))]
+    for load in loads:
+        load.start()
+    twist, untwist, c_hi, c_lo, s_hi, s_lo = held_tables
+    arrival.wait()
     blocks, piece, rows = out.shape
     half = blocks + 1
     taps = kern.shape[1]
@@ -152,6 +161,8 @@
 
                 lax.fori_loop(0, blocks, step, 0)
 
+    for load in loads:
+        load.wait()
     for which in range(2):
         for k in range(half):
             at_rows = pl.ds(which * half * piece + k * piece, piece)
@@ -223,13 +234,6 @@
             out[j, index] = held[pl.ds(j * piece, piece), :].astype(out.dtype)
 
 
-def from_blocks_kernel(pieces, out, held):
-    blocks, piece, rows = pieces.shape
-    for j in range(blocks):
-        held[pl.ds(j * piece, piece), :] = pieces[j].astype(jnp.float32)
-    out[...] = jnp.transpose(held[...]).astype(out.dtype)
-
-
 def body(gate_stream, outer_stream, value_stream, short_weight, long_filter, skip_gain):
     rows, chans = gate_stream.shape
     blocks = lax.axis_size("ctx")
@@ -253,29 +257,28 @@
     gain = lax.dynamic_slice_in_dim(skip_gain, me * piece, piece)[:, None]
 
     smem = pl.BlockSpec(memory_space=pltpu.SMEM)
+    anywhere = pl.BlockSpec(memory_space=pl.ANY)
+    tables = (twist, untwist, c_hi, c_lo, s_hi, s_lo)
     f32 = jnp.float32
     out = pl.pallas_call(
         local_kernel,
         out_shape=jax.ShapeDtypeStruct((blocks, piece, rows), jnp.bfloat16),
-        in_specs=[smem, smem] + [vmem] * 9,
+        in_specs=[smem, smem, anywhere, vmem, vmem] + [anywhere] * 6,
         out_specs=vmem,
         scratch_shapes=[
+            pltpu.VMEM(gathered.shape, gathered.dtype),
+            *[pltpu.VMEM(t.shape, t.dtype) for t in tables],
+            pltpu.SemaphoreType.DMA((7,)),
             pltpu.VMEM((blocks + 1, piece, rows), f32),
             pltpu.VMEM((blocks, piece, rows), f32),
             pltpu.VMEM((blocks, piece, rows), f32),
             pltpu.VMEM((2 * half * piece, 2 * rows), f32),
             pltpu.VMEM((half * piece, 2 * rows), f32),
         ],
-    )(first, last, gathered, kern, gain, twist, untwist, c_hi, c_lo, s_hi, s_lo)
+    )(first, last, gathered, kern, gain, *tables)
 
     returned = lax.all_to_all(out, "ctx", 0, 0)
-    return pl.pallas_call(
-        from_blocks_kernel,
-        out_shape=jax.ShapeDtypeStruct((rows, chans), jnp.bfloat16),
-        in_specs=[vmem],
-        out_specs=vmem,
-        scratch_shapes=[pltpu.VMEM((chans, rows), jnp.float32)],
-    )(returned)
+    return jnp.swapaxes(returned.reshape(chans, rows), 0, 1)
 
 
 def solution(mesh):

time: 42.9 us -> 42.6 us (level)
  Pallas kernels: 8.7 us -> 7.83 us
  local copies, waits for them, and re-layouts: 3.04 us -> 3.8 us
    pallas_call x1 -> x0, Pallas kernels: 1.66 us -> none  [body(): pl.pallas_call(from_blocks_kernel, out_shape=jax.ShapeDtypeStruct((rows,...]
    pallas_call x1, Pallas kernels: 4.92 us -> 5.72 us  [body(): pl.pallas_call(local_kernel, out_shape=jax.ShapeDtypeStruct((blocks, piec...]
    reshape x0 -> x1, local copies, waits for them, and re-layouts: none -> 0.76 us  [body(): return jnp.swapaxes(returned.reshape(chans, rows), 0, 1)]
where the time goes in v6:
time: 42.6 us; the launch traced here: 42.1 us
  waiting for transfers between devices  12.2 us (29%)
  blocking collectives  11 us (26%)
  Pallas kernels  7.83 us (18%)
  starting transfers between devices  7.25 us (17%)
  local copies, waits for them, and re-layouts  3.8 us (9%)
    all_to_all x1, waiting for transfers between devices, body(): gathered = lax.all_to_all(stacked, 'ctx', 0, 0)  12.2 us
    all_to_all x1, blocking collectives, body(): returned = lax.all_to_all(out, 'ctx', 0, 0)  11 us
    all_to_all x1, starting transfers between devices, body(): gathered = lax.all_to_all(stacked, 'ctx', 0, 0)  7.25 us
    pallas_call x1, Pallas kernels, body(): pl.pallas_call(local_kernel, out_shape=jax.ShapeDtypeStruct((blocks, piec...  5.72 us
    pallas_call x1, Pallas kernels, body(): pl.pallas_call(to_blocks_kernel, out_shape=jax.ShapeDtypeStruct((blocks,...  2.11 us
    unnamed x6, local copies, waits for them, and re-layouts  1.49 us
  transfers between devices with their start and end apart: 1, of which 1 were waited for; matrix products, arithmetic and copies ran while one was open for 4% of the time, Pallas kernels for 0%

profile of v6, /device:TPU:0, one launch (start us, length us, event | category | flops | bytes accessed | tf_op | source)
XLA Modules:
  0.0 42.1 jit_solution(17721999153466529646)
XLA Ops:
  0.0 0.0 copy-start
  0.0 2.1 %shard_map.136 = bf16[8,4,32,256]{3,2,1,0:T(8,128)(2,1)} custom-call(bf16[256,256]{1,0:T(8,128)(2,1)} %refs_0_.2, bf16[256,256]{1,0:T(8,128)(2,1)} %refs_1_.2, bf16[256,256]{1,0:T(8,128)(2,1)} %refs_2_.2, bf16[256,256]{1,0:T(8,128)(2,1)} %refs_3_.2), custom_call_target="tpu_custom_call" | custom-call | tf_op jit(solution)/shard_map/pallas_call | solution.py:246
  2.1 7.3 %all-to-all-start = ((bf16[8,4,32,256]{3,2,1,0:T(8,128)(2,1)}), bf16[8,4,32,256]{3,2,1,0:T(8,128)(2,1)S(1)}, u32[]{:S(2)}, u32[]{:S(2)}) async-start(bf16[8,4,32,256]{3,2,1,0:T(8,128)(2,1)} %shard_map.136), calls=%async_computation | async-start | bytes 1048576 | tf_op jit(solution)/shard_map/all_to_all | solution.py:253
  9.4 0.0 copy-start.2
  9.4 0.7 %copy-done.2 = bf16[3,3,256]{2,1,0:T(4,128)(2,1)S(1)} copy-done((bf16[3,3,256]{2,1,0:T(4,128)(2,1)S(1)}, bf16[3,3,256]{2,1,0:T(4,128)(2,1)}, u32[]{:S(2)}) %copy-start.2) | copy-done | bytes 4632
  10.1 0.1 bitcast_convert_fusion
  10.1 0.8 %copy.17.kern = f32[3,3,32,1]{3,2,1,0:T(8,128)} copy(f32[3,3,32,1]{2,1,0,3:T(4,128)S(1)} %bitcast_convert_fusion) | data formatting | bytes 2304 | tf_op jit(solution)/shard_map/broadcast_in_dim | solution.py:256
  10.9 0.0 copy-done
  10.9 0.1 dynamic-slice_bitcast_fusion
  11.0 0.7 %copy.18.gain = f32[32,1]{1,0:T(8,128)} copy(f32[32,1]{0,1:T(1,128)S(1)} %dynamic-slice_bitcast_fusion) | data formatting | bytes 256 | tf_op jit(solution)/shard_map/broadcast_in_dim | solution.py:257
  11.7 12.2 %all-to-all-done.sig_any = bf16[8,4,32,256]{3,2,1,0:T(8,128)(2,1)S(1)} async-done(((bf16[8,4,32,256]{3,2,1,0:T(8,128)(2,1)}), bf16[8,4,32,256]{3,2,1,0:T(8,128)(2,1)S(1)}, u32[]{:S(2)}, u32[]{:S(2)}) %all-to-all-start) | async-done | bytes 524320 | tf_op jit(solution)/shard_map/all_to_all | solution.py:253
  23.9 0.0 copy-start.1
  23.9 0.8 %copy-done.1 = bf16[8,4,32,256]{3,2,1,0:T(8,128)(2,1)} copy-done((bf16[8,4,32,256]{3,2,1,0:T(8,128)(2,1)}, bf16[8,4,32,256]{3,2,1,0:T(8,128)(2,1)S(1)}, u32[]{:S(2)}) %copy-start.1) | copy-done | bytes 524312
  24.7 5.7 %shard_map.137 = bf16[8,32,256]{2,1,0:T(8,128)(2,1)} custom-call(f32[18,8]{1,0:T(8,128)} %constant.28.clone.first, f32[8,18]{1,0:T(8,128)} %constant.29.clone.last, bf16[8,4,32,256]{3,2,1,0:T(8,128)(2,1)} %copy-done.1, f32[3,3,32,1]{3,2,1,0:T(8,128)} %copy.17.kern, f32[32,1]{1,0:T(8,128)} %copy.18.gain, f32[2,9,1,256]{3,2,1,0:T(1,128)} %constant.30.clone.refs_0_, ...), custom_call_target="tpu_custom_call" | custom-call | tf_op jit(solution)/shard_map/pallas_call | solution.py:263
  30.4 11.0 %all_to_all.10 = bf16[8,32,256]{2,1,0:T(8,128)(2,1)S(1)} all-to-all(bf16[8,32,256]{2,1,0:T(8,128)(2,1)} %shard_map.137), channel_id=1, replica_groups=mesh['groups'=2,'ctx'=8,'ch'=2] {'ctx'}, dimensions={0} | all-to-all | bytes 262144 | tf_op jit(solution)/shard_map/all_to_all | solution.py:280
  41.4 0.8 %copy.19 = bf16[256,256]{0,1:T(8,128)(2,1)} copy(bf16[256,256]{1,0:T(8,128)(2,1)S(1)} %bitcast.7) | data formatting | bytes 262144 | tf_op jit(solution)/shard_map/reshape | solution.py:281
Async XLA Ops:
  0.0 10.9 %copy-start = (f32[256]{0:T(256)S(1)}, f32[256]{0:T(256)}, u32[]{:S(2)}) copy-start(f32[256]{0:T(256)} %param.19) | copy-start | bytes 3076
  2.1 21.7 %all-to-all-start = ((bf16[8,4,32,256]{3,2,1,0:T(8,128)(2,1)}), bf16[8,4,32,256]{3,2,1,0:T(8,128)(2,1)S(1)}, u32[]{:S(2)}, u32[]{:S(2)}) async-start(bf16[8,4,32,256]{3,2,1,0:T(8,128)(2,1)} %shard_map.136), calls=%async_computation | async-start | bytes 1048576 | tf_op jit(solution)/shard_map/all_to_all | solution.py:253
  9.4 0.7 %copy-start.2 = (bf16[3,3,256]{2,1,0:T(4,128)(2,1)S(1)}, bf16[3,3,256]{2,1,0:T(4,128)(2,1)}, u32[]{:S(2)}) copy-start(bf16[3,3,256]{2,1,0:T(4,128)(2,1)} %param.17) | copy-start | bytes 13828
  23.9 0.8 %copy-start.1 = (bf16[8,4,32,256]{3,2,1,0:T(8,128)(2,1)}, bf16[8,4,32,256]{3,2,1,0:T(8,128)(2,1)S(1)}, u32[]{:S(2)}) copy-start(bf16[8,4,32,256]{3,2,1,0:T(8,128)(2,1)S(1)} %all-to-all-done.sig_any) | copy-start | bytes 1572868

commit v7 on v5

--- a/solution.py
+++ b/solution.py
@@ -217,17 +217,14 @@
 def to_blocks_kernel(*refs):
     *streams, out, held = refs
     blocks, _, piece, rows = out.shape
+    chans = held.shape[0]
+    eye = (lax.broadcasted_iota(jnp.int32, (chans, chans), 0)
+           == lax.broadcasted_iota(jnp.int32, (chans, chans), 1)).astype(jnp.bfloat16)
     for index, stream in enumerate(streams):
-        held[...] = jnp.transpose(stream[...].astype(jnp.float32))
+        held[...] = lax.dot_general(eye, stream[...], (((1,), (1,)), ((), ())),
+                                    preferred_element_type=jnp.float32)
         for j in range(blocks):
             out[j, index] = held[pl.ds(j * piece, piece), :].astype(out.dtype)
-
-
-def from_blocks_kernel(pieces, out, held):
-    blocks, piece, rows = pieces.shape
-    for j in range(blocks):
-        held[pl.ds(j * piece, piece), :] = pieces[j].astype(jnp.float32)
-    out[...] = jnp.transpose(held[...]).astype(out.dtype)
 
 
 def body(gate_stream, outer_stream, value_stream, short_weight, long_filter, skip_gain):
@@ -269,13 +266,7 @@
     )(first, last, gathered, kern, gain, twist, untwist, c_hi, c_lo, s_hi, s_lo)
 
     returned = lax.all_to_all(out, "ctx", 0, 0)
-    return pl.pallas_call(
-        from_blocks_kernel,
-        out_shape=jax.ShapeDtypeStruct((rows, chans), jnp.bfloat16),
-        in_specs=[vmem],
-        out_specs=vmem,
-        scratch_shapes=[pltpu.VMEM((chans, rows), jnp.float32)],
-    )(returned)
+    return jnp.swapaxes(returned.reshape(chans, rows), 0, 1)
 
 
 def solution(mesh):

time: 42.9 us -> 41.8 us (0.974)
  Pallas kernels: 8.7 us -> 7.16 us
  local copies, waits for them, and re-layouts: 3.04 us -> 3.8 us
    pallas_call x1 -> x0, Pallas kernels: 1.66 us -> none  [body(): pl.pallas_call(from_blocks_kernel, out_shape=jax.ShapeDtypeStruct((rows,...]
    reshape x0 -> x1, local copies, waits for them, and re-layouts: none -> 0.76 us  [body(): return jnp.swapaxes(returned.reshape(chans, rows), 0, 1)]
where the time goes in v7:
time: 41.8 us; the launch traced here: 41.4 us
  waiting for transfers between devices  12.2 us (29%)
  blocking collectives  11 us (26%)
  starting transfers between devices  7.25 us (17%)
  Pallas kernels  7.16 us (17%)
  local copies, waits for them, and re-layouts  3.8 us (9%)
    all_to_all x1, waiting for transfers between devices, body(): gathered = lax.all_to_all(stacked, 'ctx', 0, 0)  12.2 us
    all_to_all x1, blocking collectives, body(): returned = lax.all_to_all(out, 'ctx', 0, 0)  11 us
    all_to_all x1, starting transfers between devices, body(): gathered = lax.all_to_all(stacked, 'ctx', 0, 0)  7.25 us
    pallas_call x1, Pallas kernels, body(): pl.pallas_call(local_kernel, out_shape=jax.ShapeDtypeStruct((blocks, piec...  4.92 us
    pallas_call x1, Pallas kernels, body(): pl.pallas_call(to_blocks_kernel, out_shape=jax.ShapeDtypeStruct((blocks,...  2.24 us
    unnamed x6, local copies, waits for them, and re-layouts  1.49 us
  transfers between devices with their start and end apart: 1, of which 1 were waited for; matrix products, arithmetic and copies ran while one was open for 4% of the time, Pallas kernels for 0%

profile of v7, /device:TPU:0, one launch (start us, length us, event | category | flops | bytes accessed | tf_op | source)
XLA Modules:
  0.0 41.4 jit_solution(10214845630933159087)
XLA Ops:
  0.0 0.0 copy-start
  0.0 2.2 %shard_map.136 = bf16[8,4,32,256]{3,2,1,0:T(8,128)(2,1)} custom-call(bf16[256,256]{1,0:T(8,128)(2,1)} %refs_0_.1, bf16[256,256]{1,0:T(8,128)(2,1)} %refs_1_.1, bf16[256,256]{1,0:T(8,128)(2,1)} %refs_2_.1, bf16[256,256]{1,0:T(8,128)(2,1)} %refs_3_.1), custom_call_target="tpu_custom_call" | custom-call | tf_op jit(solution)/shard_map/pallas_call | solution.py:239
  2.2 7.3 %all-to-all-start = ((bf16[8,4,32,256]{3,2,1,0:T(8,128)(2,1)}), bf16[8,4,32,256]{3,2,1,0:T(8,128)(2,1)S(1)}, u32[]{:S(2)}, u32[]{:S(2)}) async-start(bf16[8,4,32,256]{3,2,1,0:T(8,128)(2,1)} %shard_map.136), calls=%async_computation | async-start | bytes 1048576 | tf_op jit(solution)/shard_map/all_to_all | solution.py:246
  9.5 0.0 copy-start.2
  9.5 0.7 %copy-done.2 = bf16[3,3,256]{2,1,0:T(4,128)(2,1)S(1)} copy-done((bf16[3,3,256]{2,1,0:T(4,128)(2,1)S(1)}, bf16[3,3,256]{2,1,0:T(4,128)(2,1)}, u32[]{:S(2)}) %copy-start.2) | copy-done | bytes 4632
  10.2 0.1 bitcast_convert_fusion
  10.3 0.8 %copy.17.kern = f32[3,3,32,1]{3,2,1,0:T(8,128)} copy(f32[3,3,32,1]{2,1,0,3:T(4,128)S(1)} %bitcast_convert_fusion) | data formatting | bytes 2304 | tf_op jit(solution)/shard_map/broadcast_in_dim | solution.py:249
  11.1 0.0 copy-done
  11.1 0.1 dynamic-slice_bitcast_fusion
  11.1 0.7 %copy.18.gain = f32[32,1]{1,0:T(8,128)} copy(f32[32,1]{0,1:T(1,128)S(1)} %dynamic-slice_bitcast_fusion) | data formatting | bytes 256 | tf_op jit(solution)/shard_map/broadcast_in_dim | solution.py:250
  11.8 12.2 %all-to-all-done.sig = bf16[8,4,32,256]{3,2,1,0:T(8,128)(2,1)S(1)} async-done(((bf16[8,4,32,256]{3,2,1,0:T(8,128)(2,1)}), bf16[8,4,32,256]{3,2,1,0:T(8,128)(2,1)S(1)}, u32[]{:S(2)}, u32[]{:S(2)}) %all-to-all-start) | async-done | bytes 524320 | tf_op jit(solution)/shard_map/all_to_all | solution.py:246
  24.0 0.0 copy-start.1
  24.0 0.8 %copy-done.1 = bf16[8,4,32,256]{3,2,1,0:T(8,128)(2,1)} copy-done((bf16[8,4,32,256]{3,2,1,0:T(8,128)(2,1)}, bf16[8,4,32,256]{3,2,1,0:T(8,128)(2,1)S(1)}, u32[]{:S(2)}) %copy-start.1) | copy-done | bytes 524312
  24.8 4.9 %shard_map.137 = bf16[8,32,256]{2,1,0:T(8,128)(2,1)} custom-call(f32[18,8]{1,0:T(8,128)} %constant.28.clone.first, f32[8,18]{1,0:T(8,128)} %constant.29.clone.last, bf16[8,4,32,256]{3,2,1,0:T(8,128)(2,1)} %copy-done.1, f32[3,3,32,1]{3,2,1,0:T(8,128)} %copy.17.kern, f32[32,1]{1,0:T(8,128)} %copy.18.gain, f32[2,9,1,256]{3,2,1,0:T(1,128)} %constant.30.clone.twist, ...), custom_call_target="tpu_custom_call" | custom-call | tf_op jit(solution)/shard_map/pallas_call | solution.py:254
  29.7 11.0 %all_to_all.10 = bf16[8,32,256]{2,1,0:T(8,128)(2,1)S(1)} all-to-all(bf16[8,32,256]{2,1,0:T(8,128)(2,1)} %shard_map.137), channel_id=1, replica_groups=mesh['groups'=2,'ctx'=8,'ch'=2] {'ctx'}, dimensions={0} | all-to-all | bytes 262144 | tf_op jit(solution)/shard_map/all_to_all | solution.py:268
  40.7 0.8 %copy.19 = bf16[256,256]{0,1:T(8,128)(2,1)} copy(bf16[256,256]{1,0:T(8,128)(2,1)S(1)} %bitcast.7) | data formatting | bytes 262144 | tf_op jit(solution)/shard_map/reshape | solution.py:269
Async XLA Ops:
  0.0 11.1 %copy-start = (f32[256]{0:T(256)S(1)}, f32[256]{0:T(256)}, u32[]{:S(2)}) copy-start(f32[256]{0:T(256)} %param.19) | copy-start | bytes 3076
  2.2 21.7 %all-to-all-start = ((bf16[8,4,32,256]{3,2,1,0:T(8,128)(2,1)}), bf16[8,4,32,256]{3,2,1,0:T(8,128)(2,1)S(1)}, u32[]{:S(2)}, u32[]{:S(2)}) async-start(bf16[8,4,32,256]{3,2,1,0:T(8,128)(2,1)} %shard_map.136), calls=%async_computation | async-start | bytes 1048576 | tf_op jit(solution)/shard_map/all_to_all | solution.py:246
  9.5 0.7 %copy-start.2 = (bf16[3,3,256]{2,1,0:T(4,128)(2,1)S(1)}, bf16[3,3,256]{2,1,0:T(4,128)(2,1)}, u32[]{:S(2)}) copy-start(bf16[3,3,256]{2,1,0:T(4,128)(2,1)} %param.17) | copy-start | bytes 13828
  24.0 0.8 %copy-start.1 = (bf16[8,4,32,256]{3,2,1,0:T(8,128)(2,1)}, bf16[8,4,32,256]{3,2,1,0:T(8,128)(2,1)S(1)}, u32[]{:S(2)}) copy-start(bf16[8,4,32,256]{3,2,1,0:T(8,128)(2,1)S(1)} %all-to-all-done.sig) | copy-start | bytes 1572868

commit v8 on v7

--- a/solution.py
+++ b/solution.py
@@ -103,15 +103,14 @@
     unrolled = blocks <= 16
     f32 = jnp.float32
     lane = lax.broadcasted_iota(jnp.int32, (blocks, piece, rows), 2)
-    ext[0] = jnp.zeros((piece, rows), f32)
 
     def conv(stream, weights):
         x = sig[:, stream].astype(f32)
         total = kern[weights, 0] * x
         for lag in range(1, taps):
             rolled = pltpu.roll(x, lag, 2)
-            ext[pl.ds(1, blocks)] = rolled
-            earlier = jnp.where(lane < lag, ext[pl.ds(0, blocks)], rolled)
+            before = jnp.concatenate([jnp.zeros_like(rolled[:1]), rolled[:-1]], axis=0)
+            earlier = jnp.where(lane < lag, before, rolled)
             total = total + kern[weights, lag] * earlier
         return total
 
@@ -131,11 +130,17 @@
                 xs = [(load_block(which, d, at), None) for d in range(blocks)]
                 spectrum = fft(xs + [(None, None)] * blocks, -1.0)
                 for k in range(half):
+                    c, s = twist[0, k], twist[1, k]
+                    re, im = spectrum[k]
+                    if im is None:
+                        turned = (re * c, re * s)
+                    elif re is None:
+                        turned = (-(im * s), im * c)
+                    else:
+                        turned = (re * c - im * s, re * s + im * c)
                     for part in range(2):
-                        value = spectrum[k][part]
-                        if value is None:
-                            value = jnp.zeros((tile, rows), f32)
-                        a_all[pl.ds(base + k * piece + tile_index * tile, tile), pl.ds(part * rows, rows)] = value
+                        a_all[pl.ds(base + k * piece + tile_index * tile, tile), pl.ds(part * rows, rows)] = (
+                            turned[part])
             else:
                 for k in range(half):
                     for part in range(2):
@@ -152,7 +157,7 @@
 
                 lax.fori_loop(0, blocks, step, 0)
 
-    for which in range(2):
+    for which in range(0 if unrolled else 2):
         for k in range(half):
             at_rows = pl.ds(which * half * piece + k * piece, piece)
             re = a_all[at_rows, pl.ds(0, rows)]
@@ -172,14 +177,21 @@
     q_im = halves(gr * hi + gi * hr)
     y_re = times(q_re, c_hi, c_lo) - times(q_im, s_hi, s_lo)
     y_im = times(q_re, s_hi, s_lo) + times(q_im, c_hi, c_lo)
-    for k in range(half):
-        at_rows = pl.ds(k * piece, piece)
+    def untwisted(k, at_tile):
+        lo = k * piece + at_tile * tile
+        yr = y_re[lo:lo + tile]
+        yi = y_im[lo:lo + tile]
         u_re = untwist[0, k]
         u_im = untwist[1, k]
-        yr = y_re[k * piece:(k + 1) * piece]
-        yi = y_im[k * piece:(k + 1) * piece]
-        a_h[at_rows, pl.ds(0, rows)] = yr * u_re - yi * u_im
-        a_h[at_rows, pl.ds(rows, rows)] = yr * u_im + yi * u_re
+        return yr * u_re - yi * u_im, yr * u_im + yi * u_re
+
+    if not unrolled:
+        for k in range(half):
+            at_rows = pl.ds(k * piece, piece)
+            yr = y_re[k * piece:(k + 1) * piece]
+            yi = y_im[k * piece:(k + 1) * piece]
+            a_h[at_rows, pl.ds(0, rows)] = yr * untwist[0, k] - yi * untwist[1, k]
+            a_h[at_rows, pl.ds(rows, rows)] = yr * untwist[1, k] + yi * untwist[0, k]
 
     for tile_index in range(piece // tile):
         at = pl.ds(tile_index * tile, tile)
@@ -195,11 +207,7 @@
             out[d, at, :] = (o_s[d, at, :] * (acc + scale * gated)).astype(out.dtype)
 
         if unrolled:
-            held = [
-                tuple(a_h[pl.ds(k * piece + tile_index * tile, tile), pl.ds(part * rows, rows)]
-                      for part in range(2))
-                for k in range(half)
-            ]
+            held = [untwisted(k, tile_index) for k in range(half)]
             full = held + [(re, -im) for re, im in reversed(held[1:blocks])]
             signal = fft(full, 1.0)
             for d in range(blocks):

time: 41.8 us -> 41.8 us (level)
  no operation moved by 1% of the time
where the time goes in v8:
time: 41.8 us; the launch traced here: 41.4 us
  waiting for transfers between devices  12.2 us (29%)
  blocking collectives  11 us (26%)
  starting transfers between devices  7.25 us (17%)
  Pallas kernels  7.16 us (17%)
  local copies, waits for them, and re-layouts  3.8 us (9%)
    all_to_all x1, waiting for transfers between devices, body(): gathered = lax.all_to_all(stacked, 'ctx', 0, 0)  12.2 us
    all_to_all x1, blocking collectives, body(): returned = lax.all_to_all(out, 'ctx', 0, 0)  11 us
    all_to_all x1, starting transfers between devices, body(): gathered = lax.all_to_all(stacked, 'ctx', 0, 0)  7.25 us
    pallas_call x1, Pallas kernels, body(): pl.pallas_call(local_kernel, out_shape=jax.ShapeDtypeStruct((blocks, piec...  4.93 us
    pallas_call x1, Pallas kernels, body(): pl.pallas_call(to_blocks_kernel, out_shape=jax.ShapeDtypeStruct((blocks,...  2.24 us
    unnamed x6, local copies, waits for them, and re-layouts  1.49 us
  transfers between devices with their start and end apart: 1, of which 1 were waited for; matrix products, arithmetic and copies ran while one was open for 4% of the time, Pallas kernels for 0%

profile of v8, /device:TPU:0, one launch (start us, length us, event | category | flops | bytes accessed | tf_op | source)
XLA Modules:
  0.0 41.4 jit_solution(10182574690993121296)
XLA Ops:
  0.0 0.0 copy-start
  0.0 2.2 %shard_map.136 = bf16[8,4,32,256]{3,2,1,0:T(8,128)(2,1)} custom-call(bf16[256,256]{1,0:T(8,128)(2,1)} %refs_0_.1, bf16[256,256]{1,0:T(8,128)(2,1)} %refs_1_.1, bf16[256,256]{1,0:T(8,128)(2,1)} %refs_2_.1, bf16[256,256]{1,0:T(8,128)(2,1)} %refs_3_.1), custom_call_target="tpu_custom_call" | custom-call | tf_op jit(solution)/shard_map/pallas_call | solution.py:247
  2.2 7.3 %all-to-all-start = ((bf16[8,4,32,256]{3,2,1,0:T(8,128)(2,1)}), bf16[8,4,32,256]{3,2,1,0:T(8,128)(2,1)S(1)}, u32[]{:S(2)}, u32[]{:S(2)}) async-start(bf16[8,4,32,256]{3,2,1,0:T(8,128)(2,1)} %shard_map.136), calls=%async_computation | async-start | bytes 1048576 | tf_op jit(solution)/shard_map/all_to_all | solution.py:254
  9.5 0.0 copy-start.2
  9.5 0.7 %copy-done.2 = bf16[3,3,256]{2,1,0:T(4,128)(2,1)S(1)} copy-done((bf16[3,3,256]{2,1,0:T(4,128)(2,1)S(1)}, bf16[3,3,256]{2,1,0:T(4,128)(2,1)}, u32[]{:S(2)}) %copy-start.2) | copy-done | bytes 4632
  10.2 0.1 bitcast_convert_fusion
  10.3 0.8 %copy.17.kern = f32[3,3,32,1]{3,2,1,0:T(8,128)} copy(f32[3,3,32,1]{2,1,0,3:T(4,128)S(1)} %bitcast_convert_fusion) | data formatting | bytes 2304 | tf_op jit(solution)/shard_map/broadcast_in_dim | solution.py:257
  11.1 0.0 copy-done
  11.1 0.1 dynamic-slice_bitcast_fusion
  11.1 0.7 %copy.18.gain = f32[32,1]{1,0:T(8,128)} copy(f32[32,1]{0,1:T(1,128)S(1)} %dynamic-slice_bitcast_fusion) | data formatting | bytes 256 | tf_op jit(solution)/shard_map/broadcast_in_dim | solution.py:258
  11.8 12.2 %all-to-all-done.sig = bf16[8,4,32,256]{3,2,1,0:T(8,128)(2,1)S(1)} async-done(((bf16[8,4,32,256]{3,2,1,0:T(8,128)(2,1)}), bf16[8,4,32,256]{3,2,1,0:T(8,128)(2,1)S(1)}, u32[]{:S(2)}, u32[]{:S(2)}) %all-to-all-start) | async-done | bytes 524320 | tf_op jit(solution)/shard_map/all_to_all | solution.py:254
  24.0 0.0 copy-start.1
  24.0 0.8 %copy-done.1 = bf16[8,4,32,256]{3,2,1,0:T(8,128)(2,1)} copy-done((bf16[8,4,32,256]{3,2,1,0:T(8,128)(2,1)}, bf16[8,4,32,256]{3,2,1,0:T(8,128)(2,1)S(1)}, u32[]{:S(2)}) %copy-start.1) | copy-done | bytes 524312
  24.8 4.9 %shard_map.137 = bf16[8,32,256]{2,1,0:T(8,128)(2,1)} custom-call(f32[18,8]{1,0:T(8,128)} %constant.28.clone.first, f32[8,18]{1,0:T(8,128)} %constant.29.clone.last, bf16[8,4,32,256]{3,2,1,0:T(8,128)(2,1)} %copy-done.1, f32[3,3,32,1]{3,2,1,0:T(8,128)} %copy.17.kern, f32[32,1]{1,0:T(8,128)} %copy.18.gain, f32[2,9,1,256]{3,2,1,0:T(1,128)} %constant.30.clone.twist, ...), custom_call_target="tpu_custom_call" | custom-call | tf_op jit(solution)/shard_map/pallas_call | solution.py:262
  29.7 11.0 %all_to_all.10 = bf16[8,32,256]{2,1,0:T(8,128)(2,1)S(1)} all-to-all(bf16[8,32,256]{2,1,0:T(8,128)(2,1)} %shard_map.137), channel_id=1, replica_groups=mesh['groups'=2,'ctx'=8,'ch'=2] {'ctx'}, dimensions={0} | all-to-all | bytes 262144 | tf_op jit(solution)/shard_map/all_to_all | solution.py:276
  40.7 0.8 %copy.19 = bf16[256,256]{0,1:T(8,128)(2,1)} copy(bf16[256,256]{1,0:T(8,128)(2,1)S(1)} %bitcast.7) | data formatting | bytes 262144 | tf_op jit(solution)/shard_map/reshape | solution.py:277
Async XLA Ops:
  0.0 11.1 %copy-start = (f32[256]{0:T(256)S(1)}, f32[256]{0:T(256)}, u32[]{:S(2)}) copy-start(f32[256]{0:T(256)} %param.19) | copy-start | bytes 3076
  2.2 21.7 %all-to-all-start = ((bf16[8,4,32,256]{3,2,1,0:T(8,128)(2,1)}), bf16[8,4,32,256]{3,2,1,0:T(8,128)(2,1)S(1)}, u32[]{:S(2)}, u32[]{:S(2)}) async-start(bf16[8,4,32,256]{3,2,1,0:T(8,128)(2,1)} %shard_map.136), calls=%async_computation | async-start | bytes 1048576 | tf_op jit(solution)/shard_map/all_to_all | solution.py:254
  9.5 0.7 %copy-start.2 = (bf16[3,3,256]{2,1,0:T(4,128)(2,1)S(1)}, bf16[3,3,256]{2,1,0:T(4,128)(2,1)}, u32[]{:S(2)}) copy-start(bf16[3,3,256]{2,1,0:T(4,128)(2,1)} %param.17) | copy-start | bytes 13828
  24.0 0.8 %copy-start.1 = (bf16[8,4,32,256]{3,2,1,0:T(8,128)(2,1)}, bf16[8,4,32,256]{3,2,1,0:T(8,128)(2,1)S(1)}, u32[]{:S(2)}) copy-start(bf16[8,4,32,256]{3,2,1,0:T(8,128)(2,1)S(1)} %all-to-all-done.sig) | copy-start | bytes 1572868

commit v9 on v8

--- a/solution.py
+++ b/solution.py
@@ -273,7 +273,8 @@
         ],
     )(first, last, gathered, kern, gain, twist, untwist, c_hi, c_lo, s_hi, s_lo)
 
-    returned = lax.all_to_all(out, "ctx", 0, 0)
+    everything = lax.all_gather(out, "ctx", axis=0)
+    returned = lax.dynamic_index_in_dim(everything, me, axis=1, keepdims=False)
     return jnp.swapaxes(returned.reshape(chans, rows), 0, 1)
 
 

time: 41.8 us -> 84.5 us (2.02)
  waiting for transfers between devices: 12.2 us -> 51.5 us
  between operations: 0.01 us -> 13.4 us
  blocking collectives: 11 us -> 0 us
  local copies, waits for them, and re-layouts: 3.8 us -> 4.7 us
    all_gather x0 -> x1, waiting for transfers between devices: none -> 39.4 us  [body(): everything = lax.all_gather(out, 'ctx', axis=0)]
    all_to_all x1 -> x0, blocking collectives: 11 us -> none  [body(): returned = lax.all_to_all(out, 'ctx', 0, 0)]
    dynamic_slice x0 -> x1, local copies, waits for them, and re-layouts: none -> 0.91 us  [body(): returned = lax.dynamic_index_in_dim(everything, me, axis=1, keepdims=False)]
  transfers between devices with their start and end apart: 1 -> 2, of which waited for: 1 -> 2; matrix products, arithmetic and copies ran while one was open for 4% -> 2% of each run, Pallas kernels for 0% -> 0%
where the time goes in v9:
time: 84.5 us; the launch traced here: 84.2 us
  waiting for transfers between devices  51.5 us (61%)
  between operations  13.4 us (16%)
  starting transfers between devices  7.29 us (9%)
  Pallas kernels  7.15 us (8%)
  local copies, waits for them, and re-layouts  4.7 us (6%)
    all_gather x1, waiting for transfers between devices, body(): everything = lax.all_gather(out, 'ctx', axis=0)  39.4 us
    all_to_all x1, waiting for transfers between devices, body(): gathered = lax.all_to_all(stacked, 'ctx', 0, 0)  12.1 us
    all_to_all x1, starting transfers between devices, body(): gathered = lax.all_to_all(stacked, 'ctx', 0, 0)  7.25 us
    pallas_call x1, Pallas kernels, body(): pl.pallas_call(local_kernel, out_shape=jax.ShapeDtypeStruct((blocks, piec...  4.92 us
    pallas_call x1, Pallas kernels, body(): pl.pallas_call(to_blocks_kernel, out_shape=jax.ShapeDtypeStruct((blocks,...  2.23 us
  transfers between devices with their start and end apart: 2, of which 2 were waited for; matrix products, arithmetic and copies ran while one was open for 2% of the time, Pallas kernels for 0%

profile of v9, /device:TPU:0, one launch (start us, length us, event | category | flops | bytes accessed | tf_op | source)
XLA Modules:
  0.0 84.2 jit_solution(4574739819152196669)
XLA Ops:
  6.5 0.0 copy-start
  6.5 2.2 %shard_map.136 = bf16[8,4,32,256]{3,2,1,0:T(8,128)(2,1)} custom-call(bf16[256,256]{1,0:T(8,128)(2,1)} %refs_0_.1, bf16[256,256]{1,0:T(8,128)(2,1)} %refs_1_.1, bf16[256,256]{1,0:T(8,128)(2,1)} %refs_2_.1, bf16[256,256]{1,0:T(8,128)(2,1)} %refs_3_.1), custom_call_target="tpu_custom_call" | custom-call | tf_op jit(solution)/shard_map/pallas_call | solution.py:247
  8.8 7.3 %all-to-all-start = ((bf16[8,4,32,256]{3,2,1,0:T(8,128)(2,1)}), bf16[8,4,32,256]{3,2,1,0:T(8,128)(2,1)S(1)}, u32[]{:S(2)}, u32[]{:S(2)}) async-start(bf16[8,4,32,256]{3,2,1,0:T(8,128)(2,1)} %shard_map.136), calls=%async_computation | async-start | bytes 1048576 | tf_op jit(solution)/shard_map/all_to_all | solution.py:254
  16.0 0.0 all-gather.3.cloned.1.call-start
  16.1 0.0 copy-start.2
  16.1 0.7 copy-done.2
  16.8 0.1 bitcast_convert_fusion
  16.8 0.8 copy.24.kern
  17.6 0.0 copy-done
  17.6 0.1 dynamic-slice_bitcast_fusion
  17.7 0.7 copy.25.gain
  18.4 12.1 %all-to-all-done.sig = bf16[8,4,32,256]{3,2,1,0:T(8,128)(2,1)S(1)} async-done(((bf16[8,4,32,256]{3,2,1,0:T(8,128)(2,1)}), bf16[8,4,32,256]{3,2,1,0:T(8,128)(2,1)S(1)}, u32[]{:S(2)}, u32[]{:S(2)}) %all-to-all-start) | async-done | bytes 524320 | tf_op jit(solution)/shard_map/all_to_all | solution.py:254
  30.5 0.0 copy-start.1
  30.5 0.8 copy-done.1
  31.3 4.9 %shard_map.137 = bf16[8,32,256]{2,1,0:T(8,128)(2,1)} custom-call(f32[18,8]{1,0:T(8,128)} %constant.33.clone.first, f32[8,18]{1,0:T(8,128)} %constant.34.clone.last, bf16[8,4,32,256]{3,2,1,0:T(8,128)(2,1)} %copy-done.1, f32[3,3,32,1]{3,2,1,0:T(8,128)} %copy.24.kern, f32[32,1]{1,0:T(8,128)} %copy.25.gain, f32[2,9,1,256]{3,2,1,0:T(1,128)} %constant.35.clone.twist, ...), custom_call_target="tpu_custom_call" | custom-call | tf_op jit(solution)/shard_map/pallas_call | solution.py:262
  36.2 0.0 all-gather.3.cloned.1.call-update
  36.2 39.4 %all-gather.3.cloned.1.call-done = bf16[64,32,256]{2,1,0:T(8,128)(2,1)} async-done(((bf16[8,32,256]{2,1,0:T(8,128)(2,1)}), bf16[64,32,256]{2,1,0:T(8,128)(2,1)}) %all-gather.3.cloned.1.call-update) | async-done | bytes 1048592 | tf_op jit(solution)/shard_map/all_gather | solution.py:276
  75.6 0.9 %constant_dynamic-slice_fusion = bf16[8,1,32,256]{3,2,1,0:T(8,128)(2,1)S(1)} fusion(bf16[8,8,32,256]{3,2,1,0:T(8,128)(2,1)} %bitcast.10, s32[]{:T(128)S(6)} %select_n.9), kind=kLoop, calls=%fused_computation.2 | loop fusion | bytes 262148 | tf_op jit(solution)/shard_map/jit(dynamic_index_in_dim)/dynamic_slice | solution.py:277
  76.6 0.8 copy.26
Async XLA Ops:
  6.5 11.1 %copy-start = (f32[256]{0:T(256)S(1)}, f32[256]{0:T(256)}, u32[]{:S(2)}) copy-start(f32[256]{0:T(256)} %param.19) | copy-start | bytes 3076
  8.8 21.7 %all-to-all-start = ((bf16[8,4,32,256]{3,2,1,0:T(8,128)(2,1)}), bf16[8,4,32,256]{3,2,1,0:T(8,128)(2,1)S(1)}, u32[]{:S(2)}, u32[]{:S(2)}) async-start(bf16[8,4,32,256]{3,2,1,0:T(8,128)(2,1)} %shard_map.136), calls=%async_computation | async-start | bytes 1048576 | tf_op jit(solution)/shard_map/all_to_all | solution.py:254
  16.0 59.6 %all-gather.3.cloned.1.call-start = ((), (), s32[]{:S(2)}) async-start(), calls=%async_computation.1 | async-start | bytes 1179648 | tf_op jit(solution)/shard_map/all_gather | solution.py:276
  16.1 0.7 copy-start.2
  30.5 0.8 copy-start.1
Sparse Core Ops, SparseCore 0:
  36.4 39.2 all-gather.2

commit v10 on v8

--- a/solution.py
+++ b/solution.py
@@ -244,12 +244,15 @@
     first, last, twist, untwist, c_hi, c_lo, s_hi, s_lo = kernel_tables(blocks, rows)
 
     vmem = pl.BlockSpec(memory_space=pltpu.VMEM)
+    steps = 2
+    step_rows = rows // steps
     stacked = pl.pallas_call(
         to_blocks_kernel,
         out_shape=jax.ShapeDtypeStruct((blocks, 4, piece, rows), jnp.bfloat16),
-        in_specs=[vmem] * 4,
-        out_specs=vmem,
-        scratch_shapes=[pltpu.VMEM((chans, rows), jnp.float32)],
+        grid=(steps,),
+        in_specs=[pl.BlockSpec((step_rows, chans), lambda i: (i, 0))] * 4,
+        out_specs=pl.BlockSpec((blocks, 4, piece, step_rows), lambda i: (0, 0, 0, i)),
+        scratch_shapes=[pltpu.VMEM((chans, step_rows), jnp.float32)],
     )(gate_stream, value_stream, outer_stream, long_filter)
     gathered = lax.all_to_all(stacked, "ctx", 0, 0)
 

time: 41.8 us -> 41.9 us (level)
  no operation moved by 1% of the time
where the time goes in v10:
time: 41.9 us; the launch traced here: 41.5 us
  waiting for transfers between devices  12.2 us (29%)
  blocking collectives  11 us (26%)
  starting transfers between devices  7.25 us (17%)
  Pallas kernels  7.22 us (17%)
  local copies, waits for them, and re-layouts  3.8 us (9%)
    all_to_all x1, waiting for transfers between devices, body(): gathered = lax.all_to_all(stacked, 'ctx', 0, 0)  12.2 us
    all_to_all x1, blocking collectives, body(): returned = lax.all_to_all(out, 'ctx', 0, 0)  11 us
    all_to_all x1, starting transfers between devices, body(): gathered = lax.all_to_all(stacked, 'ctx', 0, 0)  7.25 us
    pallas_call x1, Pallas kernels, body(): pl.pallas_call(local_kernel, out_shape=jax.ShapeDtypeStruct((blocks, piec...  4.93 us
    pallas_call x1, Pallas kernels, body(): pl.pallas_call(to_blocks_kernel, out_shape=jax.ShapeDtypeStruct((blocks,...  2.29 us
    unnamed x6, local copies, waits for them, and re-layouts  1.49 us
  transfers between devices with their start and end apart: 1, of which 1 were waited for; matrix products, arithmetic and copies ran while one was open for 4% of the time, Pallas kernels for 0%

profile of v10, /device:TPU:0, one launch (start us, length us, event | category | flops | bytes accessed | tf_op | source)
XLA Modules:
  0.0 41.5 jit_solution(8081278482059905962)
XLA Ops:
  0.0 0.0 copy-start
  0.0 2.3 %shard_map.136 = bf16[8,4,32,256]{3,2,1,0:T(8,128)(2,1)} custom-call(bf16[256,256]{1,0:T(8,128)(2,1)} %refs_0_.1, bf16[256,256]{1,0:T(8,128)(2,1)} %refs_1_.1, bf16[256,256]{1,0:T(8,128)(2,1)} %refs_2_.1, bf16[256,256]{1,0:T(8,128)(2,1)} %refs_3_.1), custom_call_target="tpu_custom_call" | custom-call | tf_op jit(solution)/shard_map/pallas_call | solution.py:249
  2.3 7.3 %all-to-all-start = ((bf16[8,4,32,256]{3,2,1,0:T(8,128)(2,1)}), bf16[8,4,32,256]{3,2,1,0:T(8,128)(2,1)S(1)}, u32[]{:S(2)}, u32[]{:S(2)}) async-start(bf16[8,4,32,256]{3,2,1,0:T(8,128)(2,1)} %shard_map.136), calls=%async_computation | async-start | bytes 1048576 | tf_op jit(solution)/shard_map/all_to_all | solution.py:257
  9.5 0.0 copy-start.2
  9.6 0.7 %copy-done.2 = bf16[3,3,256]{2,1,0:T(4,128)(2,1)S(1)} copy-done((bf16[3,3,256]{2,1,0:T(4,128)(2,1)S(1)}, bf16[3,3,256]{2,1,0:T(4,128)(2,1)}, u32[]{:S(2)}) %copy-start.2) | copy-done | bytes 4632
  10.2 0.1 bitcast_convert_fusion
  10.3 0.8 %copy.17.kern = f32[3,3,32,1]{3,2,1,0:T(8,128)} copy(f32[3,3,32,1]{2,1,0,3:T(4,128)S(1)} %bitcast_convert_fusion) | data formatting | bytes 2304 | tf_op jit(solution)/shard_map/broadcast_in_dim | solution.py:260
  11.1 0.0 copy-done
  11.1 0.1 dynamic-slice_bitcast_fusion
  11.2 0.7 %copy.18.gain = f32[32,1]{1,0:T(8,128)} copy(f32[32,1]{0,1:T(1,128)S(1)} %dynamic-slice_bitcast_fusion) | data formatting | bytes 256 | tf_op jit(solution)/shard_map/broadcast_in_dim | solution.py:261
  11.9 12.2 %all-to-all-done.sig = bf16[8,4,32,256]{3,2,1,0:T(8,128)(2,1)S(1)} async-done(((bf16[8,4,32,256]{3,2,1,0:T(8,128)(2,1)}), bf16[8,4,32,256]{3,2,1,0:T(8,128)(2,1)S(1)}, u32[]{:S(2)}, u32[]{:S(2)}) %all-to-all-start) | async-done | bytes 524320 | tf_op jit(solution)/shard_map/all_to_all | solution.py:257
  24.0 0.0 copy-start.1
  24.0 0.8 %copy-done.1 = bf16[8,4,32,256]{3,2,1,0:T(8,128)(2,1)} copy-done((bf16[8,4,32,256]{3,2,1,0:T(8,128)(2,1)}, bf16[8,4,32,256]{3,2,1,0:T(8,128)(2,1)S(1)}, u32[]{:S(2)}) %copy-start.1) | copy-done | bytes 524312
  24.8 4.9 %shard_map.137 = bf16[8,32,256]{2,1,0:T(8,128)(2,1)} custom-call(f32[18,8]{1,0:T(8,128)} %constant.28.clone.first, f32[8,18]{1,0:T(8,128)} %constant.29.clone.last, bf16[8,4,32,256]{3,2,1,0:T(8,128)(2,1)} %copy-done.1, f32[3,3,32,1]{3,2,1,0:T(8,128)} %copy.17.kern, f32[32,1]{1,0:T(8,128)} %copy.18.gain, f32[2,9,1,256]{3,2,1,0:T(1,128)} %constant.30.clone.twist, ...), custom_call_target="tpu_custom_call" | custom-call | tf_op jit(solution)/shard_map/pallas_call | solution.py:265
  29.8 11.0 %all_to_all.10 = bf16[8,32,256]{2,1,0:T(8,128)(2,1)S(1)} all-to-all(bf16[8,32,256]{2,1,0:T(8,128)(2,1)} %shard_map.137), channel_id=1, replica_groups=mesh['groups'=2,'ctx'=8,'ch'=2] {'ctx'}, dimensions={0} | all-to-all | bytes 262144 | tf_op jit(solution)/shard_map/all_to_all | solution.py:279
  40.7 0.8 %copy.19 = bf16[256,256]{0,1:T(8,128)(2,1)} copy(bf16[256,256]{1,0:T(8,128)(2,1)S(1)} %bitcast.7) | data formatting | bytes 262144 | tf_op jit(solution)/shard_map/reshape | solution.py:280
Async XLA Ops:
  0.0 11.1 %copy-start = (f32[256]{0:T(256)S(1)}, f32[256]{0:T(256)}, u32[]{:S(2)}) copy-start(f32[256]{0:T(256)} %param.19) | copy-start | bytes 3076
  2.3 21.7 %all-to-all-start = ((bf16[8,4,32,256]{3,2,1,0:T(8,128)(2,1)}), bf16[8,4,32,256]{3,2,1,0:T(8,128)(2,1)S(1)}, u32[]{:S(2)}, u32[]{:S(2)}) async-start(bf16[8,4,32,256]{3,2,1,0:T(8,128)(2,1)} %shard_map.136), calls=%async_computation | async-start | bytes 1048576 | tf_op jit(solution)/shard_map/all_to_all | solution.py:257
  9.5 0.7 %copy-start.2 = (bf16[3,3,256]{2,1,0:T(4,128)(2,1)S(1)}, bf16[3,3,256]{2,1,0:T(4,128)(2,1)}, u32[]{:S(2)}) copy-start(bf16[3,3,256]{2,1,0:T(4,128)(2,1)} %param.17) | copy-start | bytes 13828
  24.0 0.8 %copy-start.1 = (bf16[8,4,32,256]{3,2,1,0:T(8,128)(2,1)}, bf16[8,4,32,256]{3,2,1,0:T(8,128)(2,1)S(1)}, u32[]{:S(2)}) copy-start(bf16[8,4,32,256]{3,2,1,0:T(8,128)(2,1)S(1)} %all-to-all-done.sig) | copy-start | bytes 1572868

commit v11 on v8

--- a/solution.py
+++ b/solution.py
@@ -251,7 +251,8 @@
         out_specs=vmem,
         scratch_shapes=[pltpu.VMEM((chans, rows), jnp.float32)],
     )(gate_stream, value_stream, outer_stream, long_filter)
-    gathered = lax.all_to_all(stacked, "ctx", 0, 0)
+    flat = stacked.reshape(blocks * 4 * piece, rows)
+    gathered = lax.all_to_all(flat, "ctx", 0, 0, tiled=True).reshape(stacked.shape)
 
     kern = lax.dynamic_slice_in_dim(short_weight, me * piece, piece, axis=2).astype(jnp.float32)
     kern = kern[..., None]
@@ -273,8 +274,8 @@
         ],
     )(first, last, gathered, kern, gain, twist, untwist, c_hi, c_lo, s_hi, s_lo)
 
-    returned = lax.all_to_all(out, "ctx", 0, 0)
-    return jnp.swapaxes(returned.reshape(chans, rows), 0, 1)
+    returned = lax.all_to_all(out.reshape(chans, rows), "ctx", 0, 0, tiled=True)
+    return jnp.swapaxes(returned, 0, 1)
 
 
 def solution(mesh):

time: 41.8 us -> 41.8 us (level)
    all_to_all x0 -> x1, local copies, waits for them, and re-layouts: none -> 0.76 us  [body(): returned = lax.all_to_all(out.reshape(chans, rows), 'ctx', 0, 0, tiled=True)]
    reshape x1 -> x0, local copies, waits for them, and re-layouts: 0.76 us -> none  [body(): return jnp.swapaxes(returned.reshape(chans, rows), 0, 1)]
where the time goes in v11:
time: 41.8 us; the launch traced here: 41.4 us
  waiting for transfers between devices  12.2 us (29%)
  blocking collectives  11 us (26%)
  starting transfers between devices  7.25 us (17%)
  Pallas kernels  7.16 us (17%)
  local copies, waits for them, and re-layouts  3.8 us (9%)
    all_to_all x1, waiting for transfers between devices, body(): lax.all_to_all(flat, 'ctx', 0, 0, tiled=True).reshape(stacked.shape)  12.2 us
    all_to_all x1, blocking collectives, body(): returned = lax.all_to_all(out.reshape(chans, rows), 'ctx', 0, 0, tiled=True)  11 us
    all_to_all x1, starting transfers between devices, body(): lax.all_to_all(flat, 'ctx', 0, 0, tiled=True).reshape(stacked.shape)  7.25 us
    pallas_call x1, Pallas kernels, body(): pl.pallas_call(local_kernel, out_shape=jax.ShapeDtypeStruct((blocks, piec...  4.93 us
    pallas_call x1, Pallas kernels, body(): pl.pallas_call(to_blocks_kernel, out_shape=jax.ShapeDtypeStruct((blocks,...  2.24 us
    unnamed x6, local copies, waits for them, and re-layouts  1.49 us
  transfers between devices with their start and end apart: 1, of which 1 were waited for; matrix products, arithmetic and copies ran while one was open for 4% of the time, Pallas kernels for 0%

profile of v11, /device:TPU:0, one launch (start us, length us, event | category | flops | bytes accessed | tf_op | source)
XLA Modules:
  0.0 41.4 jit_solution(10460498125281923330)
XLA Ops:
  0.0 0.0 copy-start
  0.0 2.2 %shard_map.136 = bf16[8,4,32,256]{3,2,1,0:T(8,128)(2,1)} custom-call(bf16[256,256]{1,0:T(8,128)(2,1)} %refs_0_.1, bf16[256,256]{1,0:T(8,128)(2,1)} %refs_1_.1, bf16[256,256]{1,0:T(8,128)(2,1)} %refs_2_.1, bf16[256,256]{1,0:T(8,128)(2,1)} %refs_3_.1), custom_call_target="tpu_custom_call" | custom-call | tf_op jit(solution)/shard_map/pallas_call | solution.py:247
  2.2 7.3 %all-to-all-start = ((bf16[8,128,256]{2,1,0:T(8,128)(2,1)}), bf16[8,128,256]{2,1,0:T(8,128)(2,1)S(1)}, u32[]{:S(2)}, u32[]{:S(2)}) async-start(bf16[8,128,256]{2,1,0:T(8,128)(2,1)} %bitcast.10), calls=%async_computation | async-start | bytes 1048576 | tf_op jit(solution)/shard_map/all_to_all | solution.py:255
  9.5 0.0 copy-start.2
  9.5 0.7 %copy-done.2 = bf16[3,3,256]{2,1,0:T(4,128)(2,1)S(1)} copy-done((bf16[3,3,256]{2,1,0:T(4,128)(2,1)S(1)}, bf16[3,3,256]{2,1,0:T(4,128)(2,1)}, u32[]{:S(2)}) %copy-start.2) | copy-done | bytes 4632
  10.2 0.1 bitcast_convert_fusion
  10.3 0.8 %copy.17.kern = f32[3,3,32,1]{3,2,1,0:T(8,128)} copy(f32[3,3,32,1]{2,1,0,3:T(4,128)S(1)} %bitcast_convert_fusion) | data formatting | bytes 2304 | tf_op jit(solution)/shard_map/broadcast_in_dim | solution.py:258
  11.1 0.0 copy-done
  11.1 0.1 dynamic-slice_bitcast_fusion
  11.1 0.7 %copy.18.gain = f32[32,1]{1,0:T(8,128)} copy(f32[32,1]{0,1:T(1,128)S(1)} %dynamic-slice_bitcast_fusion) | data formatting | bytes 256 | tf_op jit(solution)/shard_map/broadcast_in_dim | solution.py:259
  11.8 12.2 %all-to-all-done = bf16[8,128,256]{2,1,0:T(8,128)(2,1)S(1)} async-done(((bf16[8,128,256]{2,1,0:T(8,128)(2,1)}), bf16[8,128,256]{2,1,0:T(8,128)(2,1)S(1)}, u32[]{:S(2)}, u32[]{:S(2)}) %all-to-all-start) | async-done | bytes 524320 | tf_op jit(solution)/shard_map/all_to_all | solution.py:255
  24.0 0.0 copy-start.1
  24.0 0.8 %copy-done.1 = bf16[8,128,256]{2,1,0:T(8,128)(2,1)} copy-done((bf16[8,128,256]{2,1,0:T(8,128)(2,1)}, bf16[8,128,256]{2,1,0:T(8,128)(2,1)S(1)}, u32[]{:S(2)}) %copy-start.1) | copy-done | bytes 524312
  24.8 4.9 %shard_map.137 = bf16[8,32,256]{2,1,0:T(8,128)(2,1)} custom-call(f32[18,8]{1,0:T(8,128)} %constant.28.clone.first, f32[8,18]{1,0:T(8,128)} %constant.29.clone.last, bf16[8,4,32,256]{3,2,1,0:T(8,128)(2,1)} %bitcast.9, f32[3,3,32,1]{3,2,1,0:T(8,128)} %copy.17.kern, f32[32,1]{1,0:T(8,128)} %copy.18.gain, f32[2,9,1,256]{3,2,1,0:T(1,128)} %constant.30.clone.twist, ...), custom_call_target="tpu_custom_call" | custom-call | tf_op jit(solution)/shard_map/pallas_call | solution.py:263
  29.7 11.0 %all_to_all.18 = bf16[8,32,256]{2,1,0:T(8,128)(2,1)S(1)} all-to-all(bf16[8,32,256]{2,1,0:T(8,128)(2,1)} %shard_map.137), channel_id=1, replica_groups=mesh['groups'=2,'ctx'=8,'ch'=2] {'ctx'}, dimensions={0} | all-to-all | bytes 262144 | tf_op jit(solution)/shard_map/all_to_all | solution.py:277
  40.7 0.8 %copy.19 = bf16[256,256]{0,1:T(8,128)(2,1)} copy(bf16[256,256]{1,0:T(8,128)(2,1)S(1)} %bitcast.11) | data formatting | bytes 262144 | tf_op jit(solution)/shard_map/all_to_all | solution.py:277
Async XLA Ops:
  0.0 11.1 %copy-start = (f32[256]{0:T(256)S(1)}, f32[256]{0:T(256)}, u32[]{:S(2)}) copy-start(f32[256]{0:T(256)} %param.19) | copy-start | bytes 3076
  2.2 21.7 %all-to-all-start = ((bf16[8,128,256]{2,1,0:T(8,128)(2,1)}), bf16[8,128,256]{2,1,0:T(8,128)(2,1)S(1)}, u32[]{:S(2)}, u32[]{:S(2)}) async-start(bf16[8,128,256]{2,1,0:T(8,128)(2,1)} %bitcast.10), calls=%async_computation | async-start | bytes 1048576 | tf_op jit(solution)/shard_map/all_to_all | solution.py:255
  9.5 0.7 %copy-start.2 = (bf16[3,3,256]{2,1,0:T(4,128)(2,1)S(1)}, bf16[3,3,256]{2,1,0:T(4,128)(2,1)}, u32[]{:S(2)}) copy-start(bf16[3,3,256]{2,1,0:T(4,128)(2,1)} %param.17) | copy-start | bytes 13828
  24.0 0.8 %copy-start.1 = (bf16[8,128,256]{2,1,0:T(8,128)(2,1)}, bf16[8,128,256]{2,1,0:T(8,128)(2,1)S(1)}, u32[]{:S(2)}) copy-start(bf16[8,128,256]{2,1,0:T(8,128)(2,1)S(1)} %all-to-all-done) | copy-start | bytes 1572868

commit v12 on v8

--- a/solution.py
+++ b/solution.py
@@ -38,8 +38,10 @@
     last_angle = 2.0 * np.pi * np.outer(d, k2) / (2 * blocks)
     last = clean(np.concatenate([weight * np.cos(last_angle), -weight * np.sin(last_angle)], axis=1))
     as_f32 = lambda a: jnp.asarray(a.astype(np.float32))
-    return ((as_f32(first), as_f32(last), as_f32(twist), as_f32(untwist))
-            + split_table(np.cos(row_angle)) + split_table(np.sin(row_angle)))
+    c_hi, c_lo = split_table(np.cos(row_angle))
+    s_hi, s_lo = split_table(np.sin(row_angle))
+    turns = as_f32(np.concatenate([twist, untwist], axis=0))
+    return as_f32(first), as_f32(last), turns, jnp.stack([c_hi, c_lo, s_hi, s_lo])
 
 
 def scaled(terms):
@@ -94,8 +96,10 @@
     return out + jnp.dot(high, low_ref[...], preferred_element_type=jnp.float32)
 
 
-def local_kernel(first, last, sig, kern, gain, twist, untwist, c_hi, c_lo, s_hi, s_lo, out,
+def local_kernel(first, last, sig, kern, gain, turns, tabs, out,
                  ext, g_s, o_s, a_all, a_h):
+    twist, untwist = turns.at[0:2], turns.at[2:4]
+    c_hi, c_lo, s_hi, s_lo = (tabs.at[i] for i in range(4))
     blocks, piece, rows = out.shape
     half = blocks + 1
     taps = kern.shape[1]
@@ -241,7 +245,7 @@
     piece = chans // blocks
     half = blocks + 1
     me = lax.axis_index("ctx")
-    first, last, twist, untwist, c_hi, c_lo, s_hi, s_lo = kernel_tables(blocks, rows)
+    first, last, turns, tabs = kernel_tables(blocks, rows)
 
     vmem = pl.BlockSpec(memory_space=pltpu.VMEM)
     stacked = pl.pallas_call(
@@ -262,7 +266,7 @@
     out = pl.pallas_call(
         local_kernel,
         out_shape=jax.ShapeDtypeStruct((blocks, piece, rows), jnp.bfloat16),
-        in_specs=[smem, smem] + [vmem] * 9,
+        in_specs=[smem, smem] + [vmem] * 5,
         out_specs=vmem,
         scratch_shapes=[
             pltpu.VMEM((blocks + 1, piece, rows), f32),
@@ -271,7 +275,7 @@
             pltpu.VMEM((2 * half * piece, 2 * rows), f32),
             pltpu.VMEM((half * piece, 2 * rows), f32),
         ],
-    )(first, last, gathered, kern, gain, twist, untwist, c_hi, c_lo, s_hi, s_lo)
+    )(first, last, gathered, kern, gain, turns, tabs)
 
     returned = lax.all_to_all(out, "ctx", 0, 0)
     return jnp.swapaxes(returned.reshape(chans, rows), 0, 1)

time: 41.8 us -> 41.8 us (level)
  no operation moved by 1% of the time
where the time goes in v12:
time: 41.8 us; the launch traced here: 41.4 us
  waiting for transfers between devices  12.2 us (29%)
  blocking collectives  11 us (26%)
  starting transfers between devices  7.25 us (17%)
  Pallas kernels  7.13 us (17%)
  local copies, waits for them, and re-layouts  3.8 us (9%)
    all_to_all x1, waiting for transfers between devices, body(): gathered = lax.all_to_all(stacked, 'ctx', 0, 0)  12.2 us
    all_to_all x1, blocking collectives, body(): returned = lax.all_to_all(out, 'ctx', 0, 0)  11 us
    all_to_all x1, starting transfers between devices, body(): gathered = lax.all_to_all(stacked, 'ctx', 0, 0)  7.25 us
    pallas_call x1, Pallas kernels, body(): pl.pallas_call(local_kernel, out_shape=jax.ShapeDtypeStruct((blocks, piec...  4.89 us
    pallas_call x1, Pallas kernels, body(): pl.pallas_call(to_blocks_kernel, out_shape=jax.ShapeDtypeStruct((blocks,...  2.24 us
    unnamed x6, local copies, waits for them, and re-layouts  1.49 us
  transfers between devices with their start and end apart: 1, of which 1 were waited for; matrix products, arithmetic and copies ran while one was open for 4% of the time, Pallas kernels for 0%

profile of v12, /device:TPU:0, one launch (start us, length us, event | category | flops | bytes accessed | tf_op | source)
XLA Modules:
  0.0 41.4 jit_solution(3395287704252857629)
XLA Ops:
  0.0 0.0 copy-start
  0.0 2.2 %shard_map.127 = bf16[8,4,32,256]{3,2,1,0:T(8,128)(2,1)} custom-call(bf16[256,256]{1,0:T(8,128)(2,1)} %refs_0_.1, bf16[256,256]{1,0:T(8,128)(2,1)} %refs_1_.1, bf16[256,256]{1,0:T(8,128)(2,1)} %refs_2_.1, bf16[256,256]{1,0:T(8,128)(2,1)} %refs_3_.1), custom_call_target="tpu_custom_call" | custom-call | tf_op jit(solution)/shard_map/pallas_call | solution.py:251
  2.2 7.3 %all-to-all-start = ((bf16[8,4,32,256]{3,2,1,0:T(8,128)(2,1)}), bf16[8,4,32,256]{3,2,1,0:T(8,128)(2,1)S(1)}, u32[]{:S(2)}, u32[]{:S(2)}) async-start(bf16[8,4,32,256]{3,2,1,0:T(8,128)(2,1)} %shard_map.127), calls=%async_computation | async-start | bytes 1048576 | tf_op jit(solution)/shard_map/all_to_all | solution.py:258
  9.5 0.0 copy-start.2
  9.5 0.7 %copy-done.2 = bf16[3,3,256]{2,1,0:T(4,128)(2,1)S(1)} copy-done((bf16[3,3,256]{2,1,0:T(4,128)(2,1)S(1)}, bf16[3,3,256]{2,1,0:T(4,128)(2,1)}, u32[]{:S(2)}) %copy-start.2) | copy-done | bytes 4632
  10.2 0.1 bitcast_convert_fusion
  10.3 0.8 %copy.16.kern = f32[3,3,32,1]{3,2,1,0:T(8,128)} copy(f32[3,3,32,1]{2,1,0,3:T(4,128)S(1)} %bitcast_convert_fusion) | data formatting | bytes 2304 | tf_op jit(solution)/shard_map/broadcast_in_dim | solution.py:261
  11.1 0.0 copy-done
  11.1 0.1 dynamic-slice_bitcast_fusion
  11.1 0.7 %copy.17.gain = f32[32,1]{1,0:T(8,128)} copy(f32[32,1]{0,1:T(1,128)S(1)} %dynamic-slice_bitcast_fusion) | data formatting | bytes 256 | tf_op jit(solution)/shard_map/broadcast_in_dim | solution.py:262
  11.8 12.2 %all-to-all-done.sig = bf16[8,4,32,256]{3,2,1,0:T(8,128)(2,1)S(1)} async-done(((bf16[8,4,32,256]{3,2,1,0:T(8,128)(2,1)}), bf16[8,4,32,256]{3,2,1,0:T(8,128)(2,1)S(1)}, u32[]{:S(2)}, u32[]{:S(2)}) %all-to-all-start) | async-done | bytes 524320 | tf_op jit(solution)/shard_map/all_to_all | solution.py:258
  24.0 0.0 copy-start.1
  24.0 0.8 %copy-done.1 = bf16[8,4,32,256]{3,2,1,0:T(8,128)(2,1)} copy-done((bf16[8,4,32,256]{3,2,1,0:T(8,128)(2,1)}, bf16[8,4,32,256]{3,2,1,0:T(8,128)(2,1)S(1)}, u32[]{:S(2)}) %copy-start.1) | copy-done | bytes 524312
  24.8 4.9 %shard_map.128 = bf16[8,32,256]{2,1,0:T(8,128)(2,1)} custom-call(f32[18,8]{1,0:T(8,128)} %constant.31.clone.first, f32[8,18]{1,0:T(8,128)} %constant.32.clone.last, bf16[8,4,32,256]{3,2,1,0:T(8,128)(2,1)} %copy-done.1, f32[3,3,32,1]{3,2,1,0:T(8,128)} %copy.16.kern, f32[32,1]{1,0:T(8,128)} %copy.17.gain, f32[4,9,1,256]{3,2,1,0:T(1,128)} %constant.30.clone.turns, ...), custom_call_target="tpu_custom_call" | custom-call | tf_op jit(solution)/shard_map/pallas_call | solution.py:266
  29.7 11.0 %all_to_all.10 = bf16[8,32,256]{2,1,0:T(8,128)(2,1)S(1)} all-to-all(bf16[8,32,256]{2,1,0:T(8,128)(2,1)} %shard_map.128), channel_id=1, replica_groups=mesh['groups'=2,'ctx'=8,'ch'=2] {'ctx'}, dimensions={0} | all-to-all | bytes 262144 | tf_op jit(solution)/shard_map/all_to_all | solution.py:280
  40.6 0.8 %copy.18 = bf16[256,256]{0,1:T(8,128)(2,1)} copy(bf16[256,256]{1,0:T(8,128)(2,1)S(1)} %bitcast.7) | data formatting | bytes 262144 | tf_op jit(solution)/shard_map/reshape | solution.py:281
Async XLA Ops:
  0.0 11.1 %copy-start = (f32[256]{0:T(256)S(1)}, f32[256]{0:T(256)}, u32[]{:S(2)}) copy-start(f32[256]{0:T(256)} %param.18) | copy-start | bytes 3076
  2.2 21.7 %all-to-all-start = ((bf16[8,4,32,256]{3,2,1,0:T(8,128)(2,1)}), bf16[8,4,32,256]{3,2,1,0:T(8,128)(2,1)S(1)}, u32[]{:S(2)}, u32[]{:S(2)}) async-start(bf16[8,4,32,256]{3,2,1,0:T(8,128)(2,1)} %shard_map.127), calls=%async_computation | async-start | bytes 1048576 | tf_op jit(solution)/shard_map/all_to_all | solution.py:258
  9.5 0.7 %copy-start.2 = (bf16[3,3,256]{2,1,0:T(4,128)(2,1)S(1)}, bf16[3,3,256]{2,1,0:T(4,128)(2,1)}, u32[]{:S(2)}) copy-start(bf16[3,3,256]{2,1,0:T(4,128)(2,1)} %param.16) | copy-start | bytes 13828
  24.0 0.8 %copy-start.1 = (bf16[8,4,32,256]{3,2,1,0:T(8,128)(2,1)}, bf16[8,4,32,256]{3,2,1,0:T(8,128)(2,1)S(1)}, u32[]{:S(2)}) copy-start(bf16[8,4,32,256]{3,2,1,0:T(8,128)(2,1)S(1)} %all-to-all-done.sig) | copy-start | bytes 1572868

commit v13 on v8

--- a/solution.py
+++ b/solution.py
@@ -271,6 +271,7 @@
             pltpu.VMEM((2 * half * piece, 2 * rows), f32),
             pltpu.VMEM((half * piece, 2 * rows), f32),
         ],
+        compiler_params=pltpu.CompilerParams(vmem_limit_bytes=24 * 1024 * 1024),
     )(first, last, gathered, kern, gain, twist, untwist, c_hi, c_lo, s_hi, s_lo)
 
     returned = lax.all_to_all(out, "ctx", 0, 0)

time: 41.8 us -> 39.7 us (0.950)
  local copies, waits for them, and re-layouts: 3.8 us -> 1.1 us
  waiting for transfers between devices: 12.2 us -> 14.1 us
  Pallas kernels: 7.16 us -> 5.97 us
    all_to_all x1, waiting for transfers between devices: 12.2 us -> 14.1 us  [body(): gathered = lax.all_to_all(stacked, 'ctx', 0, 0)]
    unnamed x6 -> x20, local copies, waits for them, and re-layouts: 1.49 us -> 0.04 us
    pallas_call x1, Pallas kernels: 4.93 us -> 3.74 us  [body(): pl.pallas_call(local_kernel, out_shape=jax.ShapeDtypeStruct((blocks, piec...]
    broadcast_in_dim x1, local copies, waits for them, and re-layouts: 0.79 us -> 0.13 us  [body(): kern = kern[..., None]]
    broadcast_in_dim x2, local copies, waits for them, and re-layouts: 0.76 us -> 0.17 us  [body(): gain = lax.dynamic_slice_in_dim(skip_gain, me * piece, piece)[:, None]]
  transfers between devices with their start and end apart: 1 -> 1, of which waited for: 1 -> 1; matrix products, arithmetic and copies ran while one was open for 4% -> 1% of each run, Pallas kernels for 0% -> 0%
where the time goes in v13:
time: 39.7 us; the launch traced here: 39.5 us
  waiting for transfers between devices  14.1 us (36%)
  blocking collectives  10.8 us (27%)
  starting transfers between devices  7.4 us (19%)
  Pallas kernels  5.97 us (15%)
  local copies, waits for them, and re-layouts  1.1 us (3%)
    all_to_all x1, waiting for transfers between devices, body(): gathered = lax.all_to_all(stacked, 'ctx', 0, 0)  14.1 us
    all_to_all x1, blocking collectives, body(): returned = lax.all_to_all(out, 'ctx', 0, 0)  10.8 us
    all_to_all x1, starting transfers between devices, body(): gathered = lax.all_to_all(stacked, 'ctx', 0, 0)  7.4 us
    pallas_call x1, Pallas kernels, body(): pl.pallas_call(local_kernel, out_shape=jax.ShapeDtypeStruct((blocks, piec...  3.74 us
    pallas_call x1, Pallas kernels, body(): pl.pallas_call(to_blocks_kernel, out_shape=jax.ShapeDtypeStruct((blocks,...  2.23 us
  transfers between devices with their start and end apart: 1, of which 1 were waited for; matrix products, arithmetic and copies ran while one was open for 1% of the time, Pallas kernels for 0%

profile of v13, /device:TPU:0, one launch (start us, length us, event | category | flops | bytes accessed | tf_op | source)
XLA Modules:
  0.0 39.5 jit_solution(17444908798930790900)
XLA Ops:
  0.0 0.0 copy-start
  0.0 2.2 %shard_map.136 = bf16[8,4,32,256]{3,2,1,0:T(8,128)(2,1)} custom-call(bf16[256,256]{1,0:T(8,128)(2,1)} %refs_0_.1, bf16[256,256]{1,0:T(8,128)(2,1)} %refs_1_.1, bf16[256,256]{1,0:T(8,128)(2,1)} %refs_2_.1, bf16[256,256]{1,0:T(8,128)(2,1)} %refs_3_.1), custom_call_target="tpu_custom_call" | custom-call | tf_op jit(solution)/shard_map/pallas_call | solution.py:247
  2.2 0.0 copy-start.9
  2.2 0.0 copy-start.2
  2.2 0.0 copy-start.3
  2.2 0.0 copy-start.4
  2.2 7.4 %all-to-all-start = ((bf16[8,4,32,256]{3,2,1,0:T(8,128)(2,1)}), bf16[8,4,32,256]{3,2,1,0:T(8,128)(2,1)S(1)}, u32[]{:S(2)}, u32[]{:S(2)}) async-start(bf16[8,4,32,256]{3,2,1,0:T(8,128)(2,1)} %shard_map.136), calls=%async_computation | async-start | bytes 1048576 | tf_op jit(solution)/shard_map/all_to_all | solution.py:254
  9.6 0.0 copy-start.1
  9.7 0.0 copy-done.9
  9.7 0.1 bitcast_convert_fusion
  9.7 0.0 copy-start.6
  9.7 0.0 copy-start.7
  9.7 0.0 copy-start.8
  9.8 0.1 copy.17.kern
  9.9 0.0 copy-done
  9.9 0.0 copy-start.5
  9.9 0.1 dynamic-slice_bitcast_fusion
  10.0 0.1 copy.18.gain
  10.1 14.1 %all-to-all-done.sig = bf16[8,4,32,256]{3,2,1,0:T(8,128)(2,1)S(1)} async-done(((bf16[8,4,32,256]{3,2,1,0:T(8,128)(2,1)}), bf16[8,4,32,256]{3,2,1,0:T(8,128)(2,1)S(1)}, u32[]{:S(2)}, u32[]{:S(2)}) %all-to-all-start) | async-done | bytes 524320 | tf_op jit(solution)/shard_map/all_to_all | solution.py:254
  24.1 0.0 copy-done.2
  24.1 0.0 copy-done.3
  24.1 0.0 copy-done.4
  24.1 0.0 copy-done.1
  24.2 0.0 copy-done.6
  24.2 0.0 copy-done.7
  24.2 0.0 copy-done.8
  24.2 0.0 copy-done.5
  24.2 3.7 %shard_map.137 = bf16[8,32,256]{2,1,0:T(8,128)(2,1)S(1)} custom-call(f32[18,8]{1,0:T(8,128)S(1)} %copy-done.7, f32[8,18]{1,0:T(8,128)S(1)} %copy-done.8, bf16[8,4,32,256]{3,2,1,0:T(8,128)(2,1)S(1)} %all-to-all-done.sig, f32[3,3,32,1]{3,2,1,0:T(8,128)S(1)} %copy.17.kern, f32[32,1]{1,0:T(8,128)S(1)} %copy.18.gain, f32[2,9,1,256]{3,2,1,0:T(1,128)S(1)} %copy-done.5, ...), custom_call_target="tpu_custom_call" | custom-call | tf_op jit(solution)/shard_map/pallas_call | solution.py:262
  27.9 10.8 %all_to_all.10 = bf16[8,32,256]{2,1,0:T(8,128)(2,1)S(1)} all-to-all(bf16[8,32,256]{2,1,0:T(8,128)(2,1)S(1)} %shard_map.137), channel_id=1, replica_groups=mesh['groups'=2,'ctx'=8,'ch'=2] {'ctx'}, dimensions={0} | all-to-all | bytes 262144 | tf_op jit(solution)/shard_map/all_to_all | solution.py:277
  38.7 0.8 %copy.19 = bf16[256,256]{0,1:T(8,128)(2,1)} copy(bf16[256,256]{1,0:T(8,128)(2,1)S(1)} %bitcast.7) | data formatting | bytes 262144 | tf_op jit(solution)/shard_map/reshape | solution.py:278
Async XLA Ops:
  0.0 9.9 %copy-start = (f32[256]{0:T(256)S(1)}, f32[256]{0:T(256)}, u32[]{:S(2)}) copy-start(f32[256]{0:T(256)} %param.19) | copy-start | bytes 3076
  2.2 7.4 %copy-start.9 = (bf16[3,3,256]{2,1,0:T(4,128)(2,1)S(1)}, bf16[3,3,256]{2,1,0:T(4,128)(2,1)}, u32[]{:S(2)}) copy-start(bf16[3,3,256]{2,1,0:T(4,128)(2,1)} %param.17) | copy-start | bytes 13828
  2.2 21.9 %copy-start.2 = (bf16[256,256]{1,0:T(8,128)(2,1)S(1)}, bf16[256,256]{1,0:T(8,128)(2,1)}, u32[]{:S(2)}) copy-start(bf16[256,256]{1,0:T(8,128)(2,1)} %constant.33.clone.c_lo) | copy-start | bytes 393220
  2.2 21.9 %copy-start.3 = (bf16[256,256]{1,0:T(8,128)(2,1)S(1)}, bf16[256,256]{1,0:T(8,128)(2,1)}, u32[]{:S(2)}) copy-start(bf16[256,256]{1,0:T(8,128)(2,1)} %constant.34.clone.s_hi) | copy-start | bytes 393220
  2.2 21.9 %copy-start.4 = (bf16[256,256]{1,0:T(8,128)(2,1)S(1)}, bf16[256,256]{1,0:T(8,128)(2,1)}, u32[]{:S(2)}) copy-start(bf16[256,256]{1,0:T(8,128)(2,1)} %constant.35.clone.s_lo) | copy-start | bytes 393220
  2.2 21.9 %all-to-all-start = ((bf16[8,4,32,256]{3,2,1,0:T(8,128)(2,1)}), bf16[8,4,32,256]{3,2,1,0:T(8,128)(2,1)S(1)}, u32[]{:S(2)}, u32[]{:S(2)}) async-start(bf16[8,4,32,256]{3,2,1,0:T(8,128)(2,1)} %shard_map.136), calls=%async_computation | async-start | bytes 1048576 | tf_op jit(solution)/shard_map/all_to_all | solution.py:254
  9.6 14.5 %copy-start.1 = (bf16[256,256]{1,0:T(8,128)(2,1)S(1)}, bf16[256,256]{1,0:T(8,128)(2,1)}, u32[]{:S(2)}) copy-start(bf16[256,256]{1,0:T(8,128)(2,1)} %constant.32.clone.c_hi) | copy-start | bytes 393220
  9.7 14.4 %copy-start.6 = (f32[2,9,1,256]{3,2,1,0:T(1,128)S(1)}, f32[2,9,1,256]{3,2,1,0:T(1,128)}, u32[]{:S(2)}) copy-start(f32[2,9,1,256]{3,2,1,0:T(1,128)} %constant.31.clone.untwist) | copy-start | bytes 55300
  9.7 14.4 %copy-start.7 = (f32[18,8]{1,0:T(8,128)S(1)}, f32[18,8]{1,0:T(8,128)}, u32[]{:S(2)}) copy-start(f32[18,8]{1,0:T(8,128)} %constant.28.clone.first) | copy-start | bytes 1732
  9.7 14.4 %copy-start.8 = (f32[8,18]{1,0:T(8,128)S(1)}, f32[8,18]{1,0:T(8,128)}, u32[]{:S(2)}) copy-start(f32[8,18]{1,0:T(8,128)} %constant.29.clone.last) | copy-start | bytes 1732
  9.9 14.3 %copy-start.5 = (f32[2,9,1,256]{3,2,1,0:T(1,128)S(1)}, f32[2,9,1,256]{3,2,1,0:T(1,128)}, u32[]{:S(2)}) copy-start(f32[2,9,1,256]{3,2,1,0:T(1,128)} %constant.30.clone.twist) | copy-start | bytes 55300

commit v14 on v13

--- a/solution.py
+++ b/solution.py
@@ -250,6 +250,7 @@
         in_specs=[vmem] * 4,
         out_specs=vmem,
         scratch_shapes=[pltpu.VMEM((chans, rows), jnp.float32)],
+        compiler_params=pltpu.CompilerParams(vmem_limit_bytes=16 * 1024 * 1024),
     )(gate_stream, value_stream, outer_stream, long_filter)
     gathered = lax.all_to_all(stacked, "ctx", 0, 0)
 

time: 39.7 us -> 42.3 us (1.065)
  local copies, waits for them, and re-layouts: 1.1 us -> 4.73 us
  Pallas kernels: 5.97 us -> 4.87 us
    unnamed x20 -> x28, local copies, waits for them, and re-layouts: 0.04 us -> 3.67 us
    pallas_call x1, Pallas kernels: 2.23 us -> 1.13 us  [body(): pl.pallas_call(to_blocks_kernel, out_shape=jax.ShapeDtypeStruct((blocks,...]
where the time goes in v14:
time: 42.3 us; the launch traced here: 42 us
  waiting for transfers between devices  14.1 us (33%)
  blocking collectives  10.8 us (26%)
  starting transfers between devices  7.39 us (17%)
  Pallas kernels  4.87 us (12%)
  local copies, waits for them, and re-layouts  4.73 us (11%)
    all_to_all x1, waiting for transfers between devices, body(): gathered = lax.all_to_all(stacked, 'ctx', 0, 0)  14.1 us
    all_to_all x1, blocking collectives, body(): returned = lax.all_to_all(out, 'ctx', 0, 0)  10.8 us
    all_to_all x1, starting transfers between devices, body(): gathered = lax.all_to_all(stacked, 'ctx', 0, 0)  7.39 us
    pallas_call x1, Pallas kernels, body(): pl.pallas_call(local_kernel, out_shape=jax.ShapeDtypeStruct((blocks, piec...  3.74 us
    unnamed x28, local copies, waits for them, and re-layouts  3.67 us
    pallas_call x1, Pallas kernels, body(): pl.pallas_call(to_blocks_kernel, out_shape=jax.ShapeDtypeStruct((blocks,...  1.13 us
  transfers between devices with their start and end apart: 1, of which 1 were waited for; matrix products, arithmetic and copies ran while one was open for 1% of the time, Pallas kernels for 0%

profile of v14, /device:TPU:0, one launch (start us, length us, event | category | flops | bytes accessed | tf_op | source)
XLA Modules:
  0.0 42.0 jit_solution(6946357102421961837)
XLA Ops:
  0.0 0.0 copy-start
  0.0 0.0 copy-start.1
  0.0 0.9 %copy-done.1 = bf16[256,256]{1,0:T(8,128)(2,1)S(1)} copy-done((bf16[256,256]{1,0:T(8,128)(2,1)S(1)}, bf16[256,256]{1,0:T(8,128)(2,1)}, u32[]{:S(2)}) %copy-start.1) | copy-done | bytes 131096
  0.9 0.0 copy-start.2
  0.9 0.9 %copy-done.2 = bf16[256,256]{1,0:T(8,128)(2,1)S(1)} copy-done((bf16[256,256]{1,0:T(8,128)(2,1)S(1)}, bf16[256,256]{1,0:T(8,128)(2,1)}, u32[]{:S(2)}) %copy-start.2) | copy-done | bytes 131096
  1.8 0.0 copy-start.3
  1.8 0.9 %copy-done.3 = bf16[256,256]{1,0:T(8,128)(2,1)S(1)} copy-done((bf16[256,256]{1,0:T(8,128)(2,1)S(1)}, bf16[256,256]{1,0:T(8,128)(2,1)}, u32[]{:S(2)}) %copy-start.3) | copy-done | bytes 131096
  2.7 0.0 copy-start.4
  2.7 0.9 %copy-done.4 = bf16[256,256]{1,0:T(8,128)(2,1)S(1)} copy-done((bf16[256,256]{1,0:T(8,128)(2,1)S(1)}, bf16[256,256]{1,0:T(8,128)(2,1)}, u32[]{:S(2)}) %copy-start.4) | copy-done | bytes 131096
  3.6 1.1 %shard_map.136 = bf16[8,4,32,256]{3,2,1,0:T(8,128)(2,1)} custom-call(bf16[256,256]{1,0:T(8,128)(2,1)S(1)} %copy-done.1, bf16[256,256]{1,0:T(8,128)(2,1)S(1)} %copy-done.2, bf16[256,256]{1,0:T(8,128)(2,1)S(1)} %copy-done.3, bf16[256,256]{1,0:T(8,128)(2,1)S(1)} %copy-done.4), custom_call_target="tpu_custom_call" | custom-call | tf_op jit(solution)/shard_map/pallas_call | solution.py:247
  4.8 0.0 copy-start.13
  4.8 0.0 copy-start.6
  4.8 0.0 copy-start.7
  4.8 0.0 copy-start.8
  4.8 7.4 %all-to-all-start = ((bf16[8,4,32,256]{3,2,1,0:T(8,128)(2,1)}), bf16[8,4,32,256]{3,2,1,0:T(8,128)(2,1)S(1)}, u32[]{:S(2)}, u32[]{:S(2)}) async-start(bf16[8,4,32,256]{3,2,1,0:T(8,128)(2,1)} %shard_map.136), calls=%async_computation | async-start | bytes 1048576 | tf_op jit(solution)/shard_map/all_to_all | solution.py:255
  12.2 0.0 copy-start.5
  12.2 0.0 copy-done.13
  12.2 0.1 bitcast_convert_fusion
  12.3 0.0 copy-start.10
  12.3 0.0 copy-start.11
  12.3 0.0 copy-start.12
  12.3 0.1 copy.17.kern
  12.4 0.0 copy-done
  12.4 0.0 copy-start.9
  12.4 0.1 dynamic-slice_bitcast_fusion
  12.5 0.1 copy.18.gain
  12.6 14.1 %all-to-all-done.sig = bf16[8,4,32,256]{3,2,1,0:T(8,128)(2,1)S(1)} async-done(((bf16[8,4,32,256]{3,2,1,0:T(8,128)(2,1)}), bf16[8,4,32,256]{3,2,1,0:T(8,128)(2,1)S(1)}, u32[]{:S(2)}, u32[]{:S(2)}) %all-to-all-start) | async-done | bytes 524320 | tf_op jit(solution)/shard_map/all_to_all | solution.py:255
  26.7 0.0 copy-done.6
  26.7 0.0 copy-done.7
  26.7 0.0 copy-done.8
  26.7 0.0 copy-done.5
  26.7 0.0 copy-done.10
  26.7 0.0 copy-done.11
  26.7 0.0 copy-done.12
  26.7 0.0 copy-done.9
  26.7 3.7 %shard_map.137 = bf16[8,32,256]{2,1,0:T(8,128)(2,1)S(1)} custom-call(f32[18,8]{1,0:T(8,128)S(1)} %copy-done.11, f32[8,18]{1,0:T(8,128)S(1)} %copy-done.12, bf16[8,4,32,256]{3,2,1,0:T(8,128)(2,1)S(1)} %all-to-all-done.sig, f32[3,3,32,1]{3,2,1,0:T(8,128)S(1)} %copy.17.kern, f32[32,1]{1,0:T(8,128)S(1)} %copy.18.gain, f32[2,9,1,256]{3,2,1,0:T(1,128)S(1)} %copy-done.9, ...), custom_call_target="tpu_custom_call" | custom-call | tf_op jit(solution)/shard_map/pallas_call | solution.py:263
  30.5 10.8 %all_to_all.10 = bf16[8,32,256]{2,1,0:T(8,128)(2,1)S(1)} all-to-all(bf16[8,32,256]{2,1,0:T(8,128)(2,1)S(1)} %shard_map.137), channel_id=1, replica_groups=mesh['groups'=2,'ctx'=8,'ch'=2] {'ctx'}, dimensions={0} | all-to-all | bytes 262144 | tf_op jit(solution)/shard_map/all_to_all | solution.py:278
  41.2 0.8 %copy.19 = bf16[256,256]{0,1:T(8,128)(2,1)} copy(bf16[256,256]{1,0:T(8,128)(2,1)S(1)} %bitcast.7) | data formatting | bytes 262144 | tf_op jit(solution)/shard_map/reshape | solution.py:279
Async XLA Ops:
  0.0 12.4 %copy-start = (f32[256]{0:T(256)S(1)}, f32[256]{0:T(256)}, u32[]{:S(2)}) copy-start(f32[256]{0:T(256)} %param.19) | copy-start | bytes 3076
  0.0 0.9 %copy-start.1 = (bf16[256,256]{1,0:T(8,128)(2,1)S(1)}, bf16[256,256]{1,0:T(8,128)(2,1)}, u32[]{:S(2)}) copy-start(bf16[256,256]{1,0:T(8,128)(2,1)} %refs_0_.1) | copy-start | bytes 393220
  0.9 0.9 %copy-start.2 = (bf16[256,256]{1,0:T(8,128)(2,1)S(1)}, bf16[256,256]{1,0:T(8,128)(2,1)}, u32[]{:S(2)}) copy-start(bf16[256,256]{1,0:T(8,128)(2,1)} %refs_1_.1) | copy-start | bytes 393220
  1.8 0.9 %copy-start.3 = (bf16[256,256]{1,0:T(8,128)(2,1)S(1)}, bf16[256,256]{1,0:T(8,128)(2,1)}, u32[]{:S(2)}) copy-start(bf16[256,256]{1,0:T(8,128)(2,1)} %refs_2_.1) | copy-start | bytes 393220
  2.7 0.9 %copy-start.4 = (bf16[256,256]{1,0:T(8,128)(2,1)S(1)}, bf16[256,256]{1,0:T(8,128)(2,1)}, u32[]{:S(2)}) copy-start(bf16[256,256]{1,0:T(8,128)(2,1)} %refs_3_.1) | copy-start | bytes 393220
  4.8 7.4 %copy-start.13 = (bf16[3,3,256]{2,1,0:T(4,128)(2,1)S(1)}, bf16[3,3,256]{2,1,0:T(4,128)(2,1)}, u32[]{:S(2)}) copy-start(bf16[3,3,256]{2,1,0:T(4,128)(2,1)} %param.17) | copy-start | bytes 13828
  4.8 21.9 %copy-start.6 = (bf16[256,256]{1,0:T(8,128)(2,1)S(1)}, bf16[256,256]{1,0:T(8,128)(2,1)}, u32[]{:S(2)}) copy-start(bf16[256,256]{1,0:T(8,128)(2,1)} %constant.33.clone.c_lo) | copy-start | bytes 393220
  4.8 21.9 %copy-start.7 = (bf16[256,256]{1,0:T(8,128)(2,1)S(1)}, bf16[256,256]{1,0:T(8,128)(2,1)}, u32[]{:S(2)}) copy-start(bf16[256,256]{1,0:T(8,128)(2,1)} %constant.34.clone.s_hi) | copy-start | bytes 393220
  4.8 21.9 %copy-start.8 = (bf16[256,256]{1,0:T(8,128)(2,1)S(1)}, bf16[256,256]{1,0:T(8,128)(2,1)}, u32[]{:S(2)}) copy-start(bf16[256,256]{1,0:T(8,128)(2,1)} %constant.35.clone.s_lo) | copy-start | bytes 393220
  4.8 21.9 %all-to-all-start = ((bf16[8,4,32,256]{3,2,1,0:T(8,128)(2,1)}), bf16[8,4,32,256]{3,2,1,0:T(8,128)(2,1)S(1)}, u32[]{:S(2)}, u32[]{:S(2)}) async-start(bf16[8,4,32,256]{3,2,1,0:T(8,128)(2,1)} %shard_map.136), calls=%async_computation | async-start | bytes 1048576 | tf_op jit(solution)/shard_map/all_to_all | solution.py:255
  12.2 14.5 %copy-start.5 = (bf16[256,256]{1,0:T(8,128)(2,1)S(1)}, bf16[256,256]{1,0:T(8,128)(2,1)}, u32[]{:S(2)}) copy-start(bf16[256,256]{1,0:T(8,128)(2,1)} %constant.32.clone.c_hi) | copy-start | bytes 393220
  12.3 14.4 %copy-start.10 = (f32[2,9,1,256]{3,2,1,0:T(1,128)S(1)}, f32[2,9,1,256]{3,2,1,0:T(1,128)}, u32[]{:S(2)}) copy-start(f32[2,9,1,256]{3,2,1,0:T(1,128)} %constant.31.clone.untwist) | copy-start | bytes 55300
  12.3 14.4 %copy-start.11 = (f32[18,8]{1,0:T(8,128)S(1)}, f32[18,8]{1,0:T(8,128)}, u32[]{:S(2)}) copy-start(f32[18,8]{1,0:T(8,128)} %constant.28.clone.first) | copy-start | bytes 1732
  12.3 14.4 %copy-start.12 = (f32[8,18]{1,0:T(8,128)S(1)}, f32[8,18]{1,0:T(8,128)}, u32[]{:S(2)}) copy-start(f32[8,18]{1,0:T(8,128)} %constant.29.clone.last) | copy-start | bytes 1732
  12.4 14.3 %copy-start.9 = (f32[2,9,1,256]{3,2,1,0:T(1,128)S(1)}, f32[2,9,1,256]{3,2,1,0:T(1,128)}, u32[]{:S(2)}) copy-start(f32[2,9,1,256]{3,2,1,0:T(1,128)} %constant.30.clone.twist) | copy-start | bytes 55300

commit v15 on v8

--- a/solution.py
+++ b/solution.py
@@ -271,6 +271,7 @@
             pltpu.VMEM((2 * half * piece, 2 * rows), f32),
             pltpu.VMEM((half * piece, 2 * rows), f32),
         ],
+        compiler_params=pltpu.CompilerParams(vmem_limit_bytes=12 * 1024 * 1024),
     )(first, last, gathered, kern, gain, twist, untwist, c_hi, c_lo, s_hi, s_lo)
 
     returned = lax.all_to_all(out, "ctx", 0, 0)

time: 41.8 us -> 39.7 us (0.950)
  local copies, waits for them, and re-layouts: 3.8 us -> 1.1 us
  waiting for transfers between devices: 12.2 us -> 14.1 us
  Pallas kernels: 7.16 us -> 5.97 us
    all_to_all x1, waiting for transfers between devices: 12.2 us -> 14.1 us  [body(): gathered = lax.all_to_all(stacked, 'ctx', 0, 0)]
    unnamed x6 -> x20, local copies, waits for them, and re-layouts: 1.49 us -> 0.04 us
    pallas_call x1, Pallas kernels: 4.93 us -> 3.74 us  [body(): pl.pallas_call(local_kernel, out_shape=jax.ShapeDtypeStruct((blocks, piec...]
    broadcast_in_dim x1, local copies, waits for them, and re-layouts: 0.79 us -> 0.13 us  [body(): kern = kern[..., None]]
    broadcast_in_dim x2, local copies, waits for them, and re-layouts: 0.76 us -> 0.17 us  [body(): gain = lax.dynamic_slice_in_dim(skip_gain, me * piece, piece)[:, None]]
  transfers between devices with their start and end apart: 1 -> 1, of which waited for: 1 -> 1; matrix products, arithmetic and copies ran while one was open for 4% -> 1% of each run, Pallas kernels for 0% -> 0%
where the time goes in v15:
time: 39.7 us; the launch traced here: 39.5 us
  waiting for transfers between devices  14.1 us (36%)
  blocking collectives  10.8 us (27%)
  starting transfers between devices  7.4 us (19%)
  Pallas kernels  5.97 us (15%)
  local copies, waits for them, and re-layouts  1.1 us (3%)
    all_to_all x1, waiting for transfers between devices, body(): gathered = lax.all_to_all(stacked, 'ctx', 0, 0)  14.1 us
    all_to_all x1, blocking collectives, body(): returned = lax.all_to_all(out, 'ctx', 0, 0)  10.8 us
    all_to_all x1, starting transfers between devices, body(): gathered = lax.all_to_all(stacked, 'ctx', 0, 0)  7.4 us
    pallas_call x1, Pallas kernels, body(): pl.pallas_call(local_kernel, out_shape=jax.ShapeDtypeStruct((blocks, piec...  3.74 us
    pallas_call x1, Pallas kernels, body(): pl.pallas_call(to_blocks_kernel, out_shape=jax.ShapeDtypeStruct((blocks,...  2.23 us
  transfers between devices with their start and end apart: 1, of which 1 were waited for; matrix products, arithmetic and copies ran while one was open for 1% of the time, Pallas kernels for 0%

profile of v15, /device:TPU:0, one launch (start us, length us, event | category | flops | bytes accessed | tf_op | source)
XLA Modules:
  0.0 39.5 jit_solution(13628090479707632459)
XLA Ops:
  0.0 0.0 copy-start
  0.0 2.2 %shard_map.136 = bf16[8,4,32,256]{3,2,1,0:T(8,128)(2,1)} custom-call(bf16[256,256]{1,0:T(8,128)(2,1)} %refs_0_.1, bf16[256,256]{1,0:T(8,128)(2,1)} %refs_1_.1, bf16[256,256]{1,0:T(8,128)(2,1)} %refs_2_.1, bf16[256,256]{1,0:T(8,128)(2,1)} %refs_3_.1), custom_call_target="tpu_custom_call" | custom-call | tf_op jit(solution)/shard_map/pallas_call | solution.py:247
  2.2 0.0 copy-start.9
  2.2 0.0 copy-start.2
  2.2 0.0 copy-start.3
  2.2 0.0 copy-start.4
  2.2 7.4 %all-to-all-start = ((bf16[8,4,32,256]{3,2,1,0:T(8,128)(2,1)}), bf16[8,4,32,256]{3,2,1,0:T(8,128)(2,1)S(1)}, u32[]{:S(2)}, u32[]{:S(2)}) async-start(bf16[8,4,32,256]{3,2,1,0:T(8,128)(2,1)} %shard_map.136), calls=%async_computation | async-start | bytes 1048576 | tf_op jit(solution)/shard_map/all_to_all | solution.py:254
  9.6 0.0 copy-start.1
  9.7 0.0 copy-done.9
  9.7 0.1 bitcast_convert_fusion
  9.7 0.0 copy-start.6
  9.7 0.0 copy-start.7
  9.7 0.0 copy-start.8
  9.8 0.1 copy.17.kern
  9.9 0.0 copy-done
  9.9 0.0 copy-start.5
  9.9 0.1 dynamic-slice_bitcast_fusion
  10.0 0.1 copy.18.gain
  10.1 14.1 %all-to-all-done.sig = bf16[8,4,32,256]{3,2,1,0:T(8,128)(2,1)S(1)} async-done(((bf16[8,4,32,256]{3,2,1,0:T(8,128)(2,1)}), bf16[8,4,32,256]{3,2,1,0:T(8,128)(2,1)S(1)}, u32[]{:S(2)}, u32[]{:S(2)}) %all-to-all-start) | async-done | bytes 524320 | tf_op jit(solution)/shard_map/all_to_all | solution.py:254
  24.1 0.0 copy-done.2
  24.1 0.0 copy-done.3
  24.1 0.0 copy-done.4
  24.1 0.0 copy-done.1
  24.2 0.0 copy-done.6
  24.2 0.0 copy-done.7
  24.2 0.0 copy-done.8
  24.2 0.0 copy-done.5
  24.2 3.7 %shard_map.137 = bf16[8,32,256]{2,1,0:T(8,128)(2,1)S(1)} custom-call(f32[18,8]{1,0:T(8,128)S(1)} %copy-done.7, f32[8,18]{1,0:T(8,128)S(1)} %copy-done.8, bf16[8,4,32,256]{3,2,1,0:T(8,128)(2,1)S(1)} %all-to-all-done.sig, f32[3,3,32,1]{3,2,1,0:T(8,128)S(1)} %copy.17.kern, f32[32,1]{1,0:T(8,128)S(1)} %copy.18.gain, f32[2,9,1,256]{3,2,1,0:T(1,128)S(1)} %copy-done.5, ...), custom_call_target="tpu_custom_call" | custom-call | tf_op jit(solution)/shard_map/pallas_call | solution.py:262
  27.9 10.8 %all_to_all.10 = bf16[8,32,256]{2,1,0:T(8,128)(2,1)S(1)} all-to-all(bf16[8,32,256]{2,1,0:T(8,128)(2,1)S(1)} %shard_map.137), channel_id=1, replica_groups=mesh['groups'=2,'ctx'=8,'ch'=2] {'ctx'}, dimensions={0} | all-to-all | bytes 262144 | tf_op jit(solution)/shard_map/all_to_all | solution.py:277
  38.7 0.8 %copy.19 = bf16[256,256]{0,1:T(8,128)(2,1)} copy(bf16[256,256]{1,0:T(8,128)(2,1)S(1)} %bitcast.7) | data formatting | bytes 262144 | tf_op jit(solution)/shard_map/reshape | solution.py:278
Async XLA Ops:
  0.0 9.9 %copy-start = (f32[256]{0:T(256)S(1)}, f32[256]{0:T(256)}, u32[]{:S(2)}) copy-start(f32[256]{0:T(256)} %param.19) | copy-start | bytes 3076
  2.2 7.4 %copy-start.9 = (bf16[3,3,256]{2,1,0:T(4,128)(2,1)S(1)}, bf16[3,3,256]{2,1,0:T(4,128)(2,1)}, u32[]{:S(2)}) copy-start(bf16[3,3,256]{2,1,0:T(4,128)(2,1)} %param.17) | copy-start | bytes 13828
  2.2 21.9 %copy-start.2 = (bf16[256,256]{1,0:T(8,128)(2,1)S(1)}, bf16[256,256]{1,0:T(8,128)(2,1)}, u32[]{:S(2)}) copy-start(bf16[256,256]{1,0:T(8,128)(2,1)} %constant.33.clone.c_lo) | copy-start | bytes 393220
  2.2 21.9 %copy-start.3 = (bf16[256,256]{1,0:T(8,128)(2,1)S(1)}, bf16[256,256]{1,0:T(8,128)(2,1)}, u32[]{:S(2)}) copy-start(bf16[256,256]{1,0:T(8,128)(2,1)} %constant.34.clone.s_hi) | copy-start | bytes 393220
  2.2 21.9 %copy-start.4 = (bf16[256,256]{1,0:T(8,128)(2,1)S(1)}, bf16[256,256]{1,0:T(8,128)(2,1)}, u32[]{:S(2)}) copy-start(bf16[256,256]{1,0:T(8,128)(2,1)} %constant.35.clone.s_lo) | copy-start | bytes 393220
  2.2 21.9 %all-to-all-start = ((bf16[8,4,32,256]{3,2,1,0:T(8,128)(2,1)}), bf16[8,4,32,256]{3,2,1,0:T(8,128)(2,1)S(1)}, u32[]{:S(2)}, u32[]{:S(2)}) async-start(bf16[8,4,32,256]{3,2,1,0:T(8,128)(2,1)} %shard_map.136), calls=%async_computation | async-start | bytes 1048576 | tf_op jit(solution)/shard_map/all_to_all | solution.py:254
  9.6 14.5 %copy-start.1 = (bf16[256,256]{1,0:T(8,128)(2,1)S(1)}, bf16[256,256]{1,0:T(8,128)(2,1)}, u32[]{:S(2)}) copy-start(bf16[256,256]{1,0:T(8,128)(2,1)} %constant.32.clone.c_hi) | copy-start | bytes 393220
  9.7 14.4 %copy-start.6 = (f32[2,9,1,256]{3,2,1,0:T(1,128)S(1)}, f32[2,9,1,256]{3,2,1,0:T(1,128)}, u32[]{:S(2)}) copy-start(f32[2,9,1,256]{3,2,1,0:T(1,128)} %constant.31.clone.untwist) | copy-start | bytes 55300
  9.7 14.4 %copy-start.7 = (f32[18,8]{1,0:T(8,128)S(1)}, f32[18,8]{1,0:T(8,128)}, u32[]{:S(2)}) copy-start(f32[18,8]{1,0:T(8,128)} %constant.28.clone.first) | copy-start | bytes 1732
  9.7 14.4 %copy-start.8 = (f32[8,18]{1,0:T(8,128)S(1)}, f32[8,18]{1,0:T(8,128)}, u32[]{:S(2)}) copy-start(f32[8,18]{1,0:T(8,128)} %constant.29.clone.last) | copy-start | bytes 1732
  9.9 14.3 %copy-start.5 = (f32[2,9,1,256]{3,2,1,0:T(1,128)S(1)}, f32[2,9,1,256]{3,2,1,0:T(1,128)}, u32[]{:S(2)}) copy-start(f32[2,9,1,256]{3,2,1,0:T(1,128)} %constant.30.clone.twist) | copy-start | bytes 55300

commit v16 on v12

--- a/solution.py
+++ b/solution.py
@@ -275,6 +275,7 @@
             pltpu.VMEM((2 * half * piece, 2 * rows), f32),
             pltpu.VMEM((half * piece, 2 * rows), f32),
         ],
+        compiler_params=pltpu.CompilerParams(vmem_limit_bytes=24 * 1024 * 1024),
     )(first, last, gathered, kern, gain, turns, tabs)
 
     returned = lax.all_to_all(out, "ctx", 0, 0)

time: 41.8 us -> 39.7 us (0.950)
  local copies, waits for them, and re-layouts: 3.8 us -> 1.77 us
  waiting for transfers between devices: 12.2 us -> 13.4 us
  Pallas kernels: 7.13 us -> 5.97 us
    all_to_all x1, waiting for transfers between devices: 12.2 us -> 13.4 us  [body(): gathered = lax.all_to_all(stacked, 'ctx', 0, 0)]
    pallas_call x1, Pallas kernels: 4.89 us -> 3.74 us  [body(): pl.pallas_call(local_kernel, out_shape=jax.ShapeDtypeStruct((blocks, piec...]
    unnamed x6 -> x12, local copies, waits for them, and re-layouts: 1.49 us -> 0.71 us
    broadcast_in_dim x1, local copies, waits for them, and re-layouts: 0.79 us -> 0.13 us  [body(): kern = kern[..., None]]
    broadcast_in_dim x2, local copies, waits for them, and re-layouts: 0.76 us -> 0.17 us  [body(): gain = lax.dynamic_slice_in_dim(skip_gain, me * piece, piece)[:, None]]
  transfers between devices with their start and end apart: 1 -> 1, of which waited for: 1 -> 1; matrix products, arithmetic and copies ran while one was open for 4% -> 1% of each run, Pallas kernels for 0% -> 0%
where the time goes in v16:
time: 39.7 us; the launch traced here: 39.4 us
  waiting for transfers between devices  13.4 us (34%)
  blocking collectives  10.8 us (27%)
  starting transfers between devices  7.39 us (19%)
  Pallas kernels  5.97 us (15%)
  local copies, waits for them, and re-layouts  1.77 us (4%)
    all_to_all x1, waiting for transfers between devices, body(): gathered = lax.all_to_all(stacked, 'ctx', 0, 0)  13.4 us
    all_to_all x1, blocking collectives, body(): returned = lax.all_to_all(out, 'ctx', 0, 0)  10.8 us
    all_to_all x1, starting transfers between devices, body(): gathered = lax.all_to_all(stacked, 'ctx', 0, 0)  7.39 us
    pallas_call x1, Pallas kernels, body(): pl.pallas_call(local_kernel, out_shape=jax.ShapeDtypeStruct((blocks, piec...  3.74 us
    pallas_call x1, Pallas kernels, body(): pl.pallas_call(to_blocks_kernel, out_shape=jax.ShapeDtypeStruct((blocks,...  2.23 us
  transfers between devices with their start and end apart: 1, of which 1 were waited for; matrix products, arithmetic and copies ran while one was open for 1% of the time, Pallas kernels for 0%

profile of v16, /device:TPU:0, one launch (start us, length us, event | category | flops | bytes accessed | tf_op | source)
XLA Modules:
  0.0 39.4 jit_solution(961191401267655497)
XLA Ops:
  0.0 0.0 copy-start
  0.0 2.2 %shard_map.127 = bf16[8,4,32,256]{3,2,1,0:T(8,128)(2,1)} custom-call(bf16[256,256]{1,0:T(8,128)(2,1)} %refs_0_.1, bf16[256,256]{1,0:T(8,128)(2,1)} %refs_1_.1, bf16[256,256]{1,0:T(8,128)(2,1)} %refs_2_.1, bf16[256,256]{1,0:T(8,128)(2,1)} %refs_3_.1), custom_call_target="tpu_custom_call" | custom-call | tf_op jit(solution)/shard_map/pallas_call | solution.py:251
  2.2 0.0 copy-start.1
  2.2 7.4 %all-to-all-start = ((bf16[8,4,32,256]{3,2,1,0:T(8,128)(2,1)}), bf16[8,4,32,256]{3,2,1,0:T(8,128)(2,1)S(1)}, u32[]{:S(2)}, u32[]{:S(2)}) async-start(bf16[8,4,32,256]{3,2,1,0:T(8,128)(2,1)} %shard_map.127), calls=%async_computation | async-start | bytes 1048576 | tf_op jit(solution)/shard_map/all_to_all | solution.py:258
  9.6 0.0 copy-start.5
  9.6 0.7 %copy-done.5 = bf16[3,3,256]{2,1,0:T(4,128)(2,1)S(1)} copy-done((bf16[3,3,256]{2,1,0:T(4,128)(2,1)S(1)}, bf16[3,3,256]{2,1,0:T(4,128)(2,1)}, u32[]{:S(2)}) %copy-start.5) | copy-done | bytes 4632
  10.3 0.1 bitcast_convert_fusion
  10.4 0.0 copy-start.2
  10.4 0.1 copy.16.kern
  10.5 0.0 copy-done
  10.5 0.0 copy-start.3
  10.5 0.1 dynamic-slice_bitcast_fusion
  10.6 0.0 copy-start.4
  10.6 0.1 copy.17.gain
  10.7 13.4 %all-to-all-done.sig = bf16[8,4,32,256]{3,2,1,0:T(8,128)(2,1)S(1)} async-done(((bf16[8,4,32,256]{3,2,1,0:T(8,128)(2,1)}), bf16[8,4,32,256]{3,2,1,0:T(8,128)(2,1)S(1)}, u32[]{:S(2)}, u32[]{:S(2)}) %all-to-all-start) | async-done | bytes 524320 | tf_op jit(solution)/shard_map/all_to_all | solution.py:258
  24.1 0.0 copy-done.1
  24.1 0.0 copy-done.2
  24.1 0.0 copy-done.3
  24.1 0.0 copy-done.4
  24.1 3.7 %shard_map.128 = bf16[8,32,256]{2,1,0:T(8,128)(2,1)S(1)} custom-call(f32[18,8]{1,0:T(8,128)S(1)} %copy-done.3, f32[8,18]{1,0:T(8,128)S(1)} %copy-done.4, bf16[8,4,32,256]{3,2,1,0:T(8,128)(2,1)S(1)} %all-to-all-done.sig, f32[3,3,32,1]{3,2,1,0:T(8,128)S(1)} %copy.16.kern, f32[32,1]{1,0:T(8,128)S(1)} %copy.17.gain, f32[4,9,1,256]{3,2,1,0:T(1,128)S(1)} %copy-done.2, ...), custom_call_target="tpu_custom_call" | custom-call | tf_op jit(solution)/shard_map/pallas_call | solution.py:266
  27.9 10.8 %all_to_all.10 = bf16[8,32,256]{2,1,0:T(8,128)(2,1)S(1)} all-to-all(bf16[8,32,256]{2,1,0:T(8,128)(2,1)S(1)} %shard_map.128), channel_id=1, replica_groups=mesh['groups'=2,'ctx'=8,'ch'=2] {'ctx'}, dimensions={0} | all-to-all | bytes 262144 | tf_op jit(solution)/shard_map/all_to_all | solution.py:281
  38.7 0.8 %copy.18 = bf16[256,256]{0,1:T(8,128)(2,1)} copy(bf16[256,256]{1,0:T(8,128)(2,1)S(1)} %bitcast.7) | data formatting | bytes 262144 | tf_op jit(solution)/shard_map/reshape | solution.py:282
Async XLA Ops:
  0.0 10.5 %copy-start = (f32[256]{0:T(256)S(1)}, f32[256]{0:T(256)}, u32[]{:S(2)}) copy-start(f32[256]{0:T(256)} %param.18) | copy-start | bytes 3076
  2.2 21.9 %copy-start.1 = (bf16[4,256,256]{2,1,0:T(8,128)(2,1)S(1)}, bf16[4,256,256]{2,1,0:T(8,128)(2,1)}, u32[]{:S(2)}) copy-start(bf16[4,256,256]{2,1,0:T(8,128)(2,1)} %constant.37.tabs) | copy-start | bytes 1572868
  2.2 21.9 %all-to-all-start = ((bf16[8,4,32,256]{3,2,1,0:T(8,128)(2,1)}), bf16[8,4,32,256]{3,2,1,0:T(8,128)(2,1)S(1)}, u32[]{:S(2)}, u32[]{:S(2)}) async-start(bf16[8,4,32,256]{3,2,1,0:T(8,128)(2,1)} %shard_map.127), calls=%async_computation | async-start | bytes 1048576 | tf_op jit(solution)/shard_map/all_to_all | solution.py:258
  9.6 0.7 %copy-start.5 = (bf16[3,3,256]{2,1,0:T(4,128)(2,1)S(1)}, bf16[3,3,256]{2,1,0:T(4,128)(2,1)}, u32[]{:S(2)}) copy-start(bf16[3,3,256]{2,1,0:T(4,128)(2,1)} %param.16) | copy-start | bytes 13828
  10.4 13.7 %copy-start.2 = (f32[4,9,1,256]{3,2,1,0:T(1,128)S(1)}, f32[4,9,1,256]{3,2,1,0:T(1,128)}, u32[]{:S(2)}) copy-start(f32[4,9,1,256]{3,2,1,0:T(1,128)} %constant.30.clone.turns) | copy-start | bytes 110596
  10.5 13.6 %copy-start.3 = (f32[18,8]{1,0:T(8,128)S(1)}, f32[18,8]{1,0:T(8,128)}, u32[]{:S(2)}) copy-start(f32[18,8]{1,0:T(8,128)} %constant.31.clone.first) | copy-start | bytes 1732
  10.6 13.5 %copy-start.4 = (f32[8,18]{1,0:T(8,128)S(1)}, f32[8,18]{1,0:T(8,128)}, u32[]{:S(2)}) copy-start(f32[8,18]{1,0:T(8,128)} %constant.32.clone.last) | copy-start | bytes 1732
